TPU v7x, 256 devices: a whole 4x4x8 slice. The times are simulated.
256 devices in a mesh: seq: 64 (over y, z, core), tp: 4 (over x).
Axes of the slice: x: 4, y: 4, z: 8, core: 2. Of those that a mesh axis runs over, the one named last changes fastest.
Arguments:
- tokens: bfloat16 [512, 1152], P('seq'), may hold values from -6 to 6
- attn_gain: float32 [1152], replicated, may hold values from 0.1 to 1.9
- w_query: bfloat16 [1152, 1280], P(None, 'tp'), may hold values from -0.1875 to 0.1875
- w_key: bfloat16 [1152, 384], replicated, may hold values from -0.1875 to 0.1875
- w_value: bfloat16 [1152, 384], replicated, may hold values from -0.1875 to 0.1875
- w_out: bfloat16 [1280, 1152], P('tp'), may hold values from -0.1875 to 0.1875
- prefix_keys: bfloat16 [8, 32768, 384], P(None, 'seq'), may hold values from -92 to 92
- prefix_values: bfloat16 [8, 32768, 384], P(None, 'seq'), may hold values from -6 to 6
- suffix_keys: bfloat16 [512, 128, 384], P('seq'), may hold values from -92 to 92
- suffix_values: bfloat16 [512, 128, 384], P('seq'), may hold values from -6 to 6
- group_of: int32 [512], replicated, may hold values from 0 to 7, as said below
- prefix_len: int32 [8], replicated, may hold values from 1 to 32768, as said below
- suffix_len: int32 [512], replicated, may hold values from 0 to 128, as said below
- mlp_gain: float32 [1152], replicated, may hold values from 0.1 to 1.9
- w_gate: bfloat16 [1152, 3072], P(None, 'tp'), may hold values from -0.1875 to 0.1875
- w_up: bfloat16 [1152, 3072], P(None, 'tp'), may hold values from -0.1875 to 0.1875
- w_down: bfloat16 [3072, 1152], P('tp'), may hold values from -0.109375 to 0.109375
Outputs:
- layer_out: bfloat16 [512, 1152], P('seq')
Inputs may be any that keep to these rules, and one draw needn't show every extreme that they name: `group_of`: prompt group of each request; every request reads its group's stored prefix. `prefix_len`: stored prefix positions in use for each group. `suffix_len`: stored suffix positions in use for each request.
All inputs are finite; a program needn't handle non-finite values.
Results may differ from a plain program's by a relative error of at most 0.018.
Values may be sent and summed in bfloat16 or wider, within the bound.
No kernel may reach another device: no remote copies, remote signals or barrier semaphores. Data moves between devices by JAX's collectives and lax.ppermute only.
A program may use at most 192 MiB of HBM per device.

v0:
```python
import jax
import jax.numpy as jnp
from jax import lax
from jax.sharding import PartitionSpec as P

HEADS = 18
KV_HEADS = 6
HD = 64


NEG_FILL = -1e30


def rms_scale(values_in, gain_row):
    widened = values_in.astype(jnp.float32)
    factor = lax.rsqrt(jnp.mean(widened * widened, axis=-1, keepdims=True) + 1e-05)
    return (widened * factor * gain_row).astype(jnp.bfloat16)


def rotate_heads(blocks, position):
    half_dim = blocks.shape[-1] // 2
    frequency = jnp.power(10000.0, -jnp.arange(half_dim, dtype=jnp.float32) / half_dim)
    angles = position.astype(jnp.float32)[:, None, None] * frequency
    cosine = jnp.cos(angles)
    sine_part = jnp.sin(angles)
    low_half = blocks[..., :half_dim]
    high_half = blocks[..., half_dim:]
    return jnp.concatenate(
        [low_half * cosine - high_half * sine_part, high_half * cosine + low_half * sine_part],
        axis=-1,
    )


def slot_layout(device_tp, tp_count, slot_count):
    per_device = HEADS // tp_count
    surplus = HEADS % tp_count
    start_head = per_device * device_tp + jnp.minimum(device_tp, surplus)
    used_count = per_device + (device_tp < surplus).astype(jnp.int32)
    slot_ids = jnp.arange(slot_count, dtype=jnp.int32)
    head_ids = start_head + slot_ids
    slot_used = (slot_ids < used_count).astype(jnp.float32)
    kv_ids = jnp.minimum(head_ids, HEADS - 1) // (HEADS // KV_HEADS)
    return (kv_ids, slot_used)


def on_device(
    tokens,
    attn_gain,
    w_query,
    w_key,
    w_value,
    w_out,
    prefix_keys,
    prefix_values,
    suffix_keys,
    suffix_values,
    group_of,
    prefix_len,
    suffix_len,
    mlp_gain,
    w_gate,
    w_up,
    w_down,
):
    row_count = tokens.shape[0]
    slot_count = w_query.shape[1] // HD
    group_count = prefix_keys.shape[0]
    prefix_span = prefix_keys.shape[1]
    suffix_span = suffix_keys.shape[1]
    seq_index = lax.axis_index("seq")
    kv_ids, slot_used = slot_layout(lax.axis_index("tp"), lax.axis_size("tp"), slot_count)
    normed = rms_scale(tokens, attn_gain)
    queries = jnp.dot(normed, w_query, preferred_element_type=jnp.float32).reshape(
        row_count, slot_count, HD
    )
    new_keys = jnp.dot(normed, w_key, preferred_element_type=jnp.float32).reshape(
        row_count, KV_HEADS, HD
    )
    new_values = (
        jnp.dot(normed, w_value, preferred_element_type=jnp.float32)
        .astype(jnp.bfloat16)
        .reshape(row_count, KV_HEADS, HD)
    )
    own_start = seq_index * row_count
    own_groups = lax.dynamic_slice_in_dim(group_of, own_start, row_count)
    own_suffix = lax.dynamic_slice_in_dim(suffix_len, own_start, row_count)
    group_ids = jnp.arange(group_count, dtype=jnp.int32)
    own_prefix = jnp.sum(
        jnp.where(own_groups[:, None] == group_ids[None, :], prefix_len[None, :], 0), axis=1
    )
    position = own_prefix + own_suffix
    queries = rotate_heads(queries, position).astype(jnp.bfloat16)
    new_keys = rotate_heads(new_keys, position).astype(jnp.bfloat16)
    every_query = lax.all_gather(
        queries.reshape(row_count, slot_count * HD), "seq", axis=0, tiled=True
    )
    every_query = every_query.reshape(-1, slot_count, HD)
    request_count = every_query.shape[0]
    score_scale = HD ** (-0.5)
    pre_keys = jnp.take(prefix_keys.reshape(group_count, prefix_span, KV_HEADS, HD), kv_ids, axis=2)
    pre_values = jnp.take(
        prefix_values.reshape(group_count, prefix_span, KV_HEADS, HD), kv_ids, axis=2
    )
    pre_scores = (
        jnp.einsum("rsd,gpsd->rsgp", every_query, pre_keys, preferred_element_type=jnp.float32)
        * score_scale
    )
    pre_spots = seq_index * prefix_span + jnp.arange(prefix_span, dtype=jnp.int32)
    group_match = group_of[:, None] == group_ids[None, :]
    length_match = pre_spots[None, :] < prefix_len[:, None]
    pre_live = group_match[:, None, :, None] & length_match[None, None, :, :]
    top_score = jnp.max(
        jnp.where(pre_live, pre_scores, NEG_FILL).reshape(request_count, slot_count, -1), axis=2
    )
    pre_weights = jnp.where(pre_live, jnp.exp(pre_scores - top_score[:, :, None, None]), 0.0)
    totals = jnp.sum(pre_weights, axis=(2, 3))
    mixed_sum = jnp.einsum(
        "rsgp,gpsd->rsd",
        pre_weights.astype(jnp.bfloat16),
        pre_values,
        preferred_element_type=jnp.float32,
    )
    gathered = (
        lax.all_to_all(top_score[None], "seq", split_axis=1, concat_axis=0, tiled=True),
        lax.all_to_all(totals[None], "seq", split_axis=1, concat_axis=0, tiled=True),
        lax.all_to_all(mixed_sum[None], "seq", split_axis=1, concat_axis=0, tiled=True),
    )
    part_top = jnp.max(gathered[0], axis=0)
    part_scale = jnp.exp(gathered[0] - part_top[None])
    part_total = jnp.sum(part_scale * gathered[1], axis=0)
    part_mixed = jnp.sum(part_scale[..., None] * gathered[2], axis=0)
    suf_keys = jnp.take(suffix_keys.reshape(row_count, suffix_span, KV_HEADS, HD), kv_ids, axis=2)
    suf_values = jnp.take(
        suffix_values.reshape(row_count, suffix_span, KV_HEADS, HD), kv_ids, axis=2
    )
    suf_scores = (
        jnp.einsum("rsd,rjsd->rsj", queries, suf_keys, preferred_element_type=jnp.float32)
        * score_scale
    )
    suf_live = (jnp.arange(suffix_span, dtype=jnp.int32)[None, :] < own_suffix[:, None])[:, None, :]
    suf_top = jnp.max(jnp.where(suf_live, suf_scores, NEG_FILL), axis=2)
    own_keys = jnp.take(new_keys, kv_ids, axis=1).astype(jnp.float32)
    own_values = jnp.take(new_values, kv_ids, axis=1).astype(jnp.float32)
    own_score = jnp.sum(queries.astype(jnp.float32) * own_keys, axis=-1) * score_scale
    final_top = jnp.maximum(jnp.maximum(part_top, suf_top), own_score)
    carried = jnp.exp(part_top - final_top)
    suf_weights = jnp.where(suf_live, jnp.exp(suf_scores - final_top[:, :, None]), 0.0)
    own_weight = jnp.exp(own_score - final_top)
    denominator = carried * part_total + jnp.sum(suf_weights, axis=2) + own_weight
    own_low = lax.optimization_barrier(own_weight.astype(jnp.bfloat16)).astype(jnp.float32)
    numerator = carried[..., None] * part_mixed + own_low[..., None] * own_values
    numerator = numerator + jnp.einsum(
        "rsj,rjsd->rsd",
        suf_weights.astype(jnp.bfloat16),
        suf_values,
        preferred_element_type=jnp.float32,
    )
    attended = (numerator / denominator[..., None] * slot_used[None, :, None]).astype(jnp.bfloat16)
    head_part = jnp.dot(
        attended.reshape(row_count, slot_count * HD), w_out, preferred_element_type=jnp.float32
    )
    head_total = lax.psum(head_part.astype(jnp.bfloat16), "tp").astype(jnp.float32)
    hidden = (tokens.astype(jnp.float32) + head_total).astype(jnp.bfloat16)
    mlp_in = rms_scale(hidden, mlp_gain)
    gate_part = jnp.dot(mlp_in, w_gate, preferred_element_type=jnp.float32)
    up_part = jnp.dot(mlp_in, w_up, preferred_element_type=jnp.float32)
    activation = (jax.nn.silu(gate_part) * up_part).astype(jnp.bfloat16)
    down_part = jnp.dot(activation, w_down, preferred_element_type=jnp.float32)
    down_total = lax.psum(down_part.astype(jnp.bfloat16), "tp").astype(jnp.float32)
    return (hidden.astype(jnp.float32) + down_total).astype(jnp.bfloat16)


def solution(mesh):
    return jax.shard_map(
        on_device,
        mesh=mesh,
        in_specs=(
            P("seq", None),
            P(),
            P(None, "tp"),
            P(),
            P(),
            P("tp", None),
            P(None, "seq", None),
            P(None, "seq", None),
            P("seq", None, None),
            P("seq", None, None),
            P(),
            P(),
            P(),
            P(),
            P(None, "tp"),
            P(None, "tp"),
            P("tp", None),
        ),
        out_specs=P("seq", None),
        check_vma=False,
    )
```

profile of v0, /device:TPU:2, one launch (start us, length us, event | category | flops | bytes accessed | tf_op | source)
XLA Modules:
  0.0 266.1 jit_solution(10958488884695363522)
XLA Ops:
  0.0 0.8 iota_compare_fusion
  0.8 0.8 dynamic_slice.6
  1.6 0.8 fusion.28
  3.1 0.8 select_reduce_fusion.1
  3.9 0.7 broadcast_compare_fusion
  4.6 1.4 fusion.61
  6.1 1.5 fusion.63
  7.9 0.8 add_convert_fusion.1
  9.7 52.5 %all_gather.3 = bf16[512,320]{1,0:T(8,128)(2,1)S(1)} all-gather(bf16[8,320]{1,0:T(8,128)(2,1)S(1)} %convert_element_type.88), channel_id=1, replica_groups=mesh['seq'=64,'tp'=4] {'seq'}, dimensions={0}, use_global_device_ids=true | all-gather | bytes 332800 | tf_op jit(solution)/shard_map/all_gather | solution.py:94
  62.3 4.7 %copy.81 = bf16[8,512,384]{1,2,0:T(8,128)(2,1)} copy(bf16[8,512,384]{2,1,0:T(8,128)(2,1)} %param.29) | data formatting | bytes 6291456 | tf_op args[6]
  67.0 3.9 %copy.82 = bf16[8,512,6,64]{1,3,0,2:T(8,128)(2,1)} copy(bf16[8,512,6,64]{1,3,2,0:T(8,128)(2,1)} %bitcast.92) | data formatting | bytes 6291456 | tf_op jit(solution)/shard_map/reshape | solution.py:100
  71.0 4.3 %gather_fusion = bf16[5,8,512,64]{2,3,1,0:T(8,128)(2,1)} fusion(bf16[8,512,6,64]{1,3,0,2:T(8,128)(2,1)} %copy.82, s32[1024]{0:T(1024)S(1)} %pad_clamp_fusion), kind=kCustom, calls=%fused_computation.clone | custom fusion | bytes 5242900 | tf_op jit(solution)/shard_map/jit(_take)/gather | solution.py:100
  75.2 2.1 broadcast_and_fusion
  77.3 19.6 %fusion = (f32[512,5]{0,1:T(8,128)S(1)}, f32[5,8,512,512]{3,2,1,0:T(8,128)}) fusion(pred[512,8,512]{0,2,1:T(8,128)(4,1)} %broadcast_and_fusion, bf16[512,5,64,1]{0,2,3,1:T(8,128)(2,1)S(1)} %bitcast.100, bf16[5,8,512,64]{2,3,1,0:T(8,128)(2,1)} %gather_fusion, pred[5]{0:T(512)(128)(4,1)S(1)} %get-tuple-element.36), kind=kOutput, calls=%fused_computation.8 | convolution fusion | flops 1374942720 | bytes 46999556 | tf_op jit(solution)/shard_map/rsd,gpsd->rsgp/dot_general | solution.py:105
  96.9 0.9 copy.87
  97.7 6.5 %all-to-all-start = ((f32[1,512,5]{2,0,1:T(1,128)}), f32[1,512,5]{2,0,1:T(1,128)S(1)}, u32[]{:S(2)}, u32[]{:S(2)}) async-start(f32[1,512,5]{2,0,1:T(1,128)} %copy.87), calls=%async_computation | async-start | bytes 524288 | tf_op jit(solution)/shard_map/all_to_all | solution.py:124
  104.2 1.5 copy.89
  105.7 0.7 gather_fusion.1
  106.4 2.3 copy.98
  108.7 1.8 gather_fusion.5
  110.5 4.7 %copy.92 = bf16[8,512,384]{1,2,0:T(8,128)(2,1)} copy(bf16[8,512,384]{2,1,0:T(8,128)(2,1)} %param.30) | data formatting | bytes 6291456 | tf_op args[7]
  115.2 3.9 %copy.93 = bf16[8,512,6,64]{1,3,0,2:T(8,128)(2,1)} copy(bf16[8,512,6,64]{1,3,2,0:T(8,128)(2,1)} %bitcast.93) | data formatting | bytes 6291456 | tf_op jit(solution)/shard_map/reshape | solution.py:102
  119.1 4.3 %gather_fusion.3 = bf16[5,8,512,64]{2,3,1,0:T(8,128)(2,1)} fusion(bf16[8,512,6,64]{1,3,0,2:T(8,128)(2,1)} %copy.93, s32[1024]{0:T(1024)S(1)} %pad_clamp_fusion), kind=kCustom, calls=%fused_computation.3.clone | custom fusion | bytes 5242900 | tf_op jit(solution)/shard_map/jit(_take)/gather | solution.py:101
  123.4 18.8 %fusion.3 = f32[512,5]{0,1:T(8,128)S(1)} fusion(f32[5,8,512,512]{3,2,1,0:T(8,128)} %get-tuple-element.35, f32[512,5]{0,1:T(8,128)S(1)} %get-tuple-element.34, pred[512,8,512]{0,2,1:T(8,128)(4,1)} %broadcast_and_fusion), kind=kLoop, calls=%fused_computation.11 | loop fusion | flops 41940480 | bytes 44060672 | tf_op jit(solution)/shard_map/reduce_sum | solution.py:116
  142.2 16.7 %fusion.18 = f32[1,512,5,64]{1,3,2,0:T(8,128)} fusion(f32[5,8,512,512]{3,2,1,0:T(8,128)} %get-tuple-element.35, f32[512,5]{0,1:T(8,128)S(1)} %get-tuple-element.34, pred[512,8,512]{0,2,1:T(8,128)(4,1)S(1)} %copy-done.2, bf16[5,8,512,64]{2,3,1,0:T(8,128)(2,1)S(1)} %copy-done.1, pred[5]{0:T(512)(128)(4,1)S(1)} %get-tuple-element.36), kind=kOutput, calls=%fused_computation.29 | convolution fusion | flops 1385431040 | bytes 47327236 | tf_op jit(solution)/shard_map/rsgp,gpsd->rsd/dot_general | solution.py:117
  159.0 1.3 select_bitcast_fusion.1
  160.5 0.9 copy.99
  161.4 10.4 %all-to-all-start.2 = ((f32[1,512,5]{2,0,1:T(1,128)}), f32[1,512,5]{2,0,1:T(1,128)}, u32[]{:S(2)}, u32[]{:S(2)}) async-start(f32[1,512,5]{2,0,1:T(1,128)} %copy.99), calls=%async_computation.2 | async-start | bytes 524288 | tf_op jit(solution)/shard_map/all_to_all | solution.py:125
  171.8 1.4 fusion.26
  173.9 2.4 copy.95
  176.9 5.9 %reduce.1 = f32[512,5,64]{2,1,0:T(8,128)} reduce(f32[512,5,1,64]{3,2,1,0:T(1,128)S(1)} %bitcast.96, f32[]{:T(128)} %broadcast.335), dimensions={2}, to_apply=%bitcast.79.reduce_sub_computation | reduce | bytes 1310724
  182.8 3.1 %reshape.341 = f32[64,1,2560]{2,1,0:T(1,128)} reshape(f32[512,5,64]{2,1,0:T(8,128)} %reduce.1) | data formatting | bytes 1310720
  185.9 10.5 %all-to-all-start.1 = ((f32[64,1,2560]{2,1,0:T(1,128)}), f32[64,1,2560]{2,1,0:T(1,128)S(1)}, u32[]{:S(2)}, u32[]{:S(2)}) async-start(f32[64,1,2560]{2,1,0:T(1,128)} %reshape.341), calls=%async_computation.1 | async-start | bytes 1310720 | tf_op jit(solution)/shard_map/all_to_all | solution.py:126
  197.8 1.5 copy.112
  199.5 0.6 add_add_fusion
  200.1 2.1 fusion.24
  202.3 14.0 %all-to-all-done.1 = f32[64,1,2560]{2,1,0:T(1,128)S(1)} async-done(((f32[64,1,2560]{2,1,0:T(1,128)}), f32[64,1,2560]{2,1,0:T(1,128)S(1)}, u32[]{:S(2)}, u32[]{:S(2)}) %all-to-all-start.1) | async-done | bytes 655392 | tf_op jit(solution)/shard_map/all_to_all | solution.py:126
  216.2 3.1 %reduce.2 = f32[64,2560]{1,0:T(8,128)} reduce(f32[64,1,2560]{2,1,0:T(1,128)S(1)} %all-to-all-done.1, f32[]{:T(128)} %broadcast.335), dimensions={1}, to_apply=%all_to_all.14.reduce_sub_computation | reduce | bytes 1310724 | tf_op jit(solution)/shard_map/all_to_all | solution.py:126
  219.4 2.7 %reshape.342 = f32[512,5,1,64]{3,2,1,0:T(1,128)S(1)} reshape(f32[64,2560]{1,0:T(8,128)} %reduce.2) | data formatting | bytes 1310720
  222.5 1.0 fusion.43
  223.5 0.7 reshape.268
  224.2 2.0 convolution_convert_fusion.1
  226.2 15.3 %psum.14 = bf16[8,1152]{1,0:T(8,128)(2,1)} all-reduce(bf16[8,1152]{1,0:T(8,128)(2,1)} %convolution_convert_fusion.1), channel_id=1, replica_groups=mesh['seq'=64,'tp'=4] {'tp'}, use_global_device_ids=true, to_apply=%region_10.14 | all-reduce | flops 9216 | bytes 36864 | tf_op jit(solution)/shard_map/psum | solution.py:162
  241.5 0.9 fusion.32
  242.9 2.5 fusion.53
  245.4 2.1 convolution_convert_fusion
  247.6 17.2 %psum.15 = bf16[8,1152]{1,0:T(8,128)(2,1)S(1)} all-reduce(bf16[8,1152]{1,0:T(8,128)(2,1)} %convolution_convert_fusion), channel_id=1, replica_groups=mesh['seq'=64,'tp'=4] {'tp'}, use_global_device_ids=true, to_apply=%region_12.16 | all-reduce | flops 9216 | bytes 36864 | tf_op jit(solution)/shard_map/psum | solution.py:169
  264.7 1.3 fusion.35
  (58 shorter events, 6.4 us)
Async XLA Ops:
  0.0 245.4 %copy-start = (bf16[768,1152]{1,0:T(8,128)(2,1)S(1)}, bf16[768,1152]{1,0:T(8,128)(2,1)}, u32[]{:S(2)}) copy-start(bf16[768,1152]{1,0:T(8,128)(2,1)} %param.39) | copy-start | bytes 5308420
  3.1 155.9 %copy-start.9 = (pred[5]{0:T(512)(128)(4,1)}, pred[5]{0:T(512)(128)(4,1)S(1)}, u32[]{:S(2)}) copy-start(pred[5]{0:T(512)(128)(4,1)S(1)} %get-tuple-element.36) | copy-start | bytes 19
  97.7 63.7 %all-to-all-start = ((f32[1,512,5]{2,0,1:T(1,128)}), f32[1,512,5]{2,0,1:T(1,128)S(1)}, u32[]{:S(2)}, u32[]{:S(2)}) async-start(f32[1,512,5]{2,0,1:T(1,128)} %copy.87), calls=%async_computation | async-start | bytes 524288 | tf_op jit(solution)/shard_map/all_to_all | solution.py:124
  123.4 18.8 %copy-start.1 = (bf16[5,8,512,64]{2,3,1,0:T(8,128)(2,1)S(1)}, bf16[5,8,512,64]{2,3,1,0:T(8,128)(2,1)}, u32[]{:S(2)}) copy-start(bf16[5,8,512,64]{2,3,1,0:T(8,128)(2,1)} %gather_fusion.3) | copy-start | bytes 7864324
  123.4 18.8 %copy-start.2 = (pred[512,8,512]{0,2,1:T(8,128)(4,1)S(1)}, pred[512,8,512]{0,2,1:T(8,128)(4,1)}, u32[]{:S(2)}) copy-start(pred[512,8,512]{0,2,1:T(8,128)(4,1)} %broadcast_and_fusion) | copy-start | bytes 6291460
  159.0 1.3 copy-start.4
  159.0 1.3 copy-start.5
  159.0 1.3 copy-start.7
  161.4 24.5 %all-to-all-start.2 = ((f32[1,512,5]{2,0,1:T(1,128)}), f32[1,512,5]{2,0,1:T(1,128)}, u32[]{:S(2)}, u32[]{:S(2)}) async-start(f32[1,512,5]{2,0,1:T(1,128)} %copy.99), calls=%async_computation.2 | async-start | bytes 524288 | tf_op jit(solution)/shard_map/all_to_all | solution.py:125
  185.9 30.4 %all-to-all-start.1 = ((f32[64,1,2560]{2,1,0:T(1,128)}), f32[64,1,2560]{2,1,0:T(1,128)S(1)}, u32[]{:S(2)}, u32[]{:S(2)}) async-start(f32[64,1,2560]{2,1,0:T(1,128)} %reshape.341), calls=%async_computation.1 | async-start | bytes 1310720 | tf_op jit(solution)/shard_map/all_to_all | solution.py:126
  222.5 22.9 %copy-start.3 = (bf16[1152,768]{1,0:T(8,128)(2,1)S(1)}, bf16[1152,768]{1,0:T(8,128)(2,1)}, u32[]{:S(2)}) copy-start(bf16[1152,768]{1,0:T(8,128)(2,1)} %param.38) | copy-start | bytes 5308420
  224.2 21.2 %copy-start.8 = (f32[1152]{0:T(1024)S(1)}, f32[1152]{0:T(1024)}, u32[]{:S(2)}) copy-start(f32[1152]{0:T(1024)} %param.36) | copy-start | bytes 13828
  242.3 0.6 copy-start.6
where the time goes:
time: 268 us; the launch traced here: 266 us
  blocking collectives  84.9 us (32%)
  matrix products  49.5 us (18%)
  local copies, waits for them, and re-layouts  48.6 us (18%)
  other arithmetic  41.5 us (15%)
  starting transfers between devices  27.3 us (10%)
  waiting for transfers between devices  14 us (5%)
    all_gather x1, blocking collectives, on_device(): lax.all_gather(queries.reshape(row_count, slot_count * HD), 'seq', axis=0...  52.5 us
    unnamed x28, local copies, waits for them, and re-layouts  20.3 us
    dot_general x1, matrix products, on_device(): jnp.einsum('rsd,gpsd->rsgp', every_query, pre_keys, preferred_element_typ...  19.6 us
    reduce_sum x1, other arithmetic, on_device(): totals = jnp.sum(pre_weights, axis=(2, 3))  18.8 us
    psum x1, blocking collectives, on_device(): lax.psum(down_part.astype(jnp.bfloat16), 'tp').astype(jnp.float32)  17.2 us
    dot_general x1, matrix products, on_device(): jnp.einsum('rsgp,gpsd->rsd', pre_weights.astype(jnp.bfloat16), pre_values...  16.7 us
    psum x1, blocking collectives, on_device(): lax.psum(head_part.astype(jnp.bfloat16), 'tp').astype(jnp.float32)  15.3 us
    all_to_all x1, waiting for transfers between devices, on_device(): lax.all_to_all(mixed_sum[None], 'seq', split_axis=1, concat_axis=0, tiled...  14 us
  transfers between devices with their start and end apart: 3, of which 1 were waited for; matrix products, arithmetic and copies ran while one was open for 29% of the time, Pallas kernels for 0%

commit v1 on v0

--- a/solution.py
+++ b/solution.py
@@ -41,6 +41,11 @@
     slot_used = (slot_ids < used_count).astype(jnp.float32)
     kv_ids = jnp.minimum(head_ids, HEADS - 1) // (HEADS // KV_HEADS)
     return (kv_ids, slot_used)
+
+
+def tp_sum(part):
+    pieces = lax.all_gather(part.astype(jnp.bfloat16), "tp", axis=0)
+    return jnp.sum(pieces.astype(jnp.float32), axis=0)
 
 
 def on_device(
@@ -91,8 +96,14 @@
     position = own_prefix + own_suffix
     queries = rotate_heads(queries, position).astype(jnp.bfloat16)
     new_keys = rotate_heads(new_keys, position).astype(jnp.bfloat16)
-    every_query = lax.all_gather(
-        queries.reshape(row_count, slot_count * HD), "seq", axis=0, tiled=True
+    seq_count = lax.axis_size("seq")
+    own_query = queries.reshape(1, row_count, slot_count * HD)
+    every_query = lax.all_to_all(
+        jnp.broadcast_to(own_query, (seq_count, row_count, slot_count * HD)),
+        "seq",
+        0,
+        0,
+        tiled=True,
     )
     every_query = every_query.reshape(-1, slot_count, HD)
     request_count = every_query.shape[0]
@@ -120,15 +131,14 @@
         pre_values,
         preferred_element_type=jnp.float32,
     )
-    gathered = (
-        lax.all_to_all(top_score[None], "seq", split_axis=1, concat_axis=0, tiled=True),
-        lax.all_to_all(totals[None], "seq", split_axis=1, concat_axis=0, tiled=True),
-        lax.all_to_all(mixed_sum[None], "seq", split_axis=1, concat_axis=0, tiled=True),
-    )
-    part_top = jnp.max(gathered[0], axis=0)
-    part_scale = jnp.exp(gathered[0] - part_top[None])
-    part_total = jnp.sum(part_scale * gathered[1], axis=0)
-    part_mixed = jnp.sum(part_scale[..., None] * gathered[2], axis=0)
+    payload = jnp.concatenate([top_score[..., None], totals[..., None], mixed_sum], axis=-1)
+    payload = payload.reshape(seq_count, row_count, slot_count, HD + 2)
+    gathered = lax.all_to_all(payload, "seq", 0, 0, tiled=True)
+    gathered_top = gathered[..., 0]
+    part_top = jnp.max(gathered_top, axis=0)
+    part_scale = jnp.exp(gathered_top - part_top[None])
+    part_total = jnp.sum(part_scale * gathered[..., 1], axis=0)
+    part_mixed = jnp.sum(part_scale[..., None] * gathered[..., 2:], axis=0)
     suf_keys = jnp.take(suffix_keys.reshape(row_count, suffix_span, KV_HEADS, HD), kv_ids, axis=2)
     suf_values = jnp.take(
         suffix_values.reshape(row_count, suffix_span, KV_HEADS, HD), kv_ids, axis=2
@@ -159,14 +169,14 @@
     head_part = jnp.dot(
         attended.reshape(row_count, slot_count * HD), w_out, preferred_element_type=jnp.float32
     )
-    head_total = lax.psum(head_part.astype(jnp.bfloat16), "tp").astype(jnp.float32)
+    head_total = tp_sum(head_part)
     hidden = (tokens.astype(jnp.float32) + head_total).astype(jnp.bfloat16)
     mlp_in = rms_scale(hidden, mlp_gain)
     gate_part = jnp.dot(mlp_in, w_gate, preferred_element_type=jnp.float32)
     up_part = jnp.dot(mlp_in, w_up, preferred_element_type=jnp.float32)
     activation = (jax.nn.silu(gate_part) * up_part).astype(jnp.bfloat16)
     down_part = jnp.dot(activation, w_down, preferred_element_type=jnp.float32)
-    down_total = lax.psum(down_part.astype(jnp.bfloat16), "tp").astype(jnp.float32)
+    down_total = tp_sum(down_part)
     return (hidden.astype(jnp.float32) + down_total).astype(jnp.bfloat16)
 
 

time: 268 us -> 197 us (0.74)
  blocking collectives: 84.9 us -> 23.8 us
  other arithmetic: 41.5 us -> 32.9 us
  starting transfers between devices: 27.3 us -> 22.4 us
  waiting for transfers between devices: 14 us -> 18.6 us
    psum x2 -> x0, blocking collectives: 32.5 us -> none  [the longest x1 17.2 us: on_device(): lax.psum(down_part.astype(jnp.bfloat16), 'tp').astype(jnp.float32)]
    all_gather x1 -> x2, blocking collectives: 52.5 us -> 23.8 us  [tp_sum(): pieces = lax.all_gather(part.astype(jnp.bfloat16), 'tp', axis=0)]
    unnamed x1 -> x0, other arithmetic: 5.94 us -> none
    all_to_all x3 -> x2, starting transfers between devices: 27.3 us -> 22.4 us  [the longest x1 12.1 us: on_device(): lax.all_to_all(jnp.broadcast_to(own_query, (seq_count, row_count, slot_co...]
    all_to_all x3 -> x2, waiting for transfers between devices: 14 us -> 18.6 us  [the longest x1 18.6 us: on_device(): gathered = lax.all_to_all(payload, 'seq', 0, 0, tiled=True)]
    concatenate x0 -> x3, local copies, waits for them, and re-layouts: none -> 4.53 us  [on_device(): jnp.concatenate([top_score[..., None], totals[..., None], mixed_sum], axi...]
    broadcast_in_dim x3 -> x1, local copies, waits for them, and re-layouts: 4.19 us -> 0.81 us  [on_device(): jnp.broadcast_to(own_query, (seq_count, row_count, slot_count * HD))]
    all_to_all x1 -> x0, other arithmetic: 3.13 us -> none  [on_device(): lax.all_to_all(mixed_sum[None], 'seq', split_axis=1, concat_axis=0, tiled...]
  transfers between devices with their start and end apart: 3 -> 2, of which waited for: 1 -> 1; matrix products, arithmetic and copies ran while one was open for 29% -> 22% of each run, Pallas kernels for 0% -> 0%
where the time goes in v1:
time: 197 us; the launch traced here: 196 us
  local copies, waits for them, and re-layouts  50.4 us (26%)
  matrix products  47.7 us (24%)
  other arithmetic  32.9 us (17%)
  blocking collectives  23.8 us (12%)
  starting transfers between devices  22.4 us (11%)
  waiting for transfers between devices  18.6 us (9%)
    all_gather x2, blocking collectives, tp_sum(): pieces = lax.all_gather(part.astype(jnp.bfloat16), 'tp', axis=0)  23.8 us
    dot_general x1, matrix products, on_device(): jnp.einsum('rsd,gpsd->rsgp', every_query, pre_keys, preferred_element_typ...  19.5 us
    reduce_sum x1, other arithmetic, on_device(): totals = jnp.sum(pre_weights, axis=(2, 3))  18.8 us
    all_to_all x1, waiting for transfers between devices, on_device(): gathered = lax.all_to_all(payload, 'seq', 0, 0, tiled=True)  18.6 us
    unnamed x22, local copies, waits for them, and re-layouts  17.7 us
    dot_general x1, matrix products, on_device(): jnp.einsum('rsgp,gpsd->rsd', pre_weights.astype(jnp.bfloat16), pre_values...  16.7 us
    all_to_all x1, starting transfers between devices, on_device(): lax.all_to_all(jnp.broadcast_to(own_query, (seq_count, row_count, slot_co...  12.1 us
    all_to_all x1, starting transfers between devices, on_device(): gathered = lax.all_to_all(payload, 'seq', 0, 0, tiled=True)  10.3 us
  transfers between devices with their start and end apart: 2, of which 1 were waited for; matrix products, arithmetic and copies ran while one was open for 22% of the time, Pallas kernels for 0%

profile of v1, /device:TPU:2, one launch (start us, length us, event | category | flops | bytes accessed | tf_op | source)
XLA Modules:
  0.0 196.1 jit_solution(12377535370962297862)
XLA Ops:
  0.1 1.0 fusion.29
  1.0 1.4 fusion.64
  2.7 1.4 fusion.66
  4.3 0.8 dynamic_slice.6
  5.1 0.8 select_reduce_fusion.1
  5.9 0.8 add_convert_fusion.1
  6.9 0.6 gather_fusion.3
  7.7 0.8 broadcast_in_dim.113
  8.5 12.1 %all-to-all-start = ((bf16[64,8,320]{2,1,0:T(8,128)(2,1)}), bf16[64,8,320]{2,1,0:T(8,128)(2,1)S(1)}, u32[]{:S(2)}, u32[]{:S(2)}) async-start(bf16[64,8,320]{2,1,0:T(8,128)(2,1)} %broadcast_in_dim.113), calls=%async_computation | async-start | bytes 786432 | tf_op jit(solution)/shard_map/all_to_all | solution.py:101
  20.7 4.7 %copy.113 = bf16[8,512,384]{1,2,0:T(8,128)(2,1)} copy(bf16[8,512,384]{2,1,0:T(8,128)(2,1)} %param.29) | data formatting | bytes 6291456 | tf_op args[6]
  25.4 3.9 %copy.114 = bf16[8,512,6,64]{1,3,0,2:T(8,128)(2,1)} copy(bf16[8,512,6,64]{1,3,2,0:T(8,128)(2,1)} %bitcast.98) | data formatting | bytes 6291456 | tf_op jit(solution)/shard_map/reshape | solution.py:111
  29.3 4.3 %gather_fusion = bf16[5,8,512,64]{2,3,1,0:T(8,128)(2,1)} fusion(bf16[8,512,6,64]{1,3,0,2:T(8,128)(2,1)} %copy.114, s32[1024]{0:T(1024)S(1)} %pad_clamp_fusion), kind=kCustom, calls=%fused_computation.clone | custom fusion | bytes 5242900 | tf_op jit(solution)/shard_map/jit(_take)/gather | solution.py:111
  33.6 4.7 %copy.119 = bf16[8,512,384]{1,2,0:T(8,128)(2,1)} copy(bf16[8,512,384]{2,1,0:T(8,128)(2,1)} %param.30) | data formatting | bytes 6291456 | tf_op args[7]
  38.3 3.9 %copy.120 = bf16[8,512,6,64]{1,3,0,2:T(8,128)(2,1)} copy(bf16[8,512,6,64]{1,3,2,0:T(8,128)(2,1)} %bitcast.99) | data formatting | bytes 6291456 | tf_op jit(solution)/shard_map/reshape | solution.py:113
  42.2 4.3 %gather_fusion.1 = bf16[5,8,512,64]{2,3,1,0:T(8,128)(2,1)} fusion(bf16[8,512,6,64]{1,3,0,2:T(8,128)(2,1)} %copy.120, s32[1024]{0:T(1024)S(1)} %pad_clamp_fusion), kind=kCustom, calls=%fused_computation.3.clone | custom fusion | bytes 5242900 | tf_op jit(solution)/shard_map/jit(_take)/gather | solution.py:112
  46.6 2.1 %broadcast_and_fusion = pred[512,8,512]{0,2,1:T(8,128)(4,1)} fusion(pred[8,512]{1,0:T(8,128)(4,1)S(1)} %broadcast_compare_fusion, pred[512,8]{0,1:T(8,128)(4,1)S(1)} %iota_compare_fusion), kind=kLoop, calls=%fused_computation.15 | loop fusion | flops 2097152 | bytes 2105344 | tf_op jit(solution)/shard_map/and | solution.py:122
  48.7 0.4 reshape.251
  49.1 19.5 %fusion = (f32[512,5]{0,1:T(8,128)S(1)}, f32[5,8,512,512]{3,2,1,0:T(8,128)}) fusion(pred[512,8,512]{0,2,1:T(8,128)(4,1)} %broadcast_and_fusion, bf16[512,5,64,1]{2,1,0,3:T(8,128)(2,1)S(1)} %bitcast.103, bf16[5,8,512,64]{2,3,1,0:T(8,128)(2,1)} %gather_fusion, pred[5]{0:T(512)(128)(4,1)S(1)} %compare_and_fusion), kind=kOutput, calls=%fused_computation.8 | convolution fusion | flops 1374942720 | bytes 46999556 | tf_op jit(solution)/shard_map/rsd,gpsd->rsgp/dot_general | solution.py:116
  68.6 1.1 concatenate.23
  69.7 18.8 %fusion.4 = f32[512,5]{0,1:T(8,128)S(1)} fusion(f32[5,8,512,512]{3,2,1,0:T(8,128)} %get-tuple-element.36, f32[512,5]{0,1:T(8,128)S(1)} %get-tuple-element.35, pred[512,8,512]{0,2,1:T(8,128)(4,1)} %broadcast_and_fusion), kind=kLoop, calls=%fused_computation.12 | loop fusion | flops 41940480 | bytes 44060672 | tf_op jit(solution)/shard_map/reduce_sum | solution.py:127
  88.5 16.7 %fusion.18 = f32[512,5,64]{0,2,1:T(8,128)} fusion(f32[5,8,512,512]{3,2,1,0:T(8,128)} %get-tuple-element.36, f32[512,5]{0,1:T(8,128)S(1)} %get-tuple-element.35, pred[512,8,512]{0,2,1:T(8,128)(4,1)S(1)} %copy-done.2, bf16[5,8,512,64]{2,3,1,0:T(8,128)(2,1)S(1)} %copy-done.1, pred[5]{0:T(512)(128)(4,1)S(1)} %compare_and_fusion), kind=kOutput, calls=%fused_computation.30 | convolution fusion | flops 1385431040 | bytes 47327236 | tf_op jit(solution)/shard_map/rsgp,gpsd->rsd/dot_general | solution.py:128
  105.3 2.6 %copy.122 = f32[512,5,64]{2,0,1:T(8,128)} copy(f32[512,5,64]{0,2,1:T(8,128)} %fusion.18) | data formatting | bytes 1310720 | tf_op jit(solution)/shard_map/rsgp,gpsd->rsd/transpose | solution.py:128
  107.8 2.2 %concatenate.24 = f32[64,8,5,1]{3,1,0,2:T(8,128)} reshape(f32[512,5]{0,1:T(8,128)S(1)} %fusion.4) | data formatting | bytes 20480 | tf_op jit(solution)/shard_map/concatenate | solution.py:134
  110.1 2.5 %pad_maximum_fusion = f32[64,8,5,66]{3,1,0,2:T(8,128)S(1)} fusion(f32[64,8,5,64]{3,1,0,2:T(8,128)} %bitcast.102, f32[64,8,5,1]{3,1,0,2:T(8,128)} %concatenate.24, f32[64,8,5,1]{3,1,0,2:T(8,128)S(1)} %concatenate.23), kind=kLoop, calls=%fused_computation.27 | loop fusion | flops 337920 | bytes 1351680 | tf_op jit(solution)/shard_map/concatenate | solution.py:134
  112.5 1.1 copy.125
  113.7 10.3 %all-to-all-start.1 = ((f32[64,8,5,66]{3,1,2,0:T(8,128)}), f32[64,8,5,66]{3,1,2,0:T(8,128)S(1)}, u32[]{:S(2)}, u32[]{:S(2)}) async-start(f32[64,8,5,66]{3,1,2,0:T(8,128)} %copy.125), calls=%async_computation.1 | async-start | bytes 2621440 | tf_op jit(solution)/shard_map/all_to_all | solution.py:136
  124.0 2.3 %copy.127 = bf16[8,128,384]{1,2,0:T(8,128)(2,1)} copy(bf16[8,128,384]{2,1,0:T(8,128)(2,1)} %param.31) | data formatting | bytes 1572864 | tf_op args[8]
  126.4 2.6 %gather_fusion.2 = bf16[5,8,128,64]{2,3,1,0:T(8,128)(2,1)} fusion(bf16[8,128,6,64]{1,3,2,0:T(8,128)(2,1)} %bitcast.100, s32[1024]{0:T(1024)S(1)} %pad_clamp_fusion), kind=kCustom, calls=%fused_computation.1.clone | custom fusion | bytes 1310740 | tf_op jit(solution)/shard_map/jit(_take)/gather | solution.py:142
  129.0 2.4 %copy.132 = bf16[8,128,384]{1,2,0:T(8,128)(2,1)} copy(bf16[8,128,384]{2,1,0:T(8,128)(2,1)} %param.32) | data formatting | bytes 1572864 | tf_op args[9]
  131.4 2.6 %gather_fusion.5 = bf16[5,8,128,64]{2,3,1,0:T(8,128)(2,1)} fusion(bf16[8,128,6,64]{1,3,2,0:T(8,128)(2,1)} %bitcast.101, s32[1024]{0:T(1024)S(1)} %pad_clamp_fusion), kind=kCustom, calls=%fused_computation.4.clone | custom fusion | bytes 1310740 | tf_op jit(solution)/shard_map/jit(_take)/gather | solution.py:143
  134.0 1.4 convolution_convert_fusion.2
  135.6 0.6 gather_fusion.4
  136.2 2.3 %select_bitcast_fusion.1 = (bf16[8,128,5,64]{1,3,0,2:T(8,128)(2,1)S(1)}, bf16[8,128,5,64]{1,3,0,2:T(8,128)(2,1)}) fusion(bf16[5,8,128,64]{2,3,1,0:T(8,128)(2,1)} %gather_fusion.2, pred[5]{0:T(512)(128)(4,1)S(1)} %compare_and_fusion, bf16[5,8,128,64]{2,3,1,0:T(8,128)(2,1)} %gather_fusion.5), kind=kLoop, calls=%fused_computation.40 | loop fusion | flops 655360 | bytes 2621445 | tf_op jit(solution)/shard_map/jit(_take)/select_n | solution.py:142
  138.5 0.3 fusion.27
  138.9 18.6 %all-to-all-done.1 = f32[64,8,5,66]{3,1,2,0:T(8,128)S(1)} async-done(((f32[64,8,5,66]{3,1,2,0:T(8,128)}), f32[64,8,5,66]{3,1,2,0:T(8,128)S(1)}, u32[]{:S(2)}, u32[]{:S(2)}) %all-to-all-start.1) | async-done | bytes 675872 | tf_op jit(solution)/shard_map/all_to_all | solution.py:136
  157.5 1.9 fusion.69
  159.4 0.2 fusion.49
  159.6 1.8 copy.148
  161.6 1.8 copy.151
  163.4 0.2 fusion.42
  163.5 1.5 fusion.25
  165.1 0.7 fusion.15
  166.0 1.3 convolution_convert_fusion.1
  167.4 11.9 %all-gather = bf16[32,1152]{1,0:T(8,128)(2,1)S(1)} all-gather(bf16[8,1152]{1,0:T(8,128)(2,1)S(1)} %convolution_convert_fusion.1), channel_id=2, replica_groups=mesh['seq'=64,'tp'=4] {'tp'}, dimensions={0}, use_global_device_ids=true | all-gather | bytes 92160 | tf_op jit(solution)/shard_map/all_gather | solution.py:47
  179.5 1.9 fusion.56
  181.3 2.2 %convolution_convert_fusion = bf16[8,1152]{1,0:T(8,128)(2,1)S(1)} fusion(bf16[768,1152]{1,0:T(8,128)(2,1)S(1)} %copy-done, bf16[1152,768]{1,0:T(8,128)(2,1)} %param.38, f32[8,768]{1,0:T(8,128)S(1)} %fusion.56, bf16[8,1152]{1,0:T(8,128)(2,1)S(1)} %get-tuple-element.8, f32[1152]{0:T(1024)S(1)} %copy-done.5, f32[8]{0:T(128)S(1)} %add_rsqrt_fusion), kind=kOutput, calls=%fused_computation.23 | convolution fusion | flops 28394496 | bytes 3605024 | tf_op jit(solution)/shard_map/dot_general | solution.py:178
  183.6 11.9 %all-gather.1 = bf16[32,1152]{1,0:T(8,128)(2,1)S(1)} all-gather(bf16[8,1152]{1,0:T(8,128)(2,1)S(1)} %convolution_convert_fusion), channel_id=3, replica_groups=mesh['seq'=64,'tp'=4] {'tp'}, dimensions={0}, use_global_device_ids=true | all-gather | bytes 92160 | tf_op jit(solution)/shard_map/all_gather | solution.py:47
  195.5 0.6 fusion.36
  (53 shorter events, 1.9 us)
Async XLA Ops:
  0.0 181.3 %copy-start = (bf16[768,1152]{1,0:T(8,128)(2,1)S(1)}, bf16[768,1152]{1,0:T(8,128)(2,1)}, u32[]{:S(2)}) copy-start(bf16[768,1152]{1,0:T(8,128)(2,1)} %param.39) | copy-start | bytes 5308420
  0.0 20.7 %copy-start.7 = (s32[8]{0:T(128)S(1)}, s32[8]{0:T(128)}, u32[]{:S(2)}) copy-start(s32[8]{0:T(128)} %param.34) | copy-start | bytes 100
  8.5 40.1 %all-to-all-start = ((bf16[64,8,320]{2,1,0:T(8,128)(2,1)}), bf16[64,8,320]{2,1,0:T(8,128)(2,1)S(1)}, u32[]{:S(2)}, u32[]{:S(2)}) async-start(bf16[64,8,320]{2,1,0:T(8,128)(2,1)} %broadcast_in_dim.113), calls=%async_computation | async-start | bytes 786432 | tf_op jit(solution)/shard_map/all_to_all | solution.py:101
  42.2 4.3 %copy-start.6 = (s32[512]{0:T(512)S(1)}, s32[512]{0:T(512)}, u32[]{:S(2)}) copy-start(s32[512]{0:T(512)} %param.33) | copy-start | bytes 6148
  69.7 18.8 %copy-start.1 = (bf16[5,8,512,64]{2,3,1,0:T(8,128)(2,1)S(1)}, bf16[5,8,512,64]{2,3,1,0:T(8,128)(2,1)}, u32[]{:S(2)}) copy-start(bf16[5,8,512,64]{2,3,1,0:T(8,128)(2,1)} %gather_fusion.1) | copy-start | bytes 7864324
  69.7 18.8 %copy-start.2 = (pred[512,8,512]{0,2,1:T(8,128)(4,1)S(1)}, pred[512,8,512]{0,2,1:T(8,128)(4,1)}, u32[]{:S(2)}) copy-start(pred[512,8,512]{0,2,1:T(8,128)(4,1)} %broadcast_and_fusion) | copy-start | bytes 6291460
  113.7 43.8 %all-to-all-start.1 = ((f32[64,8,5,66]{3,1,2,0:T(8,128)}), f32[64,8,5,66]{3,1,2,0:T(8,128)S(1)}, u32[]{:S(2)}, u32[]{:S(2)}) async-start(f32[64,8,5,66]{3,1,2,0:T(8,128)} %copy.125), calls=%async_computation.1 | async-start | bytes 2621440 | tf_op jit(solution)/shard_map/all_to_all | solution.py:136
  129.0 5.0 %copy-start.3 = (bf16[8,1152]{1,0:T(8,128)(2,1)S(1)}, bf16[8,1152]{1,0:T(8,128)(2,1)}, u32[]{:S(2)}) copy-start(bf16[8,1152]{1,0:T(8,128)(2,1)} %param.23) | copy-start | bytes 55300
  129.0 5.0 %copy-start.4 = (f32[1152]{0:T(1024)S(1)}, f32[1152]{0:T(1024)}, u32[]{:S(2)}) copy-start(f32[1152]{0:T(1024)} %param.24) | copy-start | bytes 13828
  161.3 18.1 %copy-start.5 = (f32[1152]{0:T(1024)S(1)}, f32[1152]{0:T(1024)}, u32[]{:S(2)}) copy-start(f32[1152]{0:T(1024)} %param.36) | copy-start | bytes 13828

commit v2 on v1

--- a/solution.py
+++ b/solution.py
@@ -1,6 +1,8 @@
 import jax
 import jax.numpy as jnp
 from jax import lax
+from jax.experimental import pallas as pl
+from jax.experimental.pallas import tpu as pltpu
 from jax.sharding import PartitionSpec as P
 
 HEADS = 18
@@ -9,6 +11,116 @@
 
 
 NEG_FILL = -1e30
+TILE = 64
+
+
+def prefix_kernel(tile_of, group_at, valid, limit, q_ref, rg_ref, cm_ref, k_ref, v_ref, m_ref, l_ref, a_ref):
+    step = pl.program_id(0)
+    tile = tile_of[step]
+    first = jnp.logical_or(step == 0, tile_of[jnp.maximum(step - 1, 0)] != tile)
+
+    @pl.when(first)
+    def _():
+        m_ref[...] = jnp.full(m_ref.shape, NEG_FILL, jnp.float32)
+        l_ref[...] = jnp.zeros(l_ref.shape, jnp.float32)
+        a_ref[...] = jnp.zeros(a_ref.shape, jnp.float32)
+
+    group = group_at[step]
+    live_count = limit[group]
+
+    @pl.when(jnp.logical_and(valid[step] == 1, live_count > 0))
+    def _():
+        scores = lax.dot_general(
+            q_ref[...], k_ref[0], (((1,), (1,)), ((), ())), preferred_element_type=jnp.float32
+        ) * (HD ** (-0.5))
+        row_live = rg_ref[...] == group
+        spots = lax.broadcasted_iota(jnp.int32, scores.shape, 1)
+        live = jnp.logical_and(spots < live_count, row_live)
+        top = jnp.max(jnp.where(live, scores, NEG_FILL), axis=1, keepdims=True)
+        weights = jnp.where(live, jnp.exp(scores - top), 0.0)
+        total = jnp.sum(weights, axis=1, keepdims=True)
+        mixed = jnp.dot(weights.astype(jnp.bfloat16), v_ref[0], preferred_element_type=jnp.float32)
+        mixed = mixed * cm_ref[...]
+        lanes = a_ref.shape[1]
+        folded = mixed[:, 0:lanes]
+        for block in range(1, mixed.shape[1] // lanes):
+            folded = folded + mixed[:, block * lanes : (block + 1) * lanes]
+        m_ref[...] = jnp.where(row_live, top, m_ref[...])
+        l_ref[...] = jnp.where(row_live, total, l_ref[...])
+        a_ref[...] = jnp.where(row_live, folded, a_ref[...])
+
+
+def prefix_partials(every_query, group_of, prefix_len, seq_index, prefix_keys, prefix_values, kv_ids):
+    request_count, slot_count, _ = every_query.shape
+    group_count, prefix_span, width = prefix_keys.shape
+    tile_count = request_count // TILE
+    visit_count = tile_count + group_count - 1
+    order_key = group_of * request_count + jnp.arange(request_count, dtype=jnp.int32)
+    rank = jnp.sum((order_key[None, :] < order_key[:, None]).astype(jnp.int32), axis=1)
+    spots = jnp.arange(request_count, dtype=jnp.int32)
+    perm = jnp.sum(
+        jnp.where(rank[None, :] == spots[:, None], spots[None, :], 0), axis=1
+    )
+    sorted_groups = jnp.take(group_of, perm)
+    sorted_query = jnp.take(every_query, perm, axis=0)
+    low = sorted_groups[0::TILE]
+    high = sorted_groups[TILE - 1 :: TILE]
+    spans = high - low + 1
+    ends = jnp.cumsum(spans)
+    starts = ends - spans
+    visits = jnp.arange(visit_count, dtype=jnp.int32)
+    tile_of = jnp.minimum(jnp.sum((ends[None, :] <= visits[:, None]).astype(jnp.int32), axis=1), tile_count - 1)
+    valid = (visits < ends[-1]).astype(jnp.int32)
+    group_at = jnp.where(valid == 1, jnp.take(low, tile_of) + visits - jnp.take(starts, tile_of), high[-1])
+    limit = jnp.clip(prefix_len - seq_index * prefix_span, 0, prefix_span).astype(jnp.int32)
+    head_blocks = width // HD
+    col_block = jnp.arange(width, dtype=jnp.int32) // HD
+    in_block = col_block[None, :] == kv_ids[:, None]
+    padded = jnp.where(
+        in_block[None], jnp.tile(sorted_query, (1, 1, head_blocks)), jnp.zeros((), sorted_query.dtype)
+    ).reshape(request_count * slot_count, width)
+    row_groups = jnp.repeat(sorted_groups, slot_count).reshape(-1, 1)
+    col_mask = jnp.tile(in_block.astype(jnp.float32), (TILE, 1))
+    rows = TILE * slot_count
+    lanes = 128
+    grid_spec = pltpu.PrefetchScalarGridSpec(
+        num_scalar_prefetch=4,
+        grid=(visit_count,),
+        in_specs=[
+            pl.BlockSpec((rows, width), lambda i, t, g, ok, lim: (t[i], 0)),
+            pl.BlockSpec((rows, 1), lambda i, t, g, ok, lim: (t[i], 0)),
+            pl.BlockSpec((rows, width), lambda i, t, g, ok, lim: (0, 0)),
+            pl.BlockSpec((1, prefix_span, width), lambda i, t, g, ok, lim: (g[i], 0, 0)),
+            pl.BlockSpec((1, prefix_span, width), lambda i, t, g, ok, lim: (g[i], 0, 0)),
+        ],
+        out_specs=[
+            pl.BlockSpec((rows, 1), lambda i, t, g, ok, lim: (t[i], 0)),
+            pl.BlockSpec((rows, 1), lambda i, t, g, ok, lim: (t[i], 0)),
+            pl.BlockSpec((rows, lanes), lambda i, t, g, ok, lim: (t[i], 0)),
+        ],
+    )
+    flops = visit_count * 4 * rows * width * prefix_span
+    top, total, mixed = pl.pallas_call(
+        prefix_kernel,
+        grid_spec=grid_spec,
+        out_shape=[
+            jax.ShapeDtypeStruct((request_count * slot_count, 1), jnp.float32),
+            jax.ShapeDtypeStruct((request_count * slot_count, 1), jnp.float32),
+            jax.ShapeDtypeStruct((request_count * slot_count, lanes), jnp.float32),
+        ],
+        compiler_params=pltpu.CompilerParams(dimension_semantics=("arbitrary",)),
+        cost_estimate=pl.CostEstimate(
+            flops=flops,
+            transcendentals=visit_count * rows * prefix_span,
+            bytes_accessed=visit_count * 2 * prefix_span * width * 2 + request_count * slot_count * width * 2,
+        ),
+    )(tile_of, group_at, valid, limit, padded, row_groups, col_mask, prefix_keys, prefix_values)
+    top = jnp.take(top.reshape(request_count, slot_count), rank, axis=0)
+    total = jnp.take(total.reshape(request_count, slot_count), rank, axis=0)
+    mixed = mixed.reshape(request_count, slot_count, lanes)
+    mixed = jnp.where((kv_ids % 2 == 0)[None, :, None], mixed[..., :HD], mixed[..., HD : 2 * HD])
+    mixed = jnp.take(mixed, rank, axis=0)
+    return top, total, mixed
 
 
 def rms_scale(values_in, gain_row):
@@ -106,30 +218,9 @@
         tiled=True,
     )
     every_query = every_query.reshape(-1, slot_count, HD)
-    request_count = every_query.shape[0]
     score_scale = HD ** (-0.5)
-    pre_keys = jnp.take(prefix_keys.reshape(group_count, prefix_span, KV_HEADS, HD), kv_ids, axis=2)
-    pre_values = jnp.take(
-        prefix_values.reshape(group_count, prefix_span, KV_HEADS, HD), kv_ids, axis=2
-    )
-    pre_scores = (
-        jnp.einsum("rsd,gpsd->rsgp", every_query, pre_keys, preferred_element_type=jnp.float32)
-        * score_scale
-    )
-    pre_spots = seq_index * prefix_span + jnp.arange(prefix_span, dtype=jnp.int32)
-    group_match = group_of[:, None] == group_ids[None, :]
-    length_match = pre_spots[None, :] < prefix_len[:, None]
-    pre_live = group_match[:, None, :, None] & length_match[None, None, :, :]
-    top_score = jnp.max(
-        jnp.where(pre_live, pre_scores, NEG_FILL).reshape(request_count, slot_count, -1), axis=2
-    )
-    pre_weights = jnp.where(pre_live, jnp.exp(pre_scores - top_score[:, :, None, None]), 0.0)
-    totals = jnp.sum(pre_weights, axis=(2, 3))
-    mixed_sum = jnp.einsum(
-        "rsgp,gpsd->rsd",
-        pre_weights.astype(jnp.bfloat16),
-        pre_values,
-        preferred_element_type=jnp.float32,
+    top_score, totals, mixed_sum = prefix_partials(
+        every_query, group_of, prefix_len, seq_index, prefix_keys, prefix_values, kv_ids
     )
     payload = jnp.concatenate([top_score[..., None], totals[..., None], mixed_sum], axis=-1)
     payload = payload.reshape(seq_count, row_count, slot_count, HD + 2)

time: 197 us -> 189 us (0.959)
  matrix products: 47.7 us -> 12 us
  Pallas kernels: 0 us -> 18.9 us
  local copies, waits for them, and re-layouts: 50.4 us -> 62.4 us
  starting transfers between devices: 22.4 us -> 20.1 us
    dot_general x2 -> x0, matrix products: 36.2 us -> none  [the longest x1 19.5 us: on_device(): jnp.einsum('rsd,gpsd->rsgp', every_query, pre_keys, preferred_element_typ...]
    pallas_call x0 -> x1, Pallas kernels: none -> 18.9 us  [prefix_partials(): pl.pallas_call(prefix_kernel, grid_spec=grid_spec, out_shape=[jax.ShapeDt...]
    reduce_sum x1 -> x3, other arithmetic: 18.8 us -> 0.52 us  [the longest x1 0.25 us: prefix_partials(): jnp.sum((order_key[None, :] < order_key[:, None]).astype(jnp.int32), axis=1)]
    another operation x0 -> x5, local copies, waits for them, and re-layouts: none -> 13.3 us  [the longest x2 10.8 us: prefix_partials(): jnp.tile(sorted_query, (1, 1, head_blocks))]
    select_n x1 -> x11, other arithmetic: 0.02 us -> 13 us  [the longest x1 4.13 us: prefix_partials(): jnp.where((kv_ids % 2 == 0)[None, :, None], mixed[..., :HD], mixed[..., H...]
    unnamed x22 -> x26, local copies, waits for them, and re-layouts: 17.7 us -> 8.86 us
    reshape x2 -> x3, local copies, waits for them, and re-layouts: 7.82 us -> 3.06 us  [the longest x1 2.63 us: prefix_partials(): mixed = mixed.reshape(request_count, slot_count, lanes)]
    gather x2 -> x7, local copies, waits for them, and re-layouts: 8.61 us -> 13.2 us  [the longest x1 3.91 us: prefix_partials(): mixed = jnp.take(mixed, rank, axis=0)]
  transfers between devices with their start and end apart: 2 -> 2, of which waited for: 1 -> 1; matrix products, arithmetic and copies ran while one was open for 22% -> 17% of each run, Pallas kernels for 0% -> 0%
where the time goes in v2:
time: 189 us; the launch traced here: 188 us
  local copies, waits for them, and re-layouts  62.4 us (33%)
  other arithmetic  32.1 us (17%)
  blocking collectives  24 us (13%)
  starting transfers between devices  20.1 us (11%)
  Pallas kernels  18.9 us (10%)
  waiting for transfers between devices  18.1 us (10%)
  matrix products  12 us (6%)
    all_gather x2, blocking collectives, tp_sum(): pieces = lax.all_gather(part.astype(jnp.bfloat16), 'tp', axis=0)  24 us
    pallas_call x1, Pallas kernels, prefix_partials(): pl.pallas_call(prefix_kernel, grid_spec=grid_spec, out_shape=[jax.ShapeDt...  18.9 us
    all_to_all x1, waiting for transfers between devices, on_device(): gathered = lax.all_to_all(payload, 'seq', 0, 0, tiled=True)  18.1 us
    all_to_all x1, starting transfers between devices, on_device(): lax.all_to_all(jnp.broadcast_to(own_query, (seq_count, row_count, slot_co...  12.3 us
    another operation x2, local copies, waits for them, and re-layouts, prefix_partials(): jnp.tile(sorted_query, (1, 1, head_blocks))  10.8 us
    unnamed x26, local copies, waits for them, and re-layouts  8.86 us
    concatenate x2, local copies, waits for them, and re-layouts, on_device(): jnp.concatenate([top_score[..., None], totals[..., None], mixed_sum], axi...  8.77 us
    all_to_all x1, starting transfers between devices, on_device(): gathered = lax.all_to_all(payload, 'seq', 0, 0, tiled=True)  7.8 us
  transfers between devices with their start and end apart: 2, of which 1 were waited for; matrix products, arithmetic and copies ran while one was open for 17% of the time, Pallas kernels for 0%

profile of v2, /device:TPU:2, one launch (start us, length us, event | category | flops | bytes accessed | tf_op | source)
XLA Modules:
  0.0 188.1 jit_solution(1028413742653875878)
XLA Ops:
  0.1 1.0 fusion.6
  1.1 1.4 fusion.44
  2.7 1.4 fusion.46
  7.2 12.3 %all-to-all-start = ((bf16[64,8,320]{2,1,0:T(8,128)(2,1)}), bf16[64,8,320]{2,1,0:T(8,128)(2,1)}, u32[]{:S(2)}, u32[]{:S(2)}) async-start(bf16[64,8,320]{2,1,0:T(8,128)(2,1)} %broadcast_in_dim.175), calls=%async_computation | async-start | bytes 786432 | tf_op jit(solution)/shard_map/all_to_all | solution.py:213
  20.0 3.5 %gather_fusion = s32[512]{0:T(512)S(1)} fusion(s32[512]{0:T(512)S(1)} %copy-done.1, s32[1024]{0:T(1024)S(1)} %pad_clamp_fusion.4), kind=kCustom, calls=%fused_computation.8 | custom fusion | bytes 6144 | tf_op jit(solution)/shard_map/jit(_take)/gather | solution.py:64
  25.8 2.2 %broadcast_in_dim.171 = pred[2560,384]{1,0:T(8,128)(4,1)} reshape(pred[512,5,384]{2,1,0:T(8,128)(4,1)S(1)} %broadcast_in_dim.170) | data formatting | bytes 1966080 | tf_op jit(solution)/shard_map/jit(_where)/broadcast_in_dim | solution.py:79
  29.3 1.2 compare_convert_fusion.1.valid
  30.7 1.6 reshape_reshape.4.rg_ref
  32.4 0.9 tile.21.cm_ref
  33.8 1.9 compare_select_fusion.9
  35.7 2.3 %reshape.368 = bf16[512,5,64]{2,1,0:T(8,128)(2,1)} reshape(bf16[64,8,320]{2,1,0:T(8,128)(2,1)} %all-to-all-done) | data formatting | bytes 655360 | tf_op jit(solution)/shard_map/reshape | solution.py:220
  38.1 2.4 %gather_fusion.1 = bf16[512,5,64]{2,1,0:T(8,128)(2,1)S(1)} fusion(bf16[512,5,64]{2,1,0:T(8,128)(2,1)} %reshape.368, s32[1024]{0:T(1024)S(1)} %pad_clamp_fusion.4), kind=kCustom, calls=%fused_computation.9 | custom fusion | bytes 657408 | tf_op jit(solution)/shard_map/jit(_take)/gather | solution.py:65
  40.4 1.8 broadcast_select_fusion
  42.2 3.2 %tile.8 = bf16[512,1,5,6,64]{4,3,2,0,1:T(8,128)(2,1)} broadcast(bf16[512,5,64]{2,1,0:T(8,128)(2,1)S(1)} %broadcast_select_fusion), dimensions={0,2,4} | broadcast | bytes 2293760 | tf_op jit(solution)/shard_map/tile | solution.py:80
  45.4 7.6 %tile.9 = bf16[2560,384]{1,0:T(8,128)(2,1)} reshape(bf16[512,1,5,6,64]{4,3,2,0,1:T(8,128)(2,1)} %tile.8) | data formatting | bytes 3932160 | tf_op jit(solution)/shard_map/tile | solution.py:80
  53.0 3.2 %broadcast_select_fusion.1.q_ref = bf16[2560,384]{1,0:T(8,128)(2,1)} fusion(pred[2560,384]{1,0:T(8,128)(4,1)S(1)} %copy-done.3, bf16[2560,384]{1,0:T(8,128)(2,1)} %tile.9), kind=kLoop, calls=%fused_computation.25 | loop fusion | flops 983040 | bytes 4915200 | tf_op jit(solution)/shard_map/jit(_where)/select_n | solution.py:79
  56.2 18.9 %shard_map.163 = (f32[2560,1]{1,0:T(8,128)}, f32[2560,1]{1,0:T(8,128)}, f32[2560,128]{1,0:T(8,128)}) custom-call(s32[15]{0:T(128)} %get-tuple-element.47.tile_of, s32[15]{0:T(128)} %get-tuple-element.46.group_at, s32[15]{0:T(128)} %compare_convert_fusion.1.valid, s32[8]{0:T(128)} %subtract_clamp_fusion.limit, ...), custom_call_target="tpu_custom_call" | custom-call | flops 3774873600 | bytes 13762560 | tf_op jit(solution)/shard_map/pallas_call | solution.py:103
  75.1 1.8 reduce.1
  77.8 1.0 gather_fusion.5
  78.8 1.0 gather_fusion.6
  79.9 0.8 select_bitcast_fusion.3
  80.7 4.3 %copy.60 = f32[64,8,5,1]{3,1,2,0:T(8,128)S(1)} copy(f32[64,8,5,1]{2,1,0,3:T(8,128)} %get-tuple-element.44) | data formatting | bytes 20480 | tf_op jit(solution)/shard_map/concatenate | solution.py:225
  85.0 4.5 %copy.61 = f32[64,8,5,1]{3,1,2,0:T(8,128)} copy(f32[64,8,5,1]{2,1,0,3:T(8,128)S(1)} %get-tuple-element.45) | data formatting | bytes 20480 | tf_op jit(solution)/shard_map/concatenate | solution.py:225
  89.5 2.6 %reshape.371 = f32[512,5,128]{2,1,0:T(8,128)} reshape(f32[2560,128]{1,0:T(8,128)} %get-tuple-element.14) | data formatting | bytes 2621440 | tf_op jit(solution)/shard_map/reshape | solution.py:120
  92.1 4.1 %slice_select_fusion = f32[512,5,64]{2,1,0:T(8,128)} fusion(f32[512,5,128]{2,1,0:T(8,128)} %reshape.371, pred[5]{0:T(512)(128)(4,1)S(1)} %get-tuple-element.53), kind=kLoop, calls=%fused_computation.13 | loop fusion | flops 163840 | bytes 1966085 | tf_op jit(solution)/shard_map/jit(_where)/select_n | solution.py:121
  96.2 3.9 %gather_fusion.2 = f32[512,5,64]{2,1,0:T(8,128)} fusion(f32[512,5,64]{2,1,0:T(8,128)} %slice_select_fusion, s32[1024]{0:T(1024)S(1)} %pad_clamp_fusion.1), kind=kCustom, calls=%fused_computation.10 | custom fusion | bytes 1312768 | tf_op jit(solution)/shard_map/jit(_take)/gather | solution.py:122
  100.1 2.0 %copy_select_fusion = f32[64,8,5,64]{3,1,2,0:T(8,128)S(1)} fusion(f32[64,8,5,64]{3,2,1,0:T(8,128)} %bitcast.78, pred[64,8]{1,0:T(8,128)(4,1)S(1)} %compare_and_fusion), kind=kLoop, calls=%fused_computation.17 | loop fusion | flops 163840 | bytes 1311232 | tf_op jit(solution)/shard_map/jit(_take)/select_n | solution.py:122
  102.2 1.9 pad_maximum_fusion
  104.0 7.8 %all-to-all-start.1 = ((f32[64,8,5,66]{3,1,2,0:T(8,128)}), f32[64,8,5,66]{3,1,2,0:T(8,128)S(1)}, u32[]{:S(2)}, u32[]{:S(2)}) async-start(f32[64,8,5,66]{3,1,2,0:T(8,128)} %pad_maximum_fusion), calls=%async_computation.1 | async-start | bytes 2621440 | tf_op jit(solution)/shard_map/all_to_all | solution.py:227
  111.9 2.3 %copy.70 = bf16[8,128,384]{1,2,0:T(8,128)(2,1)} copy(bf16[8,128,384]{2,1,0:T(8,128)(2,1)} %param.34) | data formatting | bytes 1572864 | tf_op args[9]
  114.2 2.6 %gather_fusion.10 = bf16[5,8,128,64]{2,3,1,0:T(8,128)(2,1)} fusion(bf16[8,128,6,64]{1,3,2,0:T(8,128)(2,1)} %bitcast.76, s32[1024]{0:T(1024)S(1)} %pad_clamp_fusion), kind=kCustom, calls=%fused_computation.6.clone | custom fusion | bytes 1310740 | tf_op jit(solution)/shard_map/jit(_take)/gather | solution.py:234
  116.8 2.3 %copy.63 = bf16[8,128,384]{1,2,0:T(8,128)(2,1)} copy(bf16[8,128,384]{2,1,0:T(8,128)(2,1)} %param.33) | data formatting | bytes 1572864 | tf_op args[8]
  119.2 2.7 %gather_fusion.7 = bf16[5,8,128,64]{2,3,1,0:T(8,128)(2,1)} fusion(bf16[8,128,6,64]{1,3,2,0:T(8,128)(2,1)} %bitcast.77, s32[1024]{0:T(1024)S(1)} %pad_clamp_fusion), kind=kCustom, calls=%fused_computation.2.clone | custom fusion | bytes 1310740 | tf_op jit(solution)/shard_map/jit(_take)/gather | solution.py:233
  121.9 1.4 convolution_convert_fusion.2
  124.6 2.3 %select_bitcast_fusion.1 = (bf16[8,128,5,64]{1,3,0,2:T(8,128)(2,1)S(1)}, bf16[8,128,5,64]{1,3,0,2:T(8,128)(2,1)}) fusion(bf16[5,8,128,64]{2,3,1,0:T(8,128)(2,1)} %gather_fusion.7, pred[5]{0:T(512)(128)(4,1)S(1)} %get-tuple-element.52, bf16[5,8,128,64]{2,3,1,0:T(8,128)(2,1)} %gather_fusion.10), kind=kLoop, calls=%fused_computation.31 | loop fusion | flops 655360 | bytes 2621445 | tf_op jit(solution)/shard_map/jit(_take)/select_n | solution.py:233
  127.2 18.1 %all-to-all-done.1 = f32[64,8,5,66]{3,1,2,0:T(8,128)S(1)} async-done(((f32[64,8,5,66]{3,1,2,0:T(8,128)}), f32[64,8,5,66]{3,1,2,0:T(8,128)S(1)}, u32[]{:S(2)}, u32[]{:S(2)}) %all-to-all-start.1) | async-done | bytes 675872 | tf_op jit(solution)/shard_map/all_to_all | solution.py:227
  145.4 1.9 %fusion.49 = (f32[64,8,5,1]{3,1,2,0:T(8,128)}, f32[8,5]{0,1:T(8,128)S(1)}, f32[64,8,5,1]{3,1,2,0:T(8,128)}) fusion(f32[64,8,5,66]{3,1,2,0:T(8,128)S(1)} %all-to-all-done.1), kind=kLoop, calls=%fused_computation.145 | loop fusion | flops 2520 | bytes 41120 | tf_op jit(solution)/shard_map/slice | solution.py:231
  147.2 1.8 copy.82
  149.0 1.8 copy.85
  151.4 1.5 fusion.2
  153.7 0.9 fusion.23
  155.3 1.3 convolution_convert_fusion.1
  156.6 11.9 %all-gather = bf16[32,1152]{1,0:T(8,128)(2,1)S(1)} all-gather(bf16[8,1152]{1,0:T(8,128)(2,1)S(1)} %convolution_convert_fusion.1), channel_id=2, replica_groups=mesh['seq'=64,'tp'=4] {'tp'}, dimensions={0}, use_global_device_ids=true | all-gather | bytes 92160 | tf_op jit(solution)/shard_map/all_gather | solution.py:159
  168.6 0.8 fusion.10
  170.0 2.5 %fusion.36 = f32[8,768]{1,0:T(8,128)} fusion(bf16[1152,768]{1,0:T(8,128)(2,1)} %param.39, bf16[8,1152]{1,0:T(8,128)(2,1)S(1)} %get-tuple-element.16, f32[1152]{0:T(1024)} %param.38, f32[8]{0:T(128)S(1)} %add_rsqrt_fusion), kind=kOutput, calls=%fused_computation.126 | convolution fusion | flops 14192640 | bytes 1817120 | tf_op jit(solution)/shard_map/dot_general | solution.py:266
  172.5 2.1 %convolution_convert_fusion = bf16[8,1152]{1,0:T(8,128)(2,1)} fusion(bf16[768,1152]{1,0:T(8,128)(2,1)S(1)} %copy-done, bf16[1152,768]{1,0:T(8,128)(2,1)S(1)} %copy-done.4, f32[8,768]{1,0:T(8,128)} %fusion.36, bf16[8,1152]{1,0:T(8,128)(2,1)} %copy-done.7, f32[1152]{0:T(1024)S(1)} %copy-done.9, f32[8]{0:T(128)S(1)} %add_rsqrt_fusion), kind=kOutput, calls=%fused_computation.11 | convolution fusion | flops 28394496 | bytes 3605024 | tf_op jit(solution)/shard_map/dot_general | solution.py:269
  174.7 12.1 %all-gather.1 = bf16[32,1152]{1,0:T(8,128)(2,1)S(1)} all-gather(bf16[8,1152]{1,0:T(8,128)(2,1)} %convolution_convert_fusion), channel_id=3, replica_groups=mesh['seq'=64,'tp'=4] {'tp'}, dimensions={0}, use_global_device_ids=true | all-gather | bytes 92160 | tf_op jit(solution)/shard_map/all_gather | solution.py:159
  186.8 1.3 fusion.13
  (98 shorter events, 13.3 us)
Async XLA Ops:
  0.0 172.5 %copy-start = (bf16[768,1152]{1,0:T(8,128)(2,1)S(1)}, bf16[768,1152]{1,0:T(8,128)(2,1)}, u32[]{:S(2)}) copy-start(bf16[768,1152]{1,0:T(8,128)(2,1)} %param.41) | copy-start | bytes 5308420
  0.0 4.3 %copy-start.1 = (s32[512]{0:T(512)S(1)}, s32[512]{0:T(512)}, u32[]{:S(2)}) copy-start(s32[512]{0:T(512)} %param.35) | copy-start | bytes 6148
  0.0 4.4 %copy-start.10 = (s32[8]{0:T(128)S(1)}, s32[8]{0:T(128)}, u32[]{:S(2)}) copy-start(s32[8]{0:T(128)} %param.36) | copy-start | bytes 100
  7.2 28.5 %all-to-all-start = ((bf16[64,8,320]{2,1,0:T(8,128)(2,1)}), bf16[64,8,320]{2,1,0:T(8,128)(2,1)}, u32[]{:S(2)}, u32[]{:S(2)}) async-start(bf16[64,8,320]{2,1,0:T(8,128)(2,1)} %broadcast_in_dim.175), calls=%async_computation | async-start | bytes 786432 | tf_op jit(solution)/shard_map/all_to_all | solution.py:213
  45.4 7.6 %copy-start.3 = (pred[2560,384]{1,0:T(8,128)(4,1)S(1)}, pred[2560,384]{1,0:T(8,128)(4,1)}, u32[]{:S(2)}) copy-start(pred[2560,384]{1,0:T(8,128)(4,1)} %broadcast_in_dim.171) | copy-start | bytes 2949124
  75.1 2.1 %copy-start.5 = (f32[2560,1]{1,0:T(8,128)S(1)}, f32[2560,1]{1,0:T(8,128)}, u32[]{:S(2)}) copy-start(f32[2560,1]{1,0:T(8,128)} %get-tuple-element.13) | copy-start | bytes 30724
  100.1 2.0 %copy-start.2 = (f32[64,8,5,1]{3,1,2,0:T(8,128)S(1)}, f32[64,8,5,1]{3,1,2,0:T(8,128)}, u32[]{:S(2)}) copy-start(f32[64,8,5,1]{3,1,2,0:T(8,128)} %copy.61) | copy-start | bytes 30724
  104.0 41.3 %all-to-all-start.1 = ((f32[64,8,5,66]{3,1,2,0:T(8,128)}), f32[64,8,5,66]{3,1,2,0:T(8,128)S(1)}, u32[]{:S(2)}, u32[]{:S(2)}) async-start(f32[64,8,5,66]{3,1,2,0:T(8,128)} %pad_maximum_fusion), calls=%async_computation.1 | async-start | bytes 2621440 | tf_op jit(solution)/shard_map/all_to_all | solution.py:227
  119.2 2.7 %copy-start.6 = (bf16[8,1152]{1,0:T(8,128)(2,1)S(1)}, bf16[8,1152]{1,0:T(8,128)(2,1)}, u32[]{:S(2)}) copy-start(bf16[8,1152]{1,0:T(8,128)(2,1)} %param.25) | copy-start | bytes 55300
  119.2 2.7 %copy-start.8 = (f32[1152]{0:T(1024)S(1)}, f32[1152]{0:T(1024)}, u32[]{:S(2)}) copy-start(f32[1152]{0:T(1024)} %param.26) | copy-start | bytes 13828
  153.7 18.8 %copy-start.4 = (bf16[1152,768]{1,0:T(8,128)(2,1)S(1)}, bf16[1152,768]{1,0:T(8,128)(2,1)}, u32[]{:S(2)}) copy-start(bf16[1152,768]{1,0:T(8,128)(2,1)} %param.40) | copy-start | bytes 5308420
  155.3 17.2 %copy-start.9 = (f32[1152]{0:T(1024)S(1)}, f32[1152]{0:T(1024)}, u32[]{:S(2)}) copy-start(f32[1152]{0:T(1024)} %param.38) | copy-start | bytes 13828
  169.4 0.6 copy-start.7

commit v3 on v1

--- a/solution.py
+++ b/solution.py
@@ -1,6 +1,8 @@
 import jax
 import jax.numpy as jnp
 from jax import lax
+from jax.experimental import pallas as pl
+from jax.experimental.pallas import tpu as pltpu
 from jax.sharding import PartitionSpec as P
 
 HEADS = 18
@@ -9,6 +11,130 @@
 
 
 NEG_FILL = -1e30
+TILE = 64
+
+
+def prefix_kernel(tile_of, group_at, valid, limit, kv, perm_ref, sg_ref, q_ref, k_ref, v_ref, o_ref):
+    step = pl.program_id(0)
+    tile = tile_of[step]
+    first = jnp.logical_or(step == 0, tile_of[jnp.maximum(step - 1, 0)] != tile)
+    rows, width = o_ref.shape
+    lanes = 128
+    slot_count = kv.shape[0]
+    tail_at = (slot_count // 2) * lanes
+    wide_lane = lax.broadcasted_iota(jnp.int32, (rows, width), 1)
+
+    @pl.when(first)
+    def _():
+        top_lanes = jnp.logical_and(wide_lane >= tail_at + HD, wide_lane < tail_at + HD + slot_count)
+        o_ref[...] = jnp.where(top_lanes, NEG_FILL, 0.0).astype(jnp.float32)
+
+    group = group_at[step]
+    live_count = limit[group]
+
+    @pl.when(jnp.logical_and(valid[step] == 1, live_count > 0))
+    def _():
+        request_count = q_ref.shape[0]
+        pick = (perm_ref[...] == lax.broadcasted_iota(jnp.int32, (rows, request_count), 1)).astype(jnp.bfloat16)
+        q_rows = jnp.dot(pick, q_ref[...], preferred_element_type=jnp.float32)
+        row_live = sg_ref[...] == group
+        spots = lax.broadcasted_iota(jnp.int32, (rows, k_ref.shape[1]), 1)
+        live = jnp.logical_and(spots < live_count, row_live)
+        lane = lax.broadcasted_iota(jnp.int32, (rows, lanes), 1)
+        upper = lane >= HD
+        pieces, tops, totals = [], [], []
+        for slot in range(slot_count):
+            head = kv[slot]
+            start = pl.multiple_of((head // 2) * lanes, lanes)
+            odd = head % 2 == 1
+            half = slot % 2 == 1
+            block = q_rows[:, (slot // 2) * lanes : (slot // 2 + 1) * lanes]
+            block = jnp.where(upper == half, block, 0.0)
+            block = jnp.where(odd == half, block, pltpu.roll(block, HD, 1))
+            scores = lax.dot_general(
+                block.astype(jnp.bfloat16),
+                k_ref[0, :, pl.ds(start, lanes)],
+                (((1,), (1,)), ((), ())),
+                preferred_element_type=jnp.float32,
+            ) * (HD ** (-0.5))
+            top = jnp.max(jnp.where(live, scores, NEG_FILL), axis=1, keepdims=True)
+            weights = jnp.where(live, jnp.exp(scores - top), 0.0)
+            totals.append(jnp.sum(weights, axis=1, keepdims=True))
+            tops.append(top)
+            mixed = jnp.dot(
+                weights.astype(jnp.bfloat16), v_ref[0, :, pl.ds(start, lanes)], preferred_element_type=jnp.float32
+            )
+            pieces.append(jnp.where(odd == half, mixed, pltpu.roll(mixed, HD, 1)))
+        if slot_count % 2:
+            pieces.append(jnp.zeros((rows, lanes), jnp.float32))
+        out = [jnp.where(upper, pieces[i + 1], pieces[i]) for i in range(0, len(pieces), 2)]
+        tail = out[-1]
+        for slot in range(slot_count):
+            tail = jnp.where(lane == HD + slot, tops[slot], tail)
+            tail = jnp.where(lane == HD + 8 + slot, totals[slot], tail)
+        out[-1] = tail
+        o_ref[...] = jnp.where(row_live, jnp.concatenate(out, axis=1), o_ref[...])
+
+
+def prefix_partials(every_query, group_of, prefix_len, seq_index, prefix_keys, prefix_values, kv_ids):
+    request_count, width = every_query.shape
+    group_count, prefix_span, _ = prefix_keys.shape
+    tile_count = request_count // TILE
+    visit_count = tile_count + group_count - 1
+    order_key = group_of * request_count + jnp.arange(request_count, dtype=jnp.int32)
+    rank = jnp.sum((order_key[None, :] < order_key[:, None]).astype(jnp.int32), axis=1)
+    spots = jnp.arange(request_count, dtype=jnp.int32)
+    match = rank[None, :] == spots[:, None]
+    perm = jnp.sum(jnp.where(match, spots[None, :], 0), axis=1)
+    sorted_groups = jnp.sum(jnp.where(match, group_of[None, :], 0), axis=1)
+    low = sorted_groups[0::TILE]
+    high = sorted_groups[TILE - 1 :: TILE]
+    spans = high - low + 1
+    ends = jnp.cumsum(spans)
+    starts = ends - spans
+    visits = jnp.arange(visit_count, dtype=jnp.int32)
+    tile_of = jnp.minimum(jnp.sum((ends[None, :] <= visits[:, None]).astype(jnp.int32), axis=1), tile_count - 1)
+    valid = (visits < ends[-1]).astype(jnp.int32)
+    group_at = jnp.where(valid == 1, jnp.take(low, tile_of) + visits - jnp.take(starts, tile_of), high[-1])
+    limit = jnp.clip(prefix_len - seq_index * prefix_span, 0, prefix_span).astype(jnp.int32)
+    slot_count = kv_ids.shape[0]
+    grid_spec = pltpu.PrefetchScalarGridSpec(
+        num_scalar_prefetch=5,
+        grid=(visit_count,),
+        in_specs=[
+            pl.BlockSpec((TILE, 1), lambda i, t, g, ok, lim, kv: (t[i], 0)),
+            pl.BlockSpec((TILE, 1), lambda i, t, g, ok, lim, kv: (t[i], 0)),
+            pl.BlockSpec((request_count, width), lambda i, t, g, ok, lim, kv: (0, 0)),
+            pl.BlockSpec((1, prefix_span, width), lambda i, t, g, ok, lim, kv: (g[i], 0, 0)),
+            pl.BlockSpec((1, prefix_span, width), lambda i, t, g, ok, lim, kv: (g[i], 0, 0)),
+        ],
+        out_specs=pl.BlockSpec((TILE, width), lambda i, t, g, ok, lim, kv: (t[i], 0)),
+    )
+    lanes = 128
+    flops = visit_count * (2 * TILE * request_count * width + slot_count * 4 * TILE * lanes * prefix_span)
+    out = pl.pallas_call(
+        prefix_kernel,
+        grid_spec=grid_spec,
+        out_shape=jax.ShapeDtypeStruct((request_count, width), jnp.float32),
+        compiler_params=pltpu.CompilerParams(dimension_semantics=("arbitrary",)),
+        cost_estimate=pl.CostEstimate(
+            flops=flops,
+            transcendentals=visit_count * TILE * slot_count * prefix_span,
+            bytes_accessed=visit_count * 2 * prefix_span * width * 2 + request_count * width * 6,
+        ),
+    )(
+        tile_of,
+        group_at,
+        valid,
+        limit,
+        kv_ids,
+        perm.reshape(-1, 1),
+        sorted_groups.reshape(-1, 1),
+        every_query,
+        prefix_keys,
+        prefix_values,
+    )
+    return jnp.take(out, rank, axis=0)
 
 
 def rms_scale(values_in, gain_row):
@@ -97,48 +223,33 @@
     queries = rotate_heads(queries, position).astype(jnp.bfloat16)
     new_keys = rotate_heads(new_keys, position).astype(jnp.bfloat16)
     seq_count = lax.axis_size("seq")
-    own_query = queries.reshape(1, row_count, slot_count * HD)
+    query_width = prefix_keys.shape[2]
+    own_query = jnp.pad(
+        queries.reshape(1, row_count, slot_count * HD),
+        ((0, 0), (0, 0), (0, query_width - slot_count * HD)),
+    )
     every_query = lax.all_to_all(
-        jnp.broadcast_to(own_query, (seq_count, row_count, slot_count * HD)),
+        jnp.broadcast_to(own_query, (seq_count, row_count, query_width)),
         "seq",
         0,
         0,
         tiled=True,
     )
-    every_query = every_query.reshape(-1, slot_count, HD)
-    request_count = every_query.shape[0]
+    every_query = every_query.reshape(-1, query_width)
     score_scale = HD ** (-0.5)
-    pre_keys = jnp.take(prefix_keys.reshape(group_count, prefix_span, KV_HEADS, HD), kv_ids, axis=2)
-    pre_values = jnp.take(
-        prefix_values.reshape(group_count, prefix_span, KV_HEADS, HD), kv_ids, axis=2
-    )
-    pre_scores = (
-        jnp.einsum("rsd,gpsd->rsgp", every_query, pre_keys, preferred_element_type=jnp.float32)
-        * score_scale
-    )
-    pre_spots = seq_index * prefix_span + jnp.arange(prefix_span, dtype=jnp.int32)
-    group_match = group_of[:, None] == group_ids[None, :]
-    length_match = pre_spots[None, :] < prefix_len[:, None]
-    pre_live = group_match[:, None, :, None] & length_match[None, None, :, :]
-    top_score = jnp.max(
-        jnp.where(pre_live, pre_scores, NEG_FILL).reshape(request_count, slot_count, -1), axis=2
-    )
-    pre_weights = jnp.where(pre_live, jnp.exp(pre_scores - top_score[:, :, None, None]), 0.0)
-    totals = jnp.sum(pre_weights, axis=(2, 3))
-    mixed_sum = jnp.einsum(
-        "rsgp,gpsd->rsd",
-        pre_weights.astype(jnp.bfloat16),
-        pre_values,
-        preferred_element_type=jnp.float32,
-    )
-    payload = jnp.concatenate([top_score[..., None], totals[..., None], mixed_sum], axis=-1)
-    payload = payload.reshape(seq_count, row_count, slot_count, HD + 2)
+    payload = prefix_partials(
+        every_query, group_of, prefix_len, seq_index, prefix_keys, prefix_values, kv_ids
+    )
+    payload = payload.reshape(seq_count, row_count, query_width)
     gathered = lax.all_to_all(payload, "seq", 0, 0, tiled=True)
-    gathered_top = gathered[..., 0]
+    tail_at = (slot_count // 2) * 128 + HD
+    gathered_top = gathered[..., tail_at : tail_at + slot_count]
+    gathered_total = gathered[..., tail_at + 8 : tail_at + 8 + slot_count]
+    gathered_mixed = gathered[..., : slot_count * HD].reshape(seq_count, row_count, slot_count, HD)
     part_top = jnp.max(gathered_top, axis=0)
     part_scale = jnp.exp(gathered_top - part_top[None])
-    part_total = jnp.sum(part_scale * gathered[..., 1], axis=0)
-    part_mixed = jnp.sum(part_scale[..., None] * gathered[..., 2:], axis=0)
+    part_total = jnp.sum(part_scale * gathered_total, axis=0)
+    part_mixed = jnp.sum(part_scale[..., None] * gathered_mixed, axis=0)
     suf_keys = jnp.take(suffix_keys.reshape(row_count, suffix_span, KV_HEADS, HD), kv_ids, axis=2)
     suf_values = jnp.take(
         suffix_values.reshape(row_count, suffix_span, KV_HEADS, HD), kv_ids, axis=2

time: 197 us -> 141 us (0.72)
  matrix products: 47.7 us -> 10.2 us
  Pallas kernels: 0 us -> 30.7 us
  local copies, waits for them, and re-layouts: 50.4 us -> 23.7 us
  other arithmetic: 32.9 us -> 15.7 us
  starting transfers between devices: 22.4 us -> 17.6 us
    dot_general x2 -> x0, matrix products: 36.2 us -> none  [the longest x1 19.5 us: on_device(): jnp.einsum('rsd,gpsd->rsgp', every_query, pre_keys, preferred_element_typ...]
    pallas_call x0 -> x1, Pallas kernels: none -> 30.7 us  [prefix_partials(): pl.pallas_call(prefix_kernel, grid_spec=grid_spec, out_shape=jax.ShapeDty...]
    reduce_sum x3 -> x5, other arithmetic: 19.7 us -> 2.01 us  [the longest x1 1.1 us: on_device(): part_mixed = jnp.sum(part_scale[..., None] * gathered_mixed, axis=0)]
    unnamed x22 -> x31, local copies, waits for them, and re-layouts: 17.7 us -> 7.2 us
    reshape x3 -> x2, local copies, waits for them, and re-layouts: 8.21 us -> 1.71 us  [the longest x1 0.87 us: prefix_partials(): perm.reshape(-1, 1)]
    all_to_all x1, waiting for transfers between devices: 0.01 us -> 4.94 us  [on_device(): lax.all_to_all(jnp.broadcast_to(own_query, (seq_count, row_count, query_w...]
    all_to_all x1, starting transfers between devices: 10.3 us -> 5.47 us  [on_device(): gathered = lax.all_to_all(payload, 'seq', 0, 0, tiled=True)]
    all_to_all x1, waiting for transfers between devices: 18.6 us -> 13.8 us  [on_device(): gathered = lax.all_to_all(payload, 'seq', 0, 0, tiled=True)]
  transfers between devices with their start and end apart: 2 -> 2, of which waited for: 1 -> 2; matrix products, arithmetic and copies ran while one was open for 22% -> 13% of each run, Pallas kernels for 0% -> 0%
where the time goes in v3:
time: 141 us
  Pallas kernels  30.7 us (22%)
  blocking collectives  23.8 us (17%)
  local copies, waits for them, and re-layouts  23.7 us (17%)
  waiting for transfers between devices  18.8 us (13%)
  starting transfers between devices  17.6 us (12%)
  other arithmetic  15.7 us (11%)
  matrix products  10.2 us (7%)
    pallas_call x1, Pallas kernels, prefix_partials(): pl.pallas_call(prefix_kernel, grid_spec=grid_spec, out_shape=jax.ShapeDty...  30.7 us
    all_gather x2, blocking collectives, tp_sum(): pieces = lax.all_gather(part.astype(jnp.bfloat16), 'tp', axis=0)  23.8 us
    all_to_all x1, waiting for transfers between devices, on_device(): gathered = lax.all_to_all(payload, 'seq', 0, 0, tiled=True)  13.8 us
    all_to_all x1, starting transfers between devices, on_device(): lax.all_to_all(jnp.broadcast_to(own_query, (seq_count, row_count, query_w...  12.1 us
    unnamed x31, local copies, waits for them, and re-layouts  7.2 us
    all_to_all x1, starting transfers between devices, on_device(): gathered = lax.all_to_all(payload, 'seq', 0, 0, tiled=True)  5.47 us
    all_to_all x1, waiting for transfers between devices, on_device(): lax.all_to_all(jnp.broadcast_to(own_query, (seq_count, row_count, query_w...  4.94 us
    gather x1, local copies, waits for them, and re-layouts, prefix_partials(): return jnp.take(out, rank, axis=0)  2.95 us
  transfers between devices with their start and end apart: 2, of which 2 were waited for; matrix products, arithmetic and copies ran while one was open for 13% of the time, Pallas kernels for 0%

profile of v3, /device:TPU:2, one launch (start us, length us, event | category | flops | bytes accessed | tf_op | source)
XLA Modules:
  0.0 140.7 jit_solution(16635213136019730368)
XLA Ops:
  0.0 1.0 fusion.5
  1.6 1.4 %fusion.36 = f32[8,384]{1,0:T(8,128)S(1)} fusion(bf16[1152,384]{1,0:T(8,128)(2,1)} %param.26, bf16[8,1152]{1,0:T(8,128)(2,1)} %param.23, f32[1152]{0:T(1024)} %param.24, f32[8]{0:T(128)S(1)} %add_rsqrt_fusion.1), kind=kOutput, calls=%fused_computation.111 | convolution fusion | flops 7114752 | bytes 920096 | tf_op jit(solution)/shard_map/dot_general | solution.py:207
  3.0 1.5 %fusion.38 = f32[8,320]{1,0:T(8,128)S(1)} fusion(bf16[1152,320]{0,1:T(8,128)(2,1)} %param.25, bf16[8,1152]{1,0:T(8,128)(2,1)} %param.23, f32[1152]{0:T(1024)} %param.24, f32[8]{0:T(128)S(1)} %add_rsqrt_fusion.1), kind=kOutput, calls=%fused_computation.112 | convolution fusion | flops 5935104 | bytes 770592 | tf_op jit(solution)/shard_map/dot_general | solution.py:204
  5.1 0.8 add_convert_fusion.1
  6.0 0.6 gather_fusion.4
  6.9 0.8 broadcast_in_dim.127
  7.7 12.1 %all-to-all-start = ((bf16[64,8,384]{2,1,0:T(8,128)(2,1)}), bf16[64,8,384]{2,1,0:T(8,128)(2,1)S(1)}, u32[]{:S(2)}, u32[]{:S(2)}) async-start(bf16[64,8,384]{2,1,0:T(8,128)(2,1)} %broadcast_in_dim.127), calls=%async_computation | async-start | bytes 786432 | tf_op jit(solution)/shard_map/all_to_all | solution.py:231
  19.8 0.6 and_select_fusion.kv
  21.2 0.6 slice.37
  22.0 0.6 slice.36
  22.8 0.7 gather_fusion.1
  23.5 0.7 gather_fusion.2
  24.1 0.9 copy.99.perm_ref
  25.0 0.8 copy.100.sg_ref
  25.9 1.1 compare_convert_fusion.1.valid
  27.0 0.5 subtract_clamp_fusion.limit
  27.5 1.8 %compare_select_fusion.4 = (s32[15]{0:T(128)}, s32[15]{0:T(128)}) fusion(s32[15]{0:T(128)S(1)} %gather_fusion.2, s32[15]{0:T(128)S(1)} %gather_fusion.1, s32[]{:T(128)} %bitcast.3, s32[]{:T(128)} %bitcast.2, s32[15]{0:T(128)S(1)} %convert_reduce_fusion.3), kind=kLoop, calls=%fused_computation.94 | loop fusion | flops 225 | bytes 308 | tf_op jit(solution)/shard_map/jit(_where)/select_n | solution.py:98
  29.4 4.9 %all-to-all-done = bf16[64,8,384]{2,1,0:T(8,128)(2,1)S(1)} async-done(((bf16[64,8,384]{2,1,0:T(8,128)(2,1)}), bf16[64,8,384]{2,1,0:T(8,128)(2,1)S(1)}, u32[]{:S(2)}, u32[]{:S(2)}) %all-to-all-start) | async-done | bytes 393248 | tf_op jit(solution)/shard_map/all_to_all | solution.py:231
  34.3 0.7 copy-done.2
  35.0 30.7 %shard_map.163 = f32[512,384]{1,0:T(8,128)} custom-call(s32[15]{0:T(128)} %get-tuple-element.38.tile_of, s32[15]{0:T(128)} %get-tuple-element.37.group_at, s32[15]{0:T(128)} %compare_convert_fusion.1.valid, s32[8]{0:T(128)} %subtract_clamp_fusion.limit, s32[5]{0:T(128)} %and_select_fusion.kv, s32[512,1]{1,0:T(8,128)} %copy.99.perm_ref, ...), custom_call_target="tpu_custom_call" | custom-call | flops 1635778560 | bytes 12976128 | tf_op jit(solution)/shard_map/pallas_call | solution.py:115
  65.7 3.0 %gather_fusion = f32[512,384]{1,0:T(8,128)S(1)} fusion(f32[512,384]{1,0:T(8,128)} %shard_map.163, s32[1024]{0:T(1024)S(1)} %pad_clamp_fusion.1), kind=kCustom, calls=%fused_computation.6 | custom fusion | bytes 1574912 | tf_op jit(solution)/shard_map/jit(_take)/gather | solution.py:137
  68.7 1.0 bitcast_select_fusion
  69.7 5.5 %all-to-all-start.1 = ((f32[64,8,384]{2,1,0:T(8,128)}), f32[64,8,384]{2,1,0:T(8,128)}, u32[]{:S(2)}, u32[]{:S(2)}) async-start(f32[64,8,384]{2,1,0:T(8,128)} %bitcast_select_fusion), calls=%async_computation.1 | async-start | bytes 1572864 | tf_op jit(solution)/shard_map/all_to_all | solution.py:244
  75.6 0.6 gather_fusion.5
  76.3 1.5 %copy.103 = bf16[8,128,384]{1,2,0:T(8,128)(2,1)S(1)} copy(bf16[8,128,384]{2,1,0:T(8,128)(2,1)} %param.31) | data formatting | bytes 1572864 | tf_op args[8]
  77.8 0.7 gather_fusion.3
  78.5 2.3 %copy.116 = bf16[8,128,384]{1,2,0:T(8,128)(2,1)} copy(bf16[8,128,384]{2,1,0:T(8,128)(2,1)} %param.32) | data formatting | bytes 1572864 | tf_op args[9]
  80.8 1.8 %gather_fusion.6 = bf16[5,8,128,64]{2,3,1,0:T(8,128)(2,1)S(1)} fusion(bf16[8,128,6,64]{1,3,2,0:T(8,128)(2,1)} %bitcast.64, s32[1024]{0:T(1024)S(1)} %pad_clamp_fusion), kind=kCustom, calls=%fused_computation.4.clone | custom fusion | bytes 1310740 | tf_op jit(solution)/shard_map/jit(_take)/gather | solution.py:254
  82.6 1.0 select_bitcast_fusion.1
  84.1 13.8 %all-to-all-done.1 = f32[64,8,384]{2,1,0:T(8,128)} async-done(((f32[64,8,384]{2,1,0:T(8,128)}), f32[64,8,384]{2,1,0:T(8,128)}, u32[]{:S(2)}, u32[]{:S(2)}) %all-to-all-start.1) | async-done | bytes 786464 | tf_op jit(solution)/shard_map/all_to_all | solution.py:244
  98.0 1.2 fusion.41
  100.0 0.7 fusion.24
  100.8 0.7 copy.120
  101.5 0.7 copy.108
  102.1 1.5 %copy.135 = f32[64,8,320]{0,2,1:T(8,128)S(1)} copy(f32[64,8,320]{2,1,0:T(8,128)} %bitcast.63) | data formatting | bytes 1310720
  103.8 1.1 multiply_reduce_fusion
  104.9 1.5 %reduce_sum.133 = f32[8,5,64]{2,1,0:T(8,128)} reshape(f32[8,320]{1,0:T(8,128)} %multiply_reduce_fusion) | data formatting | bytes 20480 | tf_op jit(solution)/shard_map/reduce_sum | solution.py:252
  106.4 1.5 %fusion.1 = f32[8,5,1,64]{3,2,1,0:T(1,128)S(1)} fusion(bf16[8,128,5,64]{1,3,0,2:T(8,128)(2,1)} %get-tuple-element.40, bf16[8,5,128,1]{2,0,1,3:T(8,128)(2,1)} %get-tuple-element.34), kind=kOutput, calls=%fused_computation.18 | convolution fusion | flops 655360 | bytes 675840 | tf_op jit(solution)/shard_map/rsj,rjsd->rsd/dot_general | solution.py:273
  107.9 0.9 fusion.20
  108.8 0.7 reshape.240
  109.5 1.3 convolution_convert_fusion.1
  110.9 11.9 %all-gather = bf16[32,1152]{1,0:T(8,128)(2,1)S(1)} all-gather(bf16[8,1152]{1,0:T(8,128)(2,1)S(1)} %convolution_convert_fusion.1), channel_id=2, replica_groups=mesh['seq'=64,'tp'=4] {'tp'}, dimensions={0}, use_global_device_ids=true | all-gather | bytes 92160 | tf_op jit(solution)/shard_map/all_gather | solution.py:173
  122.8 0.8 fusion.9
  123.7 0.6 copy-done.5
  124.3 1.7 %fusion.31 = f32[8,768]{1,0:T(8,128)} fusion(bf16[1152,768]{1,0:T(8,128)(2,1)S(1)} %copy-done.1, bf16[8,1152]{1,0:T(8,128)(2,1)S(1)} %get-tuple-element.11, f32[1152]{0:T(1024)} %param.36, f32[8]{0:T(128)S(1)} %add_rsqrt_fusion), kind=kOutput, calls=%fused_computation.97 | convolution fusion | flops 14192640 | bytes 1817120 | tf_op jit(solution)/shard_map/dot_general | solution.py:286
  125.9 2.2 %convolution_convert_fusion = bf16[8,1152]{1,0:T(8,128)(2,1)S(1)} fusion(bf16[768,1152]{1,0:T(8,128)(2,1)S(1)} %copy-done, bf16[1152,768]{1,0:T(8,128)(2,1)} %param.38, f32[8,768]{1,0:T(8,128)} %fusion.31, bf16[8,1152]{1,0:T(8,128)(2,1)} %copy-done.5, f32[1152]{0:T(1024)S(1)} %copy-done.8, f32[8]{0:T(128)S(1)} %add_rsqrt_fusion), kind=kOutput, calls=%fused_computation.7 | convolution fusion | flops 28394496 | bytes 3605024 | tf_op jit(solution)/shard_map/dot_general | solution.py:289
  128.2 11.9 %all-gather.1 = bf16[32,1152]{1,0:T(8,128)(2,1)S(1)} all-gather(bf16[8,1152]{1,0:T(8,128)(2,1)S(1)} %convolution_convert_fusion), channel_id=3, replica_groups=mesh['seq'=64,'tp'=4] {'tp'}, dimensions={0}, use_global_device_ids=true | all-gather | bytes 92160 | tf_op jit(solution)/shard_map/all_gather | solution.py:173
  140.1 0.6 fusion.12
  (80 shorter events, 4.9 us)
Async XLA Ops:
  0.0 125.9 %copy-start = (bf16[768,1152]{1,0:T(8,128)(2,1)S(1)}, bf16[768,1152]{1,0:T(8,128)(2,1)}, u32[]{:S(2)}) copy-start(bf16[768,1152]{1,0:T(8,128)(2,1)} %param.39) | copy-start | bytes 5308420
  0.0 4.8 %copy-start.9 = (s32[512]{0:T(512)S(1)}, s32[512]{0:T(512)}, u32[]{:S(2)}) copy-start(s32[512]{0:T(512)} %param.33) | copy-start | bytes 6148
  0.0 4.9 %copy-start.11 = (s32[8]{0:T(128)S(1)}, s32[8]{0:T(128)}, u32[]{:S(2)}) copy-start(s32[8]{0:T(128)} %param.34) | copy-start | bytes 100
  1.6 81.1 %copy-start.10 = (pred[5]{0:T(512)(128)(4,1)}, pred[5]{0:T(512)(128)(4,1)S(1)}, u32[]{:S(2)}) copy-start(pred[5]{0:T(512)(128)(4,1)S(1)} %get-tuple-element.41) | copy-start | bytes 19
  7.7 26.6 %all-to-all-start = ((bf16[64,8,384]{2,1,0:T(8,128)(2,1)}), bf16[64,8,384]{2,1,0:T(8,128)(2,1)S(1)}, u32[]{:S(2)}, u32[]{:S(2)}) async-start(bf16[64,8,384]{2,1,0:T(8,128)(2,1)} %broadcast_in_dim.127), calls=%async_computation | async-start | bytes 786432 | tf_op jit(solution)/shard_map/all_to_all | solution.py:231
  34.3 0.7 copy-start.2
  68.7 6.6 %copy-start.3 = (bf16[1152,384]{1,0:T(8,128)(2,1)S(1)}, bf16[1152,384]{1,0:T(8,128)(2,1)}, u32[]{:S(2)}) copy-start(bf16[1152,384]{1,0:T(8,128)(2,1)} %param.27) | copy-start | bytes 2654212
  68.7 6.6 %copy-start.4 = (bf16[8,1152]{1,0:T(8,128)(2,1)S(1)}, bf16[8,1152]{1,0:T(8,128)(2,1)}, u32[]{:S(2)}) copy-start(bf16[8,1152]{1,0:T(8,128)(2,1)} %param.23) | copy-start | bytes 55300
  68.7 6.6 %copy-start.7 = (f32[1152]{0:T(1024)S(1)}, f32[1152]{0:T(1024)}, u32[]{:S(2)}) copy-start(f32[1152]{0:T(1024)} %param.24) | copy-start | bytes 13828
  69.7 28.2 %all-to-all-start.1 = ((f32[64,8,384]{2,1,0:T(8,128)}), f32[64,8,384]{2,1,0:T(8,128)}, u32[]{:S(2)}, u32[]{:S(2)}) async-start(f32[64,8,384]{2,1,0:T(8,128)} %bitcast_select_fusion), calls=%async_computation.1 | async-start | bytes 1572864 | tf_op jit(solution)/shard_map/all_to_all | solution.py:244
  104.9 19.4 %copy-start.1 = (bf16[1152,768]{1,0:T(8,128)(2,1)S(1)}, bf16[1152,768]{1,0:T(8,128)(2,1)}, u32[]{:S(2)}) copy-start(bf16[1152,768]{1,0:T(8,128)(2,1)} %param.37) | copy-start | bytes 5308420
  109.5 16.4 %copy-start.8 = (f32[1152]{0:T(1024)S(1)}, f32[1152]{0:T(1024)}, u32[]{:S(2)}) copy-start(f32[1152]{0:T(1024)} %param.36) | copy-start | bytes 13828
  123.7 0.6 copy-start.5
  125.9 14.2 %copy-start.6 = (bf16[8,1152]{1,0:T(8,128)(2,1)S(1)}, bf16[8,1152]{1,0:T(8,128)(2,1)}, u32[]{:S(2)}) copy-start(bf16[8,1152]{1,0:T(8,128)(2,1)} %copy-done.5) | copy-start | bytes 55300

commit v4 on v3

--- a/solution.py
+++ b/solution.py
@@ -38,40 +38,50 @@
         pick = (perm_ref[...] == lax.broadcasted_iota(jnp.int32, (rows, request_count), 1)).astype(jnp.bfloat16)
         q_rows = jnp.dot(pick, q_ref[...], preferred_element_type=jnp.float32)
         row_live = sg_ref[...] == group
-        spots = lax.broadcasted_iota(jnp.int32, (rows, k_ref.shape[1]), 1)
-        live = jnp.logical_and(spots < live_count, row_live)
         lane = lax.broadcasted_iota(jnp.int32, (rows, lanes), 1)
         upper = lane >= HD
-        pieces, tops, totals = [], [], []
+        tile_total = width // lanes
+        padded = []
         for slot in range(slot_count):
             head = kv[slot]
-            start = pl.multiple_of((head // 2) * lanes, lanes)
             odd = head % 2 == 1
             half = slot % 2 == 1
             block = q_rows[:, (slot // 2) * lanes : (slot // 2 + 1) * lanes]
             block = jnp.where(upper == half, block, 0.0)
             block = jnp.where(odd == half, block, pltpu.roll(block, HD, 1))
-            scores = lax.dot_general(
-                block.astype(jnp.bfloat16),
-                k_ref[0, :, pl.ds(start, lanes)],
-                (((1,), (1,)), ((), ())),
-                preferred_element_type=jnp.float32,
-            ) * (HD ** (-0.5))
-            top = jnp.max(jnp.where(live, scores, NEG_FILL), axis=1, keepdims=True)
-            weights = jnp.where(live, jnp.exp(scores - top), 0.0)
-            totals.append(jnp.sum(weights, axis=1, keepdims=True))
-            tops.append(top)
-            mixed = jnp.dot(
-                weights.astype(jnp.bfloat16), v_ref[0, :, pl.ds(start, lanes)], preferred_element_type=jnp.float32
+            padded.append(
+                jnp.concatenate(
+                    [jnp.where(head // 2 == j, block, 0.0) for j in range(tile_total)], axis=1
+                ).astype(jnp.bfloat16)
             )
-            pieces.append(jnp.where(odd == half, mixed, pltpu.roll(mixed, HD, 1)))
+        padded = jnp.concatenate(padded, axis=0)
+        scores = lax.dot_general(
+            padded, k_ref[0], (((1,), (1,)), ((), ())), preferred_element_type=jnp.float32
+        ) * (HD ** (-0.5))
+        all_live = jnp.concatenate([row_live] * slot_count, axis=0)
+        spots = lax.broadcasted_iota(jnp.int32, scores.shape, 1)
+        live = jnp.logical_and(spots < live_count, all_live)
+        top = jnp.max(jnp.where(live, scores, NEG_FILL), axis=1, keepdims=True)
+        weights = jnp.where(live, jnp.exp(scores - top), 0.0)
+        total = jnp.sum(weights, axis=1, keepdims=True)
+        mixed = jnp.dot(weights.astype(jnp.bfloat16), v_ref[0], preferred_element_type=jnp.float32)
+        pieces = []
+        for slot in range(slot_count):
+            head = kv[slot]
+            odd = head % 2 == 1
+            half = slot % 2 == 1
+            mine = mixed[slot * rows : (slot + 1) * rows]
+            chosen = mine[:, 0:lanes]
+            for j in range(1, tile_total):
+                chosen = jnp.where(head // 2 == j, mine[:, j * lanes : (j + 1) * lanes], chosen)
+            pieces.append(jnp.where(odd == half, chosen, pltpu.roll(chosen, HD, 1)))
         if slot_count % 2:
             pieces.append(jnp.zeros((rows, lanes), jnp.float32))
         out = [jnp.where(upper, pieces[i + 1], pieces[i]) for i in range(0, len(pieces), 2)]
         tail = out[-1]
         for slot in range(slot_count):
-            tail = jnp.where(lane == HD + slot, tops[slot], tail)
-            tail = jnp.where(lane == HD + 8 + slot, totals[slot], tail)
+            tail = jnp.where(lane == HD + slot, top[slot * rows : (slot + 1) * rows], tail)
+            tail = jnp.where(lane == HD + 8 + slot, total[slot * rows : (slot + 1) * rows], tail)
         out[-1] = tail
         o_ref[...] = jnp.where(row_live, jnp.concatenate(out, axis=1), o_ref[...])
 
@@ -111,7 +121,7 @@
         out_specs=pl.BlockSpec((TILE, width), lambda i, t, g, ok, lim, kv: (t[i], 0)),
     )
     lanes = 128
-    flops = visit_count * (2 * TILE * request_count * width + slot_count * 4 * TILE * lanes * prefix_span)
+    flops = visit_count * (2 * TILE * request_count * width + slot_count * 4 * TILE * width * prefix_span)
     out = pl.pallas_call(
         prefix_kernel,
         grid_spec=grid_spec,

time: 141 us -> 131 us (0.929)
  Pallas kernels: 30.7 us -> 20 us
    pallas_call x1, Pallas kernels: 30.7 us -> 20 us  [prefix_partials(): pl.pallas_call(prefix_kernel, grid_spec=grid_spec, out_shape=jax.ShapeDty...]
  transfers between devices with their start and end apart: 2 -> 2, of which waited for: 2 -> 2; matrix products, arithmetic and copies ran while one was open for 13% -> 14% of each run, Pallas kernels for 0% -> 0%
where the time goes in v4:
time: 131 us; the launch traced here: 130 us
  blocking collectives  23.9 us (18%)
  local copies, waits for them, and re-layouts  23.7 us (18%)
  Pallas kernels  20 us (15%)
  waiting for transfers between devices  18.8 us (14%)
  starting transfers between devices  17.6 us (13%)
  other arithmetic  15.7 us (12%)
  matrix products  10.2 us (8%)
    all_gather x2, blocking collectives, tp_sum(): pieces = lax.all_gather(part.astype(jnp.bfloat16), 'tp', axis=0)  23.9 us
    pallas_call x1, Pallas kernels, prefix_partials(): pl.pallas_call(prefix_kernel, grid_spec=grid_spec, out_shape=jax.ShapeDty...  20 us
    all_to_all x1, waiting for transfers between devices, on_device(): gathered = lax.all_to_all(payload, 'seq', 0, 0, tiled=True)  13.8 us
    all_to_all x1, starting transfers between devices, on_device(): lax.all_to_all(jnp.broadcast_to(own_query, (seq_count, row_count, query_w...  12.1 us
    unnamed x31, local copies, waits for them, and re-layouts  7.2 us
    all_to_all x1, starting transfers between devices, on_device(): gathered = lax.all_to_all(payload, 'seq', 0, 0, tiled=True)  5.47 us
    all_to_all x1, waiting for transfers between devices, on_device(): lax.all_to_all(jnp.broadcast_to(own_query, (seq_count, row_count, query_w...  4.94 us
    gather x1, local copies, waits for them, and re-layouts, prefix_partials(): return jnp.take(out, rank, axis=0)  2.95 us
  transfers between devices with their start and end apart: 2, of which 2 were waited for; matrix products, arithmetic and copies ran while one was open for 14% of the time, Pallas kernels for 0%

profile of v4, /device:TPU:2, one launch (start us, length us, event | category | flops | bytes accessed | tf_op | source)
XLA Modules:
  0.0 130.2 jit_solution(16380244075578448100)
XLA Ops:
  0.0 1.0 fusion.5
  1.6 1.4 %fusion.36 = f32[8,384]{1,0:T(8,128)S(1)} fusion(bf16[1152,384]{1,0:T(8,128)(2,1)} %param.26, bf16[8,1152]{1,0:T(8,128)(2,1)} %param.23, f32[1152]{0:T(1024)} %param.24, f32[8]{0:T(128)S(1)} %add_rsqrt_fusion.1), kind=kOutput, calls=%fused_computation.111 | convolution fusion | flops 7114752 | bytes 920096 | tf_op jit(solution)/shard_map/dot_general | solution.py:217
  3.0 1.5 %fusion.38 = f32[8,320]{1,0:T(8,128)S(1)} fusion(bf16[1152,320]{0,1:T(8,128)(2,1)} %param.25, bf16[8,1152]{1,0:T(8,128)(2,1)} %param.23, f32[1152]{0:T(1024)} %param.24, f32[8]{0:T(128)S(1)} %add_rsqrt_fusion.1), kind=kOutput, calls=%fused_computation.112 | convolution fusion | flops 5935104 | bytes 770592 | tf_op jit(solution)/shard_map/dot_general | solution.py:214
  5.1 0.8 add_convert_fusion.1
  6.0 0.6 gather_fusion.4
  6.9 0.8 broadcast_in_dim.127
  7.7 12.1 %all-to-all-start = ((bf16[64,8,384]{2,1,0:T(8,128)(2,1)}), bf16[64,8,384]{2,1,0:T(8,128)(2,1)S(1)}, u32[]{:S(2)}, u32[]{:S(2)}) async-start(bf16[64,8,384]{2,1,0:T(8,128)(2,1)} %broadcast_in_dim.127), calls=%async_computation | async-start | bytes 786432 | tf_op jit(solution)/shard_map/all_to_all | solution.py:241
  19.8 0.6 and_select_fusion.kv
  21.2 0.6 slice.37
  22.0 0.6 slice.36
  22.8 0.7 gather_fusion.1
  23.5 0.7 gather_fusion.2
  24.1 0.9 copy.99.perm_ref
  25.0 0.8 copy.100.sg_ref
  25.9 1.1 compare_convert_fusion.1.valid
  27.0 0.5 subtract_clamp_fusion.limit
  27.5 1.8 %compare_select_fusion.4 = (s32[15]{0:T(128)}, s32[15]{0:T(128)}) fusion(s32[15]{0:T(128)S(1)} %gather_fusion.2, s32[15]{0:T(128)S(1)} %gather_fusion.1, s32[]{:T(128)} %bitcast.3, s32[]{:T(128)} %bitcast.2, s32[15]{0:T(128)S(1)} %convert_reduce_fusion.3), kind=kLoop, calls=%fused_computation.94 | loop fusion | flops 225 | bytes 308 | tf_op jit(solution)/shard_map/jit(_where)/select_n | solution.py:108
  29.4 4.9 %all-to-all-done = bf16[64,8,384]{2,1,0:T(8,128)(2,1)S(1)} async-done(((bf16[64,8,384]{2,1,0:T(8,128)(2,1)}), bf16[64,8,384]{2,1,0:T(8,128)(2,1)S(1)}, u32[]{:S(2)}, u32[]{:S(2)}) %all-to-all-start) | async-done | bytes 393248 | tf_op jit(solution)/shard_map/all_to_all | solution.py:241
  34.3 0.7 copy-done.4
  35.0 20.0 %shard_map.163 = f32[512,384]{1,0:T(8,128)} custom-call(s32[15]{0:T(128)} %get-tuple-element.38.tile_of, s32[15]{0:T(128)} %get-tuple-element.37.group_at, s32[15]{0:T(128)} %compare_convert_fusion.1.valid, s32[8]{0:T(128)} %subtract_clamp_fusion.limit, s32[5]{0:T(128)} %and_select_fusion.kv, s32[512,1]{1,0:T(8,128)} %copy.99.perm_ref, ...), custom_call_target="tpu_custom_call" | custom-call | flops 4152360960 | bytes 12976128 | tf_op jit(solution)/shard_map/pallas_call | solution.py:125
  55.1 3.0 %gather_fusion = f32[512,384]{1,0:T(8,128)S(1)} fusion(f32[512,384]{1,0:T(8,128)} %shard_map.163, s32[1024]{0:T(1024)S(1)} %pad_clamp_fusion.1), kind=kCustom, calls=%fused_computation.6 | custom fusion | bytes 1574912 | tf_op jit(solution)/shard_map/jit(_take)/gather | solution.py:147
  58.1 1.0 bitcast_select_fusion
  59.1 5.5 %all-to-all-start.1 = ((f32[64,8,384]{2,1,0:T(8,128)}), f32[64,8,384]{2,1,0:T(8,128)}, u32[]{:S(2)}, u32[]{:S(2)}) async-start(f32[64,8,384]{2,1,0:T(8,128)} %bitcast_select_fusion), calls=%async_computation.1 | async-start | bytes 1572864 | tf_op jit(solution)/shard_map/all_to_all | solution.py:254
  65.0 0.6 gather_fusion.5
  65.6 1.5 %copy.103 = bf16[8,128,384]{1,2,0:T(8,128)(2,1)S(1)} copy(bf16[8,128,384]{2,1,0:T(8,128)(2,1)} %param.31) | data formatting | bytes 1572864 | tf_op args[8]
  67.1 0.7 gather_fusion.3
  67.8 2.3 %copy.116 = bf16[8,128,384]{1,2,0:T(8,128)(2,1)} copy(bf16[8,128,384]{2,1,0:T(8,128)(2,1)} %param.32) | data formatting | bytes 1572864 | tf_op args[9]
  70.1 1.8 %gather_fusion.6 = bf16[5,8,128,64]{2,3,1,0:T(8,128)(2,1)S(1)} fusion(bf16[8,128,6,64]{1,3,2,0:T(8,128)(2,1)} %bitcast.64, s32[1024]{0:T(1024)S(1)} %pad_clamp_fusion), kind=kCustom, calls=%fused_computation.4.clone | custom fusion | bytes 1310740 | tf_op jit(solution)/shard_map/jit(_take)/gather | solution.py:264
  72.0 1.0 select_bitcast_fusion.1
  73.5 13.8 %all-to-all-done.1 = f32[64,8,384]{2,1,0:T(8,128)} async-done(((f32[64,8,384]{2,1,0:T(8,128)}), f32[64,8,384]{2,1,0:T(8,128)}, u32[]{:S(2)}, u32[]{:S(2)}) %all-to-all-start.1) | async-done | bytes 786464 | tf_op jit(solution)/shard_map/all_to_all | solution.py:254
  87.3 1.2 fusion.41
  89.4 0.7 fusion.24
  90.2 0.7 copy.120
  90.9 0.7 copy.108
  91.5 1.5 %copy.135 = f32[64,8,320]{0,2,1:T(8,128)S(1)} copy(f32[64,8,320]{2,1,0:T(8,128)} %bitcast.63) | data formatting | bytes 1310720
  93.2 1.1 multiply_reduce_fusion
  94.3 1.5 %reduce_sum.133 = f32[8,5,64]{2,1,0:T(8,128)} reshape(f32[8,320]{1,0:T(8,128)} %multiply_reduce_fusion) | data formatting | bytes 20480 | tf_op jit(solution)/shard_map/reduce_sum | solution.py:262
  95.8 1.5 %fusion.1 = f32[8,5,1,64]{3,2,1,0:T(1,128)S(1)} fusion(bf16[8,128,5,64]{1,3,0,2:T(8,128)(2,1)} %get-tuple-element.40, bf16[8,5,128,1]{2,0,1,3:T(8,128)(2,1)} %get-tuple-element.34), kind=kOutput, calls=%fused_computation.18 | convolution fusion | flops 655360 | bytes 675840 | tf_op jit(solution)/shard_map/rsj,rjsd->rsd/dot_general | solution.py:283
  97.3 0.9 fusion.20
  98.2 0.7 reshape.240
  98.9 1.3 %convolution_convert_fusion.1 = bf16[8,1152]{1,0:T(8,128)(2,1)S(1)} fusion(bf16[8,320]{1,0:T(8,128)(2,1)} %reshape.240, bf16[320,1152]{1,0:T(8,128)(2,1)} %param.28), kind=kOutput, calls=%fused_computation.8 | convolution fusion | flops 5907456 | bytes 760832 | tf_op jit(solution)/shard_map/dot_general | solution.py:290
  100.2 12.0 %all-gather = bf16[32,1152]{1,0:T(8,128)(2,1)S(1)} all-gather(bf16[8,1152]{1,0:T(8,128)(2,1)S(1)} %convolution_convert_fusion.1), channel_id=2, replica_groups=mesh['seq'=64,'tp'=4] {'tp'}, dimensions={0}, use_global_device_ids=true | all-gather | bytes 92160 | tf_op jit(solution)/shard_map/all_gather | solution.py:183
  112.2 0.8 fusion.9
  113.1 0.6 copy-done.5
  113.7 1.7 %fusion.31 = f32[8,768]{1,0:T(8,128)} fusion(bf16[1152,768]{1,0:T(8,128)(2,1)S(1)} %copy-done.1, bf16[8,1152]{1,0:T(8,128)(2,1)S(1)} %get-tuple-element.11, f32[1152]{0:T(1024)} %param.36, f32[8]{0:T(128)S(1)} %add_rsqrt_fusion), kind=kOutput, calls=%fused_computation.97 | convolution fusion | flops 14192640 | bytes 1817120 | tf_op jit(solution)/shard_map/dot_general | solution.py:296
  115.4 2.2 %convolution_convert_fusion = bf16[8,1152]{1,0:T(8,128)(2,1)S(1)} fusion(bf16[768,1152]{1,0:T(8,128)(2,1)S(1)} %copy-done, bf16[1152,768]{1,0:T(8,128)(2,1)} %param.38, f32[8,768]{1,0:T(8,128)} %fusion.31, bf16[8,1152]{1,0:T(8,128)(2,1)} %copy-done.5, f32[1152]{0:T(1024)S(1)} %copy-done.8, f32[8]{0:T(128)S(1)} %add_rsqrt_fusion), kind=kOutput, calls=%fused_computation.7 | convolution fusion | flops 28394496 | bytes 3605024 | tf_op jit(solution)/shard_map/dot_general | solution.py:299
  117.6 11.9 %all-gather.1 = bf16[32,1152]{1,0:T(8,128)(2,1)S(1)} all-gather(bf16[8,1152]{1,0:T(8,128)(2,1)S(1)} %convolution_convert_fusion), channel_id=3, replica_groups=mesh['seq'=64,'tp'=4] {'tp'}, dimensions={0}, use_global_device_ids=true | all-gather | bytes 92160 | tf_op jit(solution)/shard_map/all_gather | solution.py:183
  129.5 0.6 fusion.12
  (80 shorter events, 4.9 us)
Async XLA Ops:
  0.0 115.4 %copy-start = (bf16[768,1152]{1,0:T(8,128)(2,1)S(1)}, bf16[768,1152]{1,0:T(8,128)(2,1)}, u32[]{:S(2)}) copy-start(bf16[768,1152]{1,0:T(8,128)(2,1)} %param.39) | copy-start | bytes 5308420
  0.0 4.8 %copy-start.9 = (s32[512]{0:T(512)S(1)}, s32[512]{0:T(512)}, u32[]{:S(2)}) copy-start(s32[512]{0:T(512)} %param.33) | copy-start | bytes 6148
  0.0 4.9 %copy-start.11 = (s32[8]{0:T(128)S(1)}, s32[8]{0:T(128)}, u32[]{:S(2)}) copy-start(s32[8]{0:T(128)} %param.34) | copy-start | bytes 100
  1.6 70.5 %copy-start.10 = (pred[5]{0:T(512)(128)(4,1)}, pred[5]{0:T(512)(128)(4,1)S(1)}, u32[]{:S(2)}) copy-start(pred[5]{0:T(512)(128)(4,1)S(1)} %get-tuple-element.41) | copy-start | bytes 19
  7.7 26.6 %all-to-all-start = ((bf16[64,8,384]{2,1,0:T(8,128)(2,1)}), bf16[64,8,384]{2,1,0:T(8,128)(2,1)S(1)}, u32[]{:S(2)}, u32[]{:S(2)}) async-start(bf16[64,8,384]{2,1,0:T(8,128)(2,1)} %broadcast_in_dim.127), calls=%async_computation | async-start | bytes 786432 | tf_op jit(solution)/shard_map/all_to_all | solution.py:241
  34.3 0.7 copy-start.4
  58.0 6.6 %copy-start.2 = (bf16[1152,384]{1,0:T(8,128)(2,1)S(1)}, bf16[1152,384]{1,0:T(8,128)(2,1)}, u32[]{:S(2)}) copy-start(bf16[1152,384]{1,0:T(8,128)(2,1)} %param.27) | copy-start | bytes 2654212
  58.0 6.6 %copy-start.3 = (bf16[8,1152]{1,0:T(8,128)(2,1)S(1)}, bf16[8,1152]{1,0:T(8,128)(2,1)}, u32[]{:S(2)}) copy-start(bf16[8,1152]{1,0:T(8,128)(2,1)} %param.23) | copy-start | bytes 55300
  58.1 6.6 %copy-start.7 = (f32[1152]{0:T(1024)S(1)}, f32[1152]{0:T(1024)}, u32[]{:S(2)}) copy-start(f32[1152]{0:T(1024)} %param.24) | copy-start | bytes 13828
  59.1 28.2 %all-to-all-start.1 = ((f32[64,8,384]{2,1,0:T(8,128)}), f32[64,8,384]{2,1,0:T(8,128)}, u32[]{:S(2)}, u32[]{:S(2)}) async-start(f32[64,8,384]{2,1,0:T(8,128)} %bitcast_select_fusion), calls=%async_computation.1 | async-start | bytes 1572864 | tf_op jit(solution)/shard_map/all_to_all | solution.py:254
  94.3 19.4 %copy-start.1 = (bf16[1152,768]{1,0:T(8,128)(2,1)S(1)}, bf16[1152,768]{1,0:T(8,128)(2,1)}, u32[]{:S(2)}) copy-start(bf16[1152,768]{1,0:T(8,128)(2,1)} %param.37) | copy-start | bytes 5308420
  98.9 16.5 %copy-start.8 = (f32[1152]{0:T(1024)S(1)}, f32[1152]{0:T(1024)}, u32[]{:S(2)}) copy-start(f32[1152]{0:T(1024)} %param.36) | copy-start | bytes 13828
  113.1 0.6 copy-start.5
  115.4 14.2 %copy-start.6 = (bf16[8,1152]{1,0:T(8,128)(2,1)S(1)}, bf16[8,1152]{1,0:T(8,128)(2,1)}, u32[]{:S(2)}) copy-start(bf16[8,1152]{1,0:T(8,128)(2,1)} %copy-done.5) | copy-start | bytes 55300

commit v5 on v4

--- a/solution.py
+++ b/solution.py
@@ -12,6 +12,16 @@
 
 NEG_FILL = -1e30
 TILE = 64
+
+
+def split_parts(values, count):
+    parts = []
+    for _ in range(count - 1):
+        high = values.astype(jnp.bfloat16).astype(jnp.float32)
+        parts.append(high)
+        values = values - high
+    parts.append(values.astype(jnp.bfloat16).astype(jnp.float32))
+    return parts
 
 
 def prefix_kernel(tile_of, group_at, valid, limit, kv, perm_ref, sg_ref, q_ref, k_ref, v_ref, o_ref):
@@ -79,9 +89,10 @@
             pieces.append(jnp.zeros((rows, lanes), jnp.float32))
         out = [jnp.where(upper, pieces[i + 1], pieces[i]) for i in range(0, len(pieces), 2)]
         tail = out[-1]
-        for slot in range(slot_count):
-            tail = jnp.where(lane == HD + slot, top[slot * rows : (slot + 1) * rows], tail)
-            tail = jnp.where(lane == HD + 8 + slot, total[slot * rows : (slot + 1) * rows], tail)
+        parts = split_parts(top, 3) + split_parts(total, 3)
+        for index, part in enumerate(parts):
+            for slot in range(slot_count):
+                tail = jnp.where(lane == HD + index * slot_count + slot, part[slot * rows : (slot + 1) * rows], tail)
         out[-1] = tail
         o_ref[...] = jnp.where(row_live, jnp.concatenate(out, axis=1), o_ref[...])
 
@@ -144,7 +155,7 @@
         prefix_keys,
         prefix_values,
     )
-    return jnp.take(out, rank, axis=0)
+    return jnp.take(out, rank, axis=0).astype(jnp.bfloat16)
 
 
 def rms_scale(values_in, gain_row):
@@ -180,8 +191,13 @@
 
 
 def tp_sum(part):
-    pieces = lax.all_gather(part.astype(jnp.bfloat16), "tp", axis=0)
-    return jnp.sum(pieces.astype(jnp.float32), axis=0)
+    sent = part.astype(jnp.bfloat16)
+    count = lax.axis_size("tp")
+    total = sent.astype(jnp.float32)
+    for shift in range(1, count):
+        moved = lax.ppermute(sent, "tp", [(j, (j + shift) % count) for j in range(count)])
+        total = total + moved.astype(jnp.float32)
+    return total
 
 
 def on_device(
@@ -251,10 +267,11 @@
         every_query, group_of, prefix_len, seq_index, prefix_keys, prefix_values, kv_ids
     )
     payload = payload.reshape(seq_count, row_count, query_width)
-    gathered = lax.all_to_all(payload, "seq", 0, 0, tiled=True)
+    gathered = lax.all_to_all(payload, "seq", 0, 0, tiled=True).astype(jnp.float32)
     tail_at = (slot_count // 2) * 128 + HD
-    gathered_top = gathered[..., tail_at : tail_at + slot_count]
-    gathered_total = gathered[..., tail_at + 8 : tail_at + 8 + slot_count]
+    tail_parts = [gathered[..., tail_at + i * slot_count : tail_at + (i + 1) * slot_count] for i in range(6)]
+    gathered_top = (tail_parts[0] + tail_parts[1]) + tail_parts[2]
+    gathered_total = (tail_parts[3] + tail_parts[4]) + tail_parts[5]
     gathered_mixed = gathered[..., : slot_count * HD].reshape(seq_count, row_count, slot_count, HD)
     part_top = jnp.max(gathered_top, axis=0)
     part_scale = jnp.exp(gathered_top - part_top[None])

time: 131 us -> 123 us (0.939)
  blocking collectives: 23.9 us -> 0 us
  starting transfers between devices: 17.6 us -> 26.4 us
  other arithmetic: 15.7 us -> 19 us
  local copies, waits for them, and re-layouts: 23.7 us -> 25.6 us
  waiting for transfers between devices: 18.8 us -> 17.4 us
    all_gather x2 -> x0, blocking collectives: 23.9 us -> none  [tp_sum(): pieces = lax.all_gather(part.astype(jnp.bfloat16), 'tp', axis=0)]
    ppermute x0 -> x6, starting transfers between devices: none -> 8.97 us  [tp_sum(): lax.ppermute(sent, 'tp', [(j, (j + shift) % count) for j in range(count)])]
    ppermute x0 -> x6, waiting for transfers between devices: none -> 5.44 us  [tp_sum(): lax.ppermute(sent, 'tp', [(j, (j + shift) % count) for j in range(count)])]
    all_to_all x1, waiting for transfers between devices: 4.94 us -> 0.01 us  [on_device(): lax.all_to_all(jnp.broadcast_to(own_query, (seq_count, row_count, query_w...]
    unnamed x31 -> x28, local copies, waits for them, and re-layouts: 7.2 us -> 4.44 us
    convert_element_type x0 -> x2, other arithmetic: none -> 2.13 us  [the longest x1 1.24 us: on_device(): lax.all_to_all(payload, 'seq', 0, 0, tiled=True).astype(jnp.float32)]
    all_to_all x1, waiting for transfers between devices: 13.8 us -> 11.9 us  [on_device(): lax.all_to_all(payload, 'seq', 0, 0, tiled=True).astype(jnp.float32)]
    add x1, other arithmetic: 0.01 us -> 1.32 us  [on_device(): carried * part_total + jnp.sum(suf_weights, axis=2) + own_weight]
  transfers between devices with their start and end apart: 2 -> 8, of which waited for: 2 -> 4; matrix products, arithmetic and copies ran while one was open for 14% -> 16% of each run, Pallas kernels for 0% -> 0%
where the time goes in v5:
time: 123 us; the launch traced here: 121 us
  starting transfers between devices  26.4 us (21%)
  local copies, waits for them, and re-layouts  25.6 us (21%)
  Pallas kernels  21.2 us (17%)
  other arithmetic  19 us (15%)
  waiting for transfers between devices  17.4 us (14%)
  matrix products  11.3 us (9%)
    pallas_call x1, Pallas kernels, prefix_partials(): pl.pallas_call(prefix_kernel, grid_spec=grid_spec, out_shape=jax.ShapeDty...  21.2 us
    all_to_all x1, starting transfers between devices, on_device(): lax.all_to_all(jnp.broadcast_to(own_query, (seq_count, row_count, query_w...  12.3 us
    all_to_all x1, waiting for transfers between devices, on_device(): lax.all_to_all(payload, 'seq', 0, 0, tiled=True).astype(jnp.float32)  11.9 us
    ppermute x6, starting transfers between devices, tp_sum(): lax.ppermute(sent, 'tp', [(j, (j + shift) % count) for j in range(count)])  8.97 us
    ppermute x6, waiting for transfers between devices, tp_sum(): lax.ppermute(sent, 'tp', [(j, (j + shift) % count) for j in range(count)])  5.44 us
    all_to_all x1, starting transfers between devices, on_device(): lax.all_to_all(payload, 'seq', 0, 0, tiled=True).astype(jnp.float32)  5.1 us
    unnamed x28, local copies, waits for them, and re-layouts  4.44 us
    gather x1, local copies, waits for them, and re-layouts, prefix_partials(): return jnp.take(out, rank, axis=0).astype(jnp.bfloat16)  2.94 us
  transfers between devices with their start and end apart: 8, of which 4 were waited for; matrix products, arithmetic and copies ran while one was open for 16% of the time, Pallas kernels for 0%

profile of v5, /device:TPU:2, one launch (start us, length us, event | category | flops | bytes accessed | tf_op | source)
XLA Modules:
  0.0 121.1 jit_solution(7922853670846052608)
XLA Ops:
  0.7 0.8 fusion.7
  1.5 1.4 %fusion.41 = f32[8,384]{1,0:T(8,128)S(1)} fusion(bf16[1152,384]{1,0:T(8,128)(2,1)} %param.26, bf16[8,1152]{1,0:T(8,128)(2,1)} %param.23, f32[1152]{0:T(1024)} %param.24, f32[8]{0:T(128)S(1)} %add_rsqrt_fusion.1), kind=kOutput, calls=%fused_computation.116 | convolution fusion | flops 7114752 | bytes 920096 | tf_op jit(solution)/shard_map/dot_general | solution.py:233
  3.2 1.4 %fusion.43 = f32[8,320]{1,0:T(8,128)S(1)} fusion(bf16[1152,320]{0,1:T(8,128)(2,1)} %param.25, bf16[8,1152]{1,0:T(8,128)(2,1)} %param.23, f32[1152]{0:T(1024)} %param.24, f32[8]{0:T(128)S(1)} %add_rsqrt_fusion.1), kind=kOutput, calls=%fused_computation.117 | convolution fusion | flops 5935104 | bytes 770592 | tf_op jit(solution)/shard_map/dot_general | solution.py:230
  5.1 0.8 add_convert_fusion.1
  6.9 0.8 broadcast_in_dim.127
  7.7 12.3 %all-to-all-start = ((bf16[64,8,384]{2,1,0:T(8,128)(2,1)}), bf16[64,8,384]{2,1,0:T(8,128)(2,1)}, u32[]{:S(2)}, u32[]{:S(2)}) async-start(bf16[64,8,384]{2,1,0:T(8,128)(2,1)} %broadcast_in_dim.127), calls=%async_computation | async-start | bytes 786432 | tf_op jit(solution)/shard_map/all_to_all | solution.py:257
  23.0 1.2 compare_convert_fusion.1.valid
  24.8 1.5 %copy.73 = bf16[8,128,384]{1,2,0:T(8,128)(2,1)S(1)} copy(bf16[8,128,384]{2,1,0:T(8,128)(2,1)} %param.31) | data formatting | bytes 1572864 | tf_op args[8]
  26.3 0.7 gather_fusion.3
  27.0 2.3 %copy.83 = bf16[8,128,384]{1,2,0:T(8,128)(2,1)} copy(bf16[8,128,384]{2,1,0:T(8,128)(2,1)} %param.32) | data formatting | bytes 1572864 | tf_op args[9]
  29.3 1.8 %gather_fusion.6 = bf16[5,8,128,64]{2,3,1,0:T(8,128)(2,1)S(1)} fusion(bf16[8,128,6,64]{1,3,2,0:T(8,128)(2,1)} %bitcast.60, s32[1024]{0:T(1024)S(1)} %pad_clamp_fusion), kind=kCustom, calls=%fused_computation.4.clone | custom fusion | bytes 1310740 | tf_op jit(solution)/shard_map/jit(_take)/gather | solution.py:281
  31.9 0.7 gather_fusion.2
  32.5 0.9 copy.70.perm_ref
  33.4 0.9 copy.71.sg_ref
  34.3 1.9 %compare_select_fusion.4 = (s32[15]{0:T(128)}, s32[15]{0:T(128)}) fusion(s32[15]{0:T(128)S(1)} %gather_fusion.2, s32[15]{0:T(128)S(1)} %gather_fusion.1, s32[]{:T(128)} %bitcast.3, s32[]{:T(128)} %bitcast.2, s32[15]{0:T(128)S(1)} %convert_reduce_fusion.1), kind=kLoop, calls=%fused_computation.99 | loop fusion | flops 225 | bytes 308 | tf_op jit(solution)/shard_map/jit(_where)/select_n | solution.py:119
  36.2 1.3 %select_bitcast_fusion.1 = (bf16[8,128,5,64]{1,3,0,2:T(8,128)(2,1)}, bf16[8,128,5,64]{1,3,0,2:T(8,128)(2,1)}) fusion(bf16[5,8,128,64]{2,3,1,0:T(8,128)(2,1)S(1)} %gather_fusion.3, pred[5]{0:T(512)(128)(4,1)S(1)} %get-tuple-element.38, bf16[5,8,128,64]{2,3,1,0:T(8,128)(2,1)S(1)} %gather_fusion.6), kind=kLoop, calls=%fused_computation.25 | loop fusion | flops 655360 | bytes 2621445 | tf_op jit(solution)/shard_map/jit(_take)/select_n | solution.py:280
  37.4 21.2 %shard_map.163 = f32[512,384]{1,0:T(8,128)} custom-call(s32[15]{0:T(128)} %get-tuple-element.35.tile_of, s32[15]{0:T(128)} %get-tuple-element.34.group_at, s32[15]{0:T(128)} %compare_convert_fusion.1.valid, s32[8]{0:T(128)} %subtract_clamp_fusion.limit, s32[5]{0:T(128)} %and_select_fusion.kv, s32[512,1]{1,0:T(8,128)} %copy.70.perm_ref, ...), custom_call_target="tpu_custom_call" | custom-call | flops 4152360960 | bytes 12976128 | tf_op jit(solution)/shard_map/pallas_call | solution.py:136
  58.6 2.9 %gather_fusion = bf16[512,384]{1,0:T(8,128)(2,1)S(1)} fusion(f32[512,384]{1,0:T(8,128)} %shard_map.163, s32[1024]{0:T(1024)S(1)} %pad_clamp_fusion.1), kind=kCustom, calls=%fused_computation.6 | custom fusion | bytes 788480 | tf_op jit(solution)/shard_map/jit(_take)/gather | solution.py:158
  61.6 0.9 fusion.2
  62.5 5.1 %all-to-all-start.1 = ((bf16[64,8,384]{2,1,0:T(8,128)(2,1)}), bf16[64,8,384]{2,1,0:T(8,128)(2,1)S(1)}, u32[]{:S(2)}, u32[]{:S(2)}) async-start(bf16[64,8,384]{2,1,0:T(8,128)(2,1)} %fusion.2), calls=%async_computation.1 | async-start | bytes 786432 | tf_op jit(solution)/shard_map/all_to_all | solution.py:270
  67.7 1.4 %fusion.5 = f32[8,5,1,128]{3,2,1,0:T(1,128)S(1)} fusion(bf16[8,128,5,64]{1,3,0,2:T(8,128)(2,1)} %get-tuple-element.36, bf16[8,5,64,1]{2,0,1,3:T(8,128)(2,1)S(1)} %bitcast.62), kind=kOutput, calls=%fused_computation.22 | convolution fusion | flops 655360 | bytes 680960 | tf_op jit(solution)/shard_map/rsd,rjsd->rsj/dot_general | solution.py:285
  70.2 11.9 %all-to-all-done.1 = bf16[64,8,384]{2,1,0:T(8,128)(2,1)S(1)} async-done(((bf16[64,8,384]{2,1,0:T(8,128)(2,1)}), bf16[64,8,384]{2,1,0:T(8,128)(2,1)S(1)}, u32[]{:S(2)}, u32[]{:S(2)}) %all-to-all-start.1) | async-done | bytes 393248 | tf_op jit(solution)/shard_map/all_to_all | solution.py:270
  82.1 1.2 %copy.72 = bf16[64,8,384]{0,2,1:T(8,128)(2,1)} copy(bf16[64,8,384]{2,1,0:T(8,128)(2,1)S(1)} %all-to-all-done.1) | data formatting | bytes 786432 | tf_op jit(solution)/shard_map/all_to_all | solution.py:270
  83.4 1.2 %convert_element_type.132 = f32[64,8,384]{0,2,1:T(8,128)S(1)} convert(bf16[64,8,384]{0,2,1:T(8,128)(2,1)} %copy.72) | non-fusion elementwise | flops 196608 | bytes 1179648 | tf_op jit(solution)/shard_map/convert_element_type | solution.py:270
  84.7 0.8 fusion.16
  86.1 1.3 %fusion.28 = (f32[8,5]{0,1:T(8,128)}, bf16[8,5,128,1]{2,0,1,3:T(8,128)(2,1)}) fusion(f32[8,5,1,128]{3,2,1,0:T(1,128)S(1)} %fusion.5, f32[8,5]{0,1:T(8,128)S(1)} %copy.82, pred[8,128]{1,0:T(8,128)(4,1)S(1)} %iota_compare_fusion.1), kind=kLoop, calls=%fused_computation.71 | loop fusion | flops 25560 | bytes 32064 | tf_op jit(solution)/shard_map/reduce_sum | solution.py:297
  87.5 1.1 fusion
  88.6 1.5 %reduce_sum.115 = f32[8,5,64]{2,1,0:T(8,128)} reshape(f32[8,320]{1,0:T(8,128)} %fusion) | data formatting | bytes 20480 | tf_op jit(solution)/shard_map/reduce_sum | solution.py:279
  90.1 1.3 %copy.84 = f32[8,5]{1,0:T(8,128)} copy(f32[8,5]{0,1:T(8,128)} %get-tuple-element.30) | data formatting | bytes 320 | tf_op jit(solution)/shard_map/reduce_sum | solution.py:297
  91.5 1.3 %add_add_fusion = (f32[8,5]{1,0:T(8,128)}, f32[8,5]{1,0:T(8,128)}) fusion(f32[8,5]{1,0:T(8,128)} %copy.84, f32[8,5]{1,0:T(8,128)} %get-tuple-element.16, f32[8,5]{1,0:T(8,128)} %copy-done.8, f32[8,5]{1,0:T(8,128)} %copy-done.7, f32[8,5]{1,0:T(8,128)S(1)} %fusion.39), kind=kLoop, calls=%fused_computation.83 | loop fusion | flops 240 | bytes 1120 | tf_op jit(solution)/shard_map/add | solution.py:297
  92.8 0.8 copy.85
  93.5 1.4 %copy.80 = f32[8,5]{0,1:T(8,128)} copy(bf16[8,5]{1,0:T(8,128)(2,1)} %get-tuple-element.12) | data formatting | bytes 240 | tf_op jit(solution)/shard_map/convert_element_type | solution.py:298
  94.9 1.3 %copy.78 = f32[8,5]{0,1:T(8,128)} copy(f32[8,5]{1,0:T(8,128)} %get-tuple-element.15) | data formatting | bytes 320 | tf_op jit(solution)/shard_map/exp | solution.py:294
  96.2 1.5 %fusion.3 = f32[8,5,1,64]{3,2,1,0:T(1,128)S(1)} fusion(bf16[8,128,5,64]{1,3,0,2:T(8,128)(2,1)} %get-tuple-element.37, bf16[8,5,128,1]{2,0,1,3:T(8,128)(2,1)} %get-tuple-element.31), kind=kOutput, calls=%fused_computation.20 | convolution fusion | flops 655360 | bytes 675840 | tf_op jit(solution)/shard_map/rsj,rjsd->rsd/dot_general | solution.py:300
  97.8 0.9 fusion.24
  98.7 0.7 reshape.240
  99.4 1.3 %convolution_convert_fusion.1 = bf16[8,1152]{1,0:T(8,128)(2,1)S(1)} fusion(bf16[8,320]{1,0:T(8,128)(2,1)} %reshape.240, bf16[320,1152]{1,0:T(8,128)(2,1)} %param.28), kind=kOutput, calls=%fused_computation.8 | convolution fusion | flops 5907456 | bytes 760832 | tf_op jit(solution)/shard_map/dot_general | solution.py:307
  101.3 2.4 %collective-permute-start.1 = (bf16[8,1152]{1,0:T(8,128)(2,1)S(1)}, bf16[8,1152]{1,0:T(8,128)(2,1)S(1)}, u32[]{:S(2)}, u32[]{:S(2)}) collective-permute-start(bf16[8,1152]{1,0:T(8,128)(2,1)S(1)} %convolution_convert_fusion.1), channel_id=1, source_target_pairs={{0,2},{1,3},{2,0},{3,1},{4,6},{5,7},{6,4},{7,5},{8,10},{9,11},{10,... | collective-permute-start | bytes 55304 | tf_op jit(solution)/shard_map/ppermute | solution.py:198
  103.7 1.8 %collective-permute-start = (bf16[8,1152]{1,0:T(8,128)(2,1)S(1)}, bf16[8,1152]{1,0:T(8,128)(2,1)S(1)}, u32[]{:S(2)}, u32[]{:S(2)}) collective-permute-start(bf16[8,1152]{1,0:T(8,128)(2,1)S(1)} %convolution_convert_fusion.1), channel_id=1, source_target_pairs={{0,1},{1,2},{2,3},{3,0},{4,5},{5,6},{6,7},{7,4},{8,9},{9,10},{10,1... | collective-permute-start | bytes 55304 | tf_op jit(solution)/shard_map/ppermute | solution.py:198
  105.5 1.0 collective-permute-done.1
  106.6 0.9 collective-permute-done
  107.5 0.9 fusion.11
  108.9 1.7 %fusion.35 = f32[8,768]{1,0:T(8,128)} fusion(bf16[1152,768]{1,0:T(8,128)(2,1)S(1)} %copy-done.1, bf16[8,1152]{1,0:T(8,128)(2,1)S(1)} %get-tuple-element.11, f32[1152]{0:T(1024)} %param.36, f32[8]{0:T(128)S(1)} %add_rsqrt_fusion), kind=kOutput, calls=%fused_computation.102 | convolution fusion | flops 14192640 | bytes 1817120 | tf_op jit(solution)/shard_map/dot_general | solution.py:313
  110.6 2.2 %convolution_convert_fusion = bf16[8,1152]{1,0:T(8,128)(2,1)S(1)} fusion(bf16[768,1152]{1,0:T(8,128)(2,1)S(1)} %copy-done, bf16[1152,768]{1,0:T(8,128)(2,1)} %param.38, f32[8,768]{1,0:T(8,128)} %fusion.35, bf16[8,1152]{1,0:T(8,128)(2,1)} %copy-done.4, f32[1152]{0:T(1024)S(1)} %copy-done.9, f32[8]{0:T(128)S(1)} %add_rsqrt_fusion), kind=kOutput, calls=%fused_computation.7 | convolution fusion | flops 28394496 | bytes 3605024 | tf_op jit(solution)/shard_map/dot_general | solution.py:316
  112.9 2.4 %collective-permute-start.5 = (bf16[8,1152]{1,0:T(8,128)(2,1)S(1)}, bf16[8,1152]{1,0:T(8,128)(2,1)S(1)}, u32[]{:S(2)}, u32[]{:S(2)}) collective-permute-start(bf16[8,1152]{1,0:T(8,128)(2,1)S(1)} %convolution_convert_fusion), channel_id=1, source_target_pairs={{0,3},{1,0},{2,1},{3,2},{4,7},{5,4},{6,5},{7,6},{8,11},{9,8},{10,9... | collective-permute-start | bytes 55304 | tf_op jit(solution)/shard_map/ppermute | solution.py:198
  115.2 0.9 collective-permute-start.4
  116.2 0.9 collective-permute-start.3
  117.0 3.5 %collective-permute-done.4 = bf16[8,1152]{1,0:T(8,128)(2,1)S(1)} collective-permute-done((bf16[8,1152]{1,0:T(8,128)(2,1)S(1)}, bf16[8,1152]{1,0:T(8,128)(2,1)S(1)}, u32[]{:S(2)}, u32[]{:S(2)}) %collective-permute-start.4) | collective-permute-done | bytes 18464 | tf_op jit(solution)/shard_map/ppermute | solution.py:198
  (86 shorter events, 10.6 us)
Async XLA Ops:
  0.0 110.6 %copy-start = (bf16[768,1152]{1,0:T(8,128)(2,1)S(1)}, bf16[768,1152]{1,0:T(8,128)(2,1)}, u32[]{:S(2)}) copy-start(bf16[768,1152]{1,0:T(8,128)(2,1)} %param.39) | copy-start | bytes 5308420
  0.0 4.8 %copy-start.10 = (s32[512]{0:T(512)S(1)}, s32[512]{0:T(512)}, u32[]{:S(2)}) copy-start(s32[512]{0:T(512)} %param.33) | copy-start | bytes 6148
  0.0 4.9 %copy-start.12 = (s32[8]{0:T(128)S(1)}, s32[8]{0:T(128)}, u32[]{:S(2)}) copy-start(s32[8]{0:T(128)} %param.34) | copy-start | bytes 100
  0.7 35.5 %copy-start.11 = (pred[5]{0:T(512)(128)(4,1)}, pred[5]{0:T(512)(128)(4,1)S(1)}, u32[]{:S(2)}) copy-start(pred[5]{0:T(512)(128)(4,1)S(1)} %get-tuple-element.38) | copy-start | bytes 19
  7.7 29.8 %all-to-all-start = ((bf16[64,8,384]{2,1,0:T(8,128)(2,1)}), bf16[64,8,384]{2,1,0:T(8,128)(2,1)}, u32[]{:S(2)}, u32[]{:S(2)}) async-start(bf16[64,8,384]{2,1,0:T(8,128)(2,1)} %broadcast_in_dim.127), calls=%async_computation | async-start | bytes 786432 | tf_op jit(solution)/shard_map/all_to_all | solution.py:257
  31.2 54.2 %copy-start.7 = (f32[8,5]{1,0:T(8,128)}, f32[8,5]{1,0:T(8,128)S(1)}, u32[]{:S(2)}) copy-start(f32[8,5]{1,0:T(8,128)S(1)} %copy.77) | copy-start | bytes 484
  61.6 7.6 %copy-start.2 = (bf16[1152,384]{1,0:T(8,128)(2,1)S(1)}, bf16[1152,384]{1,0:T(8,128)(2,1)}, u32[]{:S(2)}) copy-start(bf16[1152,384]{1,0:T(8,128)(2,1)} %param.27) | copy-start | bytes 2654212
  61.6 7.6 %copy-start.3 = (bf16[8,1152]{1,0:T(8,128)(2,1)S(1)}, bf16[8,1152]{1,0:T(8,128)(2,1)}, u32[]{:S(2)}) copy-start(bf16[8,1152]{1,0:T(8,128)(2,1)} %param.23) | copy-start | bytes 55300
  61.6 7.6 %copy-start.6 = (f32[1152]{0:T(1024)S(1)}, f32[1152]{0:T(1024)}, u32[]{:S(2)}) copy-start(f32[1152]{0:T(1024)} %param.24) | copy-start | bytes 13828
  62.5 19.6 %all-to-all-start.1 = ((bf16[64,8,384]{2,1,0:T(8,128)(2,1)}), bf16[64,8,384]{2,1,0:T(8,128)(2,1)S(1)}, u32[]{:S(2)}, u32[]{:S(2)}) async-start(bf16[64,8,384]{2,1,0:T(8,128)(2,1)} %fusion.2), calls=%async_computation.1 | async-start | bytes 786432 | tf_op jit(solution)/shard_map/all_to_all | solution.py:270
  86.1 1.4 %copy-start.8 = (f32[8,5]{1,0:T(8,128)}, f32[8,5]{1,0:T(8,128)S(1)}, u32[]{:S(2)}) copy-start(f32[8,5]{1,0:T(8,128)S(1)} %get-tuple-element.13) | copy-start | bytes 484
  88.6 20.3 %copy-start.1 = (bf16[1152,768]{1,0:T(8,128)(2,1)S(1)}, bf16[1152,768]{1,0:T(8,128)(2,1)}, u32[]{:S(2)}) copy-start(bf16[1152,768]{1,0:T(8,128)(2,1)} %param.37) | copy-start | bytes 5308420
  99.4 11.3 %copy-start.9 = (f32[1152]{0:T(1024)S(1)}, f32[1152]{0:T(1024)}, u32[]{:S(2)}) copy-start(f32[1152]{0:T(1024)} %param.36) | copy-start | bytes 13828
  100.7 4.8 %collective-permute-start.2 = (bf16[8,1152]{1,0:T(8,128)(2,1)S(1)}, bf16[8,1152]{1,0:T(8,128)(2,1)S(1)}, u32[]{:S(2)}, u32[]{:S(2)}) collective-permute-start(bf16[8,1152]{1,0:T(8,128)(2,1)S(1)} %convolution_convert_fusion.1), channel_id=1, source_target_pairs={{0,3},{1,0},{2,1},{3,2},{4,7},{5,4},{6,5},{7,6},{8,11},{9,8},{10,9... | collective-permute-start | bytes 55304 | tf_op jit(solution)/shard_map/ppermute | solution.py:198
  101.3 5.3 %collective-permute-start.1 = (bf16[8,1152]{1,0:T(8,128)(2,1)S(1)}, bf16[8,1152]{1,0:T(8,128)(2,1)S(1)}, u32[]{:S(2)}, u32[]{:S(2)}) collective-permute-start(bf16[8,1152]{1,0:T(8,128)(2,1)S(1)} %convolution_convert_fusion.1), channel_id=1, source_target_pairs={{0,2},{1,3},{2,0},{3,1},{4,6},{5,7},{6,4},{7,5},{8,10},{9,11},{10,... | collective-permute-start | bytes 55304 | tf_op jit(solution)/shard_map/ppermute | solution.py:198
  103.7 3.8 %collective-permute-start = (bf16[8,1152]{1,0:T(8,128)(2,1)S(1)}, bf16[8,1152]{1,0:T(8,128)(2,1)S(1)}, u32[]{:S(2)}, u32[]{:S(2)}) collective-permute-start(bf16[8,1152]{1,0:T(8,128)(2,1)S(1)} %convolution_convert_fusion.1), channel_id=1, source_target_pairs={{0,1},{1,2},{2,3},{3,0},{4,5},{5,6},{6,7},{7,4},{8,9},{9,10},{10,1... | collective-permute-start | bytes 55304 | tf_op jit(solution)/shard_map/ppermute | solution.py:198
  108.3 0.6 copy-start.4
  110.6 9.9 %copy-start.5 = (bf16[8,1152]{1,0:T(8,128)(2,1)S(1)}, bf16[8,1152]{1,0:T(8,128)(2,1)}, u32[]{:S(2)}) copy-start(bf16[8,1152]{1,0:T(8,128)(2,1)} %copy-done.4) | copy-start | bytes 55300
  112.9 4.2 %collective-permute-start.5 = (bf16[8,1152]{1,0:T(8,128)(2,1)S(1)}, bf16[8,1152]{1,0:T(8,128)(2,1)S(1)}, u32[]{:S(2)}, u32[]{:S(2)}) collective-permute-start(bf16[8,1152]{1,0:T(8,128)(2,1)S(1)} %convolution_convert_fusion), channel_id=1, source_target_pairs={{0,3},{1,0},{2,1},{3,2},{4,7},{5,4},{6,5},{7,6},{8,11},{9,8},{10,9... | collective-permute-start | bytes 55304 | tf_op jit(solution)/shard_map/ppermute | solution.py:198
  115.2 5.3 %collective-permute-start.4 = (bf16[8,1152]{1,0:T(8,128)(2,1)S(1)}, bf16[8,1152]{1,0:T(8,128)(2,1)S(1)}, u32[]{:S(2)}, u32[]{:S(2)}) collective-permute-start(bf16[8,1152]{1,0:T(8,128)(2,1)S(1)} %convolution_convert_fusion), channel_id=1, source_target_pairs={{0,2},{1,3},{2,0},{3,1},{4,6},{5,7},{6,4},{7,5},{8,10},{9,11},{10,... | collective-permute-start | bytes 55304 | tf_op jit(solution)/shard_map/ppermute | solution.py:198
  116.2 4.4 %collective-permute-start.3 = (bf16[8,1152]{1,0:T(8,128)(2,1)S(1)}, bf16[8,1152]{1,0:T(8,128)(2,1)S(1)}, u32[]{:S(2)}, u32[]{:S(2)}) collective-permute-start(bf16[8,1152]{1,0:T(8,128)(2,1)S(1)} %convolution_convert_fusion), channel_id=1, source_target_pairs={{0,1},{1,2},{2,3},{3,0},{4,5},{5,6},{6,7},{7,4},{8,9},{9,10},{10,1... | collective-permute-start | bytes 55304 | tf_op jit(solution)/shard_map/ppermute | solution.py:198

commit v6 on v5

--- a/solution.py
+++ b/solution.py
@@ -290,19 +290,22 @@
     own_keys = jnp.take(new_keys, kv_ids, axis=1).astype(jnp.float32)
     own_values = jnp.take(new_values, kv_ids, axis=1).astype(jnp.float32)
     own_score = jnp.sum(queries.astype(jnp.float32) * own_keys, axis=-1) * score_scale
-    final_top = jnp.maximum(jnp.maximum(part_top, suf_top), own_score)
-    carried = jnp.exp(part_top - final_top)
-    suf_weights = jnp.where(suf_live, jnp.exp(suf_scores - final_top[:, :, None]), 0.0)
-    own_weight = jnp.exp(own_score - final_top)
-    denominator = carried * part_total + jnp.sum(suf_weights, axis=2) + own_weight
+    local_top = jnp.maximum(suf_top, own_score)
+    suf_weights = jnp.where(suf_live, jnp.exp(suf_scores - local_top[:, :, None]), 0.0)
+    own_weight = jnp.exp(own_score - local_top)
+    local_total = jnp.sum(suf_weights, axis=2) + own_weight
     own_low = lax.optimization_barrier(own_weight.astype(jnp.bfloat16)).astype(jnp.float32)
-    numerator = carried[..., None] * part_mixed + own_low[..., None] * own_values
-    numerator = numerator + jnp.einsum(
+    local_mixed = own_low[..., None] * own_values + jnp.einsum(
         "rsj,rjsd->rsd",
         suf_weights.astype(jnp.bfloat16),
         suf_values,
         preferred_element_type=jnp.float32,
     )
+    final_top = jnp.maximum(part_top, local_top)
+    carried = jnp.exp(part_top - final_top)
+    kept = jnp.exp(local_top - final_top)
+    denominator = carried * part_total + kept * local_total
+    numerator = carried[..., None] * part_mixed + kept[..., None] * local_mixed
     attended = (numerator / denominator[..., None] * slot_used[None, :, None]).astype(jnp.bfloat16)
     head_part = jnp.dot(
         attended.reshape(row_count, slot_count * HD), w_out, preferred_element_type=jnp.float32

time: 123 us -> 117 us (0.951)
  other arithmetic: 19 us -> 15.6 us
  waiting for transfers between devices: 17.4 us -> 15 us
  starting transfers between devices: 26.4 us -> 28.3 us
    all_to_all x1, waiting for transfers between devices: 11.9 us -> 9.58 us  [on_device(): lax.all_to_all(payload, 'seq', 0, 0, tiled=True).astype(jnp.float32)]
    all_to_all x1, starting transfers between devices: 5.1 us -> 7 us  [on_device(): lax.all_to_all(payload, 'seq', 0, 0, tiled=True).astype(jnp.float32)]
    exp x0 -> x1, local copies, waits for them, and re-layouts: none -> 1.34 us  [on_device(): kept = jnp.exp(local_top - final_top)]
  transfers between devices with their start and end apart: 8 -> 8, of which waited for: 4 -> 4; matrix products, arithmetic and copies ran while one was open for 16% -> 19% of each run, Pallas kernels for 0% -> 0%
where the time goes in v6:
time: 117 us; the launch traced here: 116 us
  starting transfers between devices  28.3 us (24%)
  local copies, waits for them, and re-layouts  24.9 us (21%)
  Pallas kernels  21.2 us (18%)
  other arithmetic  15.6 us (13%)
  waiting for transfers between devices  15 us (13%)
  matrix products  10.8 us (9%)
    pallas_call x1, Pallas kernels, prefix_partials(): pl.pallas_call(prefix_kernel, grid_spec=grid_spec, out_shape=jax.ShapeDty...  21.2 us
    all_to_all x1, starting transfers between devices, on_device(): lax.all_to_all(jnp.broadcast_to(own_query, (seq_count, row_count, query_w...  12.3 us
    all_to_all x1, waiting for transfers between devices, on_device(): lax.all_to_all(payload, 'seq', 0, 0, tiled=True).astype(jnp.float32)  9.58 us
    ppermute x6, starting transfers between devices, tp_sum(): lax.ppermute(sent, 'tp', [(j, (j + shift) % count) for j in range(count)])  8.97 us
    all_to_all x1, starting transfers between devices, on_device(): lax.all_to_all(payload, 'seq', 0, 0, tiled=True).astype(jnp.float32)  7 us
    ppermute x6, waiting for transfers between devices, tp_sum(): lax.ppermute(sent, 'tp', [(j, (j + shift) % count) for j in range(count)])  5.43 us
    unnamed x28, local copies, waits for them, and re-layouts  4.69 us
    gather x1, local copies, waits for them, and re-layouts, prefix_partials(): return jnp.take(out, rank, axis=0).astype(jnp.bfloat16)  3.01 us
  transfers between devices with their start and end apart: 8, of which 4 were waited for; matrix products, arithmetic and copies ran while one was open for 19% of the time, Pallas kernels for 0%

profile of v6, /device:TPU:2, one launch (start us, length us, event | category | flops | bytes accessed | tf_op | source)
XLA Modules:
  0.0 116.1 jit_solution(18251504785294851947)
XLA Ops:
  0.7 0.8 fusion.7
  1.5 1.4 %fusion.44 = f32[8,384]{1,0:T(8,128)S(1)} fusion(bf16[1152,384]{1,0:T(8,128)(2,1)} %param.26, bf16[8,1152]{1,0:T(8,128)(2,1)} %param.23, f32[1152]{0:T(1024)} %param.24, f32[8]{0:T(128)S(1)} %add_rsqrt_fusion.1), kind=kOutput, calls=%fused_computation.120 | convolution fusion | flops 7114752 | bytes 920096 | tf_op jit(solution)/shard_map/dot_general | solution.py:233
  3.1 1.4 %fusion.46 = f32[8,320]{1,0:T(8,128)S(1)} fusion(bf16[1152,320]{0,1:T(8,128)(2,1)} %param.25, bf16[8,1152]{1,0:T(8,128)(2,1)} %param.23, f32[1152]{0:T(1024)} %param.24, f32[8]{0:T(128)S(1)} %add_rsqrt_fusion.1), kind=kOutput, calls=%fused_computation.121 | convolution fusion | flops 5935104 | bytes 770592 | tf_op jit(solution)/shard_map/dot_general | solution.py:230
  5.0 0.8 add_convert_fusion.1
  6.9 0.8 broadcast_in_dim.128
  7.7 12.3 %all-to-all-start = ((bf16[64,8,384]{2,1,0:T(8,128)(2,1)}), bf16[64,8,384]{2,1,0:T(8,128)(2,1)}, u32[]{:S(2)}, u32[]{:S(2)}) async-start(bf16[64,8,384]{2,1,0:T(8,128)(2,1)} %broadcast_in_dim.128), calls=%async_computation | async-start | bytes 786432 | tf_op jit(solution)/shard_map/all_to_all | solution.py:257
  22.2 0.6 and_select_fusion.kv
  22.9 1.5 %copy.75 = bf16[8,128,384]{1,2,0:T(8,128)(2,1)S(1)} copy(bf16[8,128,384]{2,1,0:T(8,128)(2,1)} %param.31) | data formatting | bytes 1572864 | tf_op args[8]
  24.4 0.7 gather_fusion.3
  25.1 2.3 %copy.86 = bf16[8,128,384]{1,2,0:T(8,128)(2,1)} copy(bf16[8,128,384]{2,1,0:T(8,128)(2,1)} %param.32) | data formatting | bytes 1572864 | tf_op args[9]
  27.4 1.8 %gather_fusion.6 = bf16[5,8,128,64]{2,3,1,0:T(8,128)(2,1)S(1)} fusion(bf16[8,128,6,64]{1,3,2,0:T(8,128)(2,1)} %bitcast.64, s32[1024]{0:T(1024)S(1)} %pad_clamp_fusion), kind=kCustom, calls=%fused_computation.4.clone | custom fusion | bytes 1310740 | tf_op jit(solution)/shard_map/jit(_take)/gather | solution.py:281
  29.4 1.0 select_bitcast_fusion.1
  31.0 0.7 gather_fusion.1
  31.6 0.7 gather_fusion.2
  32.3 0.9 copy.72.perm_ref
  33.1 0.9 copy.73.sg_ref
  34.0 1.1 compare_convert_fusion.1.valid
  35.6 1.8 %compare_select_fusion.4 = (s32[15]{0:T(128)}, s32[15]{0:T(128)}) fusion(s32[15]{0:T(128)S(1)} %gather_fusion.2, s32[15]{0:T(128)S(1)} %gather_fusion.1, s32[]{:T(128)} %bitcast.3, s32[]{:T(128)} %bitcast.2, s32[15]{0:T(128)S(1)} %convert_reduce_fusion.1), kind=kLoop, calls=%fused_computation.103 | loop fusion | flops 225 | bytes 308 | tf_op jit(solution)/shard_map/jit(_where)/select_n | solution.py:119
  37.4 21.2 %shard_map.163 = f32[512,384]{1,0:T(8,128)} custom-call(s32[15]{0:T(128)} %get-tuple-element.36.tile_of, s32[15]{0:T(128)} %get-tuple-element.35.group_at, s32[15]{0:T(128)} %compare_convert_fusion.1.valid, s32[8]{0:T(128)} %subtract_clamp_fusion.limit, s32[5]{0:T(128)} %and_select_fusion.kv, s32[512,1]{1,0:T(8,128)} %copy.72.perm_ref, ...), custom_call_target="tpu_custom_call" | custom-call | flops 4152360960 | bytes 12976128 | tf_op jit(solution)/shard_map/pallas_call | solution.py:136
  58.6 3.0 %gather_fusion = bf16[512,384]{1,0:T(8,128)(2,1)S(1)} fusion(f32[512,384]{1,0:T(8,128)} %shard_map.163, s32[1024]{0:T(1024)S(1)} %pad_clamp_fusion.1), kind=kCustom, calls=%fused_computation.6 | custom fusion | bytes 788480 | tf_op jit(solution)/shard_map/jit(_take)/gather | solution.py:158
  61.6 0.9 fusion.2
  62.5 7.0 %all-to-all-start.1 = ((bf16[64,8,384]{2,1,0:T(8,128)(2,1)}), bf16[64,8,384]{2,1,0:T(8,128)(2,1)S(1)}, u32[]{:S(2)}, u32[]{:S(2)}) async-start(bf16[64,8,384]{2,1,0:T(8,128)(2,1)} %fusion.2), calls=%async_computation.1 | async-start | bytes 786432 | tf_op jit(solution)/shard_map/all_to_all | solution.py:270
  71.0 0.7 copy.87
  71.6 0.7 copy.83
  72.3 2.1 %fusion.3 = f32[8,5,1,64]{3,2,1,0:T(1,128)} fusion(bf16[8,128,5,64]{1,3,0,2:T(8,128)(2,1)} %get-tuple-element.38, bf16[8,5,128,1]{2,0,1,3:T(8,128)(2,1)S(1)} %get-tuple-element.32), kind=kOutput, calls=%fused_computation.20 | convolution fusion | flops 655360 | bytes 675840 | tf_op jit(solution)/shard_map/rsj,rjsd->rsd/dot_general | solution.py:298
  74.4 9.6 %all-to-all-done.1 = bf16[64,8,384]{2,1,0:T(8,128)(2,1)S(1)} async-done(((bf16[64,8,384]{2,1,0:T(8,128)(2,1)}), bf16[64,8,384]{2,1,0:T(8,128)(2,1)S(1)}, u32[]{:S(2)}, u32[]{:S(2)}) %all-to-all-start.1) | async-done | bytes 393248 | tf_op jit(solution)/shard_map/all_to_all | solution.py:270
  84.7 0.8 fusion.16
  85.6 1.1 fusion
  86.6 1.4 %reduce_sum.115 = f32[8,5,64]{2,1,0:T(8,128)} reshape(f32[8,320]{1,0:T(8,128)} %fusion) | data formatting | bytes 20480 | tf_op jit(solution)/shard_map/reduce_sum | solution.py:279
  88.0 1.3 %multiply_add_fusion.1 = (f32[8,5]{1,0:T(8,128)}, f32[8,5]{1,0:T(8,128)}, f32[8,5]{1,0:T(8,128)}) fusion(f32[8,5]{1,0:T(8,128)} %copy.87, f32[8,5]{1,0:T(8,128)} %get-tuple-element.17, f32[8,5]{1,0:T(8,128)} %copy-done.7, f32[8,5]{1,0:T(8,128)S(1)} %copy.78, f32[8,5]{1,0:T(8,128)} %copy-done.8), kind=kLoop, calls=%fused_computation.88 | loop fusion | flops 360 | bytes 1280 | tf_op jit(solution)/shard_map/add | solution.py:307
  89.3 0.8 copy.88
  90.1 1.3 %copy.82 = f32[8,5]{0,1:T(8,128)} copy(f32[8,5]{1,0:T(8,128)} %get-tuple-element.16) | data formatting | bytes 320 | tf_op jit(solution)/shard_map/exp | solution.py:306
  91.4 1.3 %copy.80 = f32[8,5]{0,1:T(8,128)} copy(f32[8,5]{1,0:T(8,128)} %get-tuple-element.15) | data formatting | bytes 320 | tf_op jit(solution)/shard_map/exp | solution.py:305
  92.8 0.9 fusion.28
  93.6 0.7 reshape.247
  94.3 1.3 %convolution_convert_fusion.1 = bf16[8,1152]{1,0:T(8,128)(2,1)S(1)} fusion(bf16[8,320]{1,0:T(8,128)(2,1)} %reshape.247, bf16[320,1152]{1,0:T(8,128)(2,1)} %param.28), kind=kOutput, calls=%fused_computation.8 | convolution fusion | flops 5907456 | bytes 760832 | tf_op jit(solution)/shard_map/dot_general | solution.py:310
  96.3 2.4 %collective-permute-start.1 = (bf16[8,1152]{1,0:T(8,128)(2,1)S(1)}, bf16[8,1152]{1,0:T(8,128)(2,1)S(1)}, u32[]{:S(2)}, u32[]{:S(2)}) collective-permute-start(bf16[8,1152]{1,0:T(8,128)(2,1)S(1)} %convolution_convert_fusion.1), channel_id=1, source_target_pairs={{0,2},{1,3},{2,0},{3,1},{4,6},{5,7},{6,4},{7,5},{8,10},{9,11},{10,... | collective-permute-start | bytes 55304 | tf_op jit(solution)/shard_map/ppermute | solution.py:198
  98.7 1.8 %collective-permute-start = (bf16[8,1152]{1,0:T(8,128)(2,1)S(1)}, bf16[8,1152]{1,0:T(8,128)(2,1)S(1)}, u32[]{:S(2)}, u32[]{:S(2)}) collective-permute-start(bf16[8,1152]{1,0:T(8,128)(2,1)S(1)} %convolution_convert_fusion.1), channel_id=1, source_target_pairs={{0,1},{1,2},{2,3},{3,0},{4,5},{5,6},{6,7},{7,4},{8,9},{9,10},{10,1... | collective-permute-start | bytes 55304 | tf_op jit(solution)/shard_map/ppermute | solution.py:198
  100.5 1.0 collective-permute-done.1
  101.5 0.9 collective-permute-done
  102.4 0.9 fusion.11
  103.9 1.7 %fusion.38 = f32[8,768]{1,0:T(8,128)} fusion(bf16[1152,768]{1,0:T(8,128)(2,1)S(1)} %copy-done.1, bf16[8,1152]{1,0:T(8,128)(2,1)S(1)} %get-tuple-element.11, f32[1152]{0:T(1024)} %param.36, f32[8]{0:T(128)S(1)} %add_rsqrt_fusion), kind=kOutput, calls=%fused_computation.106 | convolution fusion | flops 14192640 | bytes 1817120 | tf_op jit(solution)/shard_map/dot_general | solution.py:316
  105.6 2.2 %convolution_convert_fusion = bf16[8,1152]{1,0:T(8,128)(2,1)S(1)} fusion(bf16[768,1152]{1,0:T(8,128)(2,1)S(1)} %copy-done, bf16[1152,768]{1,0:T(8,128)(2,1)} %param.38, f32[8,768]{1,0:T(8,128)} %fusion.38, bf16[8,1152]{1,0:T(8,128)(2,1)} %copy-done.4, f32[1152]{0:T(1024)S(1)} %copy-done.9, f32[8]{0:T(128)S(1)} %add_rsqrt_fusion), kind=kOutput, calls=%fused_computation.7 | convolution fusion | flops 28394496 | bytes 3605024 | tf_op jit(solution)/shard_map/dot_general | solution.py:319
  107.8 2.4 %collective-permute-start.5 = (bf16[8,1152]{1,0:T(8,128)(2,1)S(1)}, bf16[8,1152]{1,0:T(8,128)(2,1)S(1)}, u32[]{:S(2)}, u32[]{:S(2)}) collective-permute-start(bf16[8,1152]{1,0:T(8,128)(2,1)S(1)} %convolution_convert_fusion), channel_id=1, source_target_pairs={{0,3},{1,0},{2,1},{3,2},{4,7},{5,4},{6,5},{7,6},{8,11},{9,8},{10,9... | collective-permute-start | bytes 55304 | tf_op jit(solution)/shard_map/ppermute | solution.py:198
  110.2 0.9 collective-permute-start.4
  111.1 0.9 collective-permute-start.3
  112.0 3.5 %collective-permute-done.4 = bf16[8,1152]{1,0:T(8,128)(2,1)S(1)} collective-permute-done((bf16[8,1152]{1,0:T(8,128)(2,1)S(1)}, bf16[8,1152]{1,0:T(8,128)(2,1)S(1)}, u32[]{:S(2)}, u32[]{:S(2)}) %collective-permute-start.4) | collective-permute-done | bytes 18464 | tf_op jit(solution)/shard_map/ppermute | solution.py:198
  115.5 0.6 fusion.14
  (87 shorter events, 9.2 us)
Async XLA Ops:
  0.0 105.6 %copy-start = (bf16[768,1152]{1,0:T(8,128)(2,1)S(1)}, bf16[768,1152]{1,0:T(8,128)(2,1)}, u32[]{:S(2)}) copy-start(bf16[768,1152]{1,0:T(8,128)(2,1)} %param.39) | copy-start | bytes 5308420
  0.0 4.8 %copy-start.10 = (s32[512]{0:T(512)S(1)}, s32[512]{0:T(512)}, u32[]{:S(2)}) copy-start(s32[512]{0:T(512)} %param.33) | copy-start | bytes 6148
  0.0 4.9 %copy-start.12 = (s32[8]{0:T(128)S(1)}, s32[8]{0:T(128)}, u32[]{:S(2)}) copy-start(s32[8]{0:T(128)} %param.34) | copy-start | bytes 100
  0.7 28.7 %copy-start.11 = (pred[5]{0:T(512)(128)(4,1)}, pred[5]{0:T(512)(128)(4,1)S(1)}, u32[]{:S(2)}) copy-start(pred[5]{0:T(512)(128)(4,1)S(1)} %get-tuple-element.39) | copy-start | bytes 19
  7.7 29.7 %all-to-all-start = ((bf16[64,8,384]{2,1,0:T(8,128)(2,1)}), bf16[64,8,384]{2,1,0:T(8,128)(2,1)}, u32[]{:S(2)}, u32[]{:S(2)}) async-start(bf16[64,8,384]{2,1,0:T(8,128)(2,1)} %broadcast_in_dim.128), calls=%async_computation | async-start | bytes 786432 | tf_op jit(solution)/shard_map/all_to_all | solution.py:257
  58.6 11.1 %copy-start.2 = (bf16[1152,384]{1,0:T(8,128)(2,1)S(1)}, bf16[1152,384]{1,0:T(8,128)(2,1)}, u32[]{:S(2)}) copy-start(bf16[1152,384]{1,0:T(8,128)(2,1)} %param.27) | copy-start | bytes 2654212
  58.6 11.1 %copy-start.3 = (bf16[8,1152]{1,0:T(8,128)(2,1)S(1)}, bf16[8,1152]{1,0:T(8,128)(2,1)}, u32[]{:S(2)}) copy-start(bf16[8,1152]{1,0:T(8,128)(2,1)} %param.23) | copy-start | bytes 55300
  58.6 11.1 %copy-start.6 = (f32[1152]{0:T(1024)S(1)}, f32[1152]{0:T(1024)}, u32[]{:S(2)}) copy-start(f32[1152]{0:T(1024)} %param.24) | copy-start | bytes 13828
  62.5 21.5 %all-to-all-start.1 = ((bf16[64,8,384]{2,1,0:T(8,128)(2,1)}), bf16[64,8,384]{2,1,0:T(8,128)(2,1)S(1)}, u32[]{:S(2)}, u32[]{:S(2)}) async-start(bf16[64,8,384]{2,1,0:T(8,128)(2,1)} %fusion.2), calls=%async_computation.1 | async-start | bytes 786432 | tf_op jit(solution)/shard_map/all_to_all | solution.py:270
  69.5 0.6 copy-start.7
  84.7 0.8 copy-start.8
  85.5 18.4 %copy-start.1 = (bf16[1152,768]{1,0:T(8,128)(2,1)S(1)}, bf16[1152,768]{1,0:T(8,128)(2,1)}, u32[]{:S(2)}) copy-start(bf16[1152,768]{1,0:T(8,128)(2,1)} %param.37) | copy-start | bytes 5308420
  94.3 11.3 %copy-start.9 = (f32[1152]{0:T(1024)S(1)}, f32[1152]{0:T(1024)}, u32[]{:S(2)}) copy-start(f32[1152]{0:T(1024)} %param.36) | copy-start | bytes 13828
  95.7 4.8 %collective-permute-start.2 = (bf16[8,1152]{1,0:T(8,128)(2,1)S(1)}, bf16[8,1152]{1,0:T(8,128)(2,1)S(1)}, u32[]{:S(2)}, u32[]{:S(2)}) collective-permute-start(bf16[8,1152]{1,0:T(8,128)(2,1)S(1)} %convolution_convert_fusion.1), channel_id=1, source_target_pairs={{0,3},{1,0},{2,1},{3,2},{4,7},{5,4},{6,5},{7,6},{8,11},{9,8},{10,9... | collective-permute-start | bytes 55304 | tf_op jit(solution)/shard_map/ppermute | solution.py:198
  96.3 5.3 %collective-permute-start.1 = (bf16[8,1152]{1,0:T(8,128)(2,1)S(1)}, bf16[8,1152]{1,0:T(8,128)(2,1)S(1)}, u32[]{:S(2)}, u32[]{:S(2)}) collective-permute-start(bf16[8,1152]{1,0:T(8,128)(2,1)S(1)} %convolution_convert_fusion.1), channel_id=1, source_target_pairs={{0,2},{1,3},{2,0},{3,1},{4,6},{5,7},{6,4},{7,5},{8,10},{9,11},{10,... | collective-permute-start | bytes 55304 | tf_op jit(solution)/shard_map/ppermute | solution.py:198
  98.7 3.8 %collective-permute-start = (bf16[8,1152]{1,0:T(8,128)(2,1)S(1)}, bf16[8,1152]{1,0:T(8,128)(2,1)S(1)}, u32[]{:S(2)}, u32[]{:S(2)}) collective-permute-start(bf16[8,1152]{1,0:T(8,128)(2,1)S(1)} %convolution_convert_fusion.1), channel_id=1, source_target_pairs={{0,1},{1,2},{2,3},{3,0},{4,5},{5,6},{6,7},{7,4},{8,9},{9,10},{10,1... | collective-permute-start | bytes 55304 | tf_op jit(solution)/shard_map/ppermute | solution.py:198
  103.3 0.6 copy-start.4
  105.6 9.9 %copy-start.5 = (bf16[8,1152]{1,0:T(8,128)(2,1)S(1)}, bf16[8,1152]{1,0:T(8,128)(2,1)}, u32[]{:S(2)}) copy-start(bf16[8,1152]{1,0:T(8,128)(2,1)} %copy-done.4) | copy-start | bytes 55300
  107.8 4.2 %collective-permute-start.5 = (bf16[8,1152]{1,0:T(8,128)(2,1)S(1)}, bf16[8,1152]{1,0:T(8,128)(2,1)S(1)}, u32[]{:S(2)}, u32[]{:S(2)}) collective-permute-start(bf16[8,1152]{1,0:T(8,128)(2,1)S(1)} %convolution_convert_fusion), channel_id=1, source_target_pairs={{0,3},{1,0},{2,1},{3,2},{4,7},{5,4},{6,5},{7,6},{8,11},{9,8},{10,9... | collective-permute-start | bytes 55304 | tf_op jit(solution)/shard_map/ppermute | solution.py:198
  110.2 5.3 %collective-permute-start.4 = (bf16[8,1152]{1,0:T(8,128)(2,1)S(1)}, bf16[8,1152]{1,0:T(8,128)(2,1)S(1)}, u32[]{:S(2)}, u32[]{:S(2)}) collective-permute-start(bf16[8,1152]{1,0:T(8,128)(2,1)S(1)} %convolution_convert_fusion), channel_id=1, source_target_pairs={{0,2},{1,3},{2,0},{3,1},{4,6},{5,7},{6,4},{7,5},{8,10},{9,11},{10,... | collective-permute-start | bytes 55304 | tf_op jit(solution)/shard_map/ppermute | solution.py:198
  111.1 4.4 %collective-permute-start.3 = (bf16[8,1152]{1,0:T(8,128)(2,1)S(1)}, bf16[8,1152]{1,0:T(8,128)(2,1)S(1)}, u32[]{:S(2)}, u32[]{:S(2)}) collective-permute-start(bf16[8,1152]{1,0:T(8,128)(2,1)S(1)} %convolution_convert_fusion), channel_id=1, source_target_pairs={{0,1},{1,2},{2,3},{3,0},{4,5},{5,6},{6,7},{7,4},{8,9},{9,10},{10,1... | collective-permute-start | bytes 55304 | tf_op jit(solution)/shard_map/ppermute | solution.py:198

commit v7 on v6

--- a/solution.py
+++ b/solution.py
@@ -37,7 +37,7 @@
     @pl.when(first)
     def _():
         top_lanes = jnp.logical_and(wide_lane >= tail_at + HD, wide_lane < tail_at + HD + slot_count)
-        o_ref[...] = jnp.where(top_lanes, NEG_FILL, 0.0).astype(jnp.float32)
+        o_ref[...] = jnp.where(top_lanes, NEG_FILL, 0.0).astype(o_ref.dtype)
 
     group = group_at[step]
     live_count = limit[group]
@@ -94,7 +94,7 @@
             for slot in range(slot_count):
                 tail = jnp.where(lane == HD + index * slot_count + slot, part[slot * rows : (slot + 1) * rows], tail)
         out[-1] = tail
-        o_ref[...] = jnp.where(row_live, jnp.concatenate(out, axis=1), o_ref[...])
+        o_ref[...] = jnp.where(row_live, jnp.concatenate(out, axis=1).astype(o_ref.dtype), o_ref[...])
 
 
 def prefix_partials(every_query, group_of, prefix_len, seq_index, prefix_keys, prefix_values, kv_ids):
@@ -136,7 +136,7 @@
     out = pl.pallas_call(
         prefix_kernel,
         grid_spec=grid_spec,
-        out_shape=jax.ShapeDtypeStruct((request_count, width), jnp.float32),
+        out_shape=jax.ShapeDtypeStruct((request_count, width), jnp.bfloat16),
         compiler_params=pltpu.CompilerParams(dimension_semantics=("arbitrary",)),
         cost_estimate=pl.CostEstimate(
             flops=flops,
@@ -155,7 +155,8 @@
         prefix_keys,
         prefix_values,
     )
-    return jnp.take(out, rank, axis=0).astype(jnp.bfloat16)
+    unsort = (rank[:, None] == spots[None, :]).astype(jnp.bfloat16)
+    return jnp.dot(unsort, out, preferred_element_type=jnp.float32).astype(jnp.bfloat16)
 
 
 def rms_scale(values_in, gain_row):

time: 117 us -> 114 us (0.974)
  local copies, waits for them, and re-layouts: 24.9 us -> 21.8 us
  matrix products: 10.8 us -> 13.1 us
    gather x1 -> x0, local copies, waits for them, and re-layouts: 3.01 us -> none  [prefix_partials(): return jnp.take(out, rank, axis=0).astype(jnp.bfloat16)]
    dot_general x0 -> x1, matrix products: none -> 2.31 us  [prefix_partials(): jnp.dot(unsort, out, preferred_element_type=jnp.float32)]
where the time goes in v7:
time: 114 us
  starting transfers between devices  27.2 us (24%)
  local copies, waits for them, and re-layouts  21.8 us (19%)
  Pallas kernels  21.6 us (19%)
  waiting for transfers between devices  15 us (13%)
  other arithmetic  14.8 us (13%)
  matrix products  13.1 us (11%)
    pallas_call x1, Pallas kernels, prefix_partials(): pl.pallas_call(prefix_kernel, grid_spec=grid_spec, out_shape=jax.ShapeDty...  21.6 us
    all_to_all x1, starting transfers between devices, on_device(): lax.all_to_all(jnp.broadcast_to(own_query, (seq_count, row_count, query_w...  12.3 us
    all_to_all x1, waiting for transfers between devices, on_device(): lax.all_to_all(payload, 'seq', 0, 0, tiled=True).astype(jnp.float32)  9.58 us
    ppermute x6, starting transfers between devices, tp_sum(): lax.ppermute(sent, 'tp', [(j, (j + shift) % count) for j in range(count)])  8.97 us
    all_to_all x1, starting transfers between devices, on_device(): lax.all_to_all(payload, 'seq', 0, 0, tiled=True).astype(jnp.float32)  5.87 us
    ppermute x6, waiting for transfers between devices, tp_sum(): lax.ppermute(sent, 'tp', [(j, (j + shift) % count) for j in range(count)])  5.44 us
    unnamed x28, local copies, waits for them, and re-layouts  4.68 us
    dot_general x1, matrix products, prefix_partials(): jnp.dot(unsort, out, preferred_element_type=jnp.float32)  2.31 us
  transfers between devices with their start and end apart: 8, of which 4 were waited for; matrix products, arithmetic and copies ran while one was open for 19% of the time, Pallas kernels for 0%

profile of v7, /device:TPU:2, one launch (start us, length us, event | category | flops | bytes accessed | tf_op | source)
XLA Modules:
  0.0 113.7 jit_solution(9799329270823719792)
XLA Ops:
  0.6 0.8 fusion.8
  1.5 1.4 %fusion.45 = f32[8,384]{1,0:T(8,128)S(1)} fusion(bf16[1152,384]{1,0:T(8,128)(2,1)} %param.26, bf16[8,1152]{1,0:T(8,128)(2,1)} %param.23, f32[1152]{0:T(1024)} %param.24, f32[8]{0:T(128)S(1)} %add_rsqrt_fusion.1), kind=kOutput, calls=%fused_computation.117 | convolution fusion | flops 7114752 | bytes 920096 | tf_op jit(solution)/shard_map/dot_general | solution.py:234
  3.1 1.4 %fusion.47 = f32[8,320]{1,0:T(8,128)S(1)} fusion(bf16[1152,320]{0,1:T(8,128)(2,1)} %param.25, bf16[8,1152]{1,0:T(8,128)(2,1)} %param.23, f32[1152]{0:T(1024)} %param.24, f32[8]{0:T(128)S(1)} %add_rsqrt_fusion.1), kind=kOutput, calls=%fused_computation.118 | convolution fusion | flops 5935104 | bytes 770592 | tf_op jit(solution)/shard_map/dot_general | solution.py:231
  5.0 0.8 add_convert_fusion.1
  6.8 0.8 broadcast_in_dim.116
  7.6 12.3 %all-to-all-start = ((bf16[64,8,384]{2,1,0:T(8,128)(2,1)}), bf16[64,8,384]{2,1,0:T(8,128)(2,1)}, u32[]{:S(2)}, u32[]{:S(2)}) async-start(bf16[64,8,384]{2,1,0:T(8,128)(2,1)} %broadcast_in_dim.116), calls=%async_computation | async-start | bytes 786432 | tf_op jit(solution)/shard_map/all_to_all | solution.py:258
  20.8 0.6 slice.49
  22.2 1.5 %copy.74 = bf16[8,128,384]{1,2,0:T(8,128)(2,1)S(1)} copy(bf16[8,128,384]{2,1,0:T(8,128)(2,1)} %param.31) | data formatting | bytes 1572864 | tf_op args[8]
  23.7 0.7 gather_fusion.2
  24.4 2.3 %copy.85 = bf16[8,128,384]{1,2,0:T(8,128)(2,1)} copy(bf16[8,128,384]{2,1,0:T(8,128)(2,1)} %param.32) | data formatting | bytes 1572864 | tf_op args[9]
  26.7 1.8 %gather_fusion.5 = bf16[5,8,128,64]{2,3,1,0:T(8,128)(2,1)S(1)} fusion(bf16[8,128,6,64]{1,3,2,0:T(8,128)(2,1)} %bitcast.61, s32[1024]{0:T(1024)S(1)} %pad_clamp_fusion), kind=kCustom, calls=%fused_computation.4.clone | custom fusion | bytes 1310740 | tf_op jit(solution)/shard_map/jit(_take)/gather | solution.py:282
  28.7 1.0 select_bitcast_fusion.1
  30.2 0.7 gather_fusion
  30.9 0.7 gather_fusion.1
  31.6 0.9 copy.71.perm_ref
  32.4 0.9 copy.72.sg_ref
  33.8 1.2 %compare_convert_fusion.1.valid = s32[15]{0:T(128)} fusion(s32[]{:T(128)} %bitcast.2), kind=kLoop, calls=%fused_computation.101 | loop fusion | flops 30 | bytes 64 | tf_op jit(solution)/shard_map/convert_element_type | solution.py:118
  35.5 1.8 %compare_select_fusion.2 = (s32[15]{0:T(128)}, s32[15]{0:T(128)}) fusion(s32[15]{0:T(128)S(1)} %gather_fusion.1, s32[15]{0:T(128)S(1)} %gather_fusion, s32[]{:T(128)} %bitcast.3, s32[]{:T(128)} %bitcast.2, s32[15]{0:T(128)S(1)} %convert_reduce_fusion.1), kind=kLoop, calls=%fused_computation.100 | loop fusion | flops 225 | bytes 308 | tf_op jit(solution)/shard_map/jit(_where)/select_n | solution.py:119
  37.4 21.6 %shard_map.163 = bf16[512,384]{1,0:T(8,128)(2,1)} custom-call(s32[15]{0:T(128)} %get-tuple-element.36.tile_of, s32[15]{0:T(128)} %get-tuple-element.35.group_at, s32[15]{0:T(128)} %compare_convert_fusion.1.valid, s32[8]{0:T(128)} %subtract_clamp_fusion.limit, s32[5]{0:T(128)} %and_select_fusion.kv, s32[512,1]{1,0:T(8,128)} %copy.71.perm_ref, ...), custom_call_target="tpu_custom_call" | custom-call | flops 4152360960 | bytes 12976128 | tf_op jit(solution)/shard_map/pallas_call | solution.py:136
  59.0 2.3 %fusion.1 = bf16[64,8,384]{2,1,0:T(8,128)(2,1)} fusion(bf16[512,384]{1,0:T(8,128)(2,1)} %shard_map.163, s32[512]{0:T(512)S(1)} %convert_reduce_fusion), kind=kOutput, calls=%fused_computation.11 | convolution fusion | flops 201785344 | bytes 788480 | tf_op jit(solution)/shard_map/dot_general | solution.py:159
  61.3 5.9 %all-to-all-start.1 = ((bf16[64,8,384]{2,1,0:T(8,128)(2,1)}), bf16[64,8,384]{2,1,0:T(8,128)(2,1)S(1)}, u32[]{:S(2)}, u32[]{:S(2)}) async-start(bf16[64,8,384]{2,1,0:T(8,128)(2,1)} %fusion.1), calls=%async_computation.1 | async-start | bytes 786432 | tf_op jit(solution)/shard_map/all_to_all | solution.py:271
  68.6 0.7 copy.86
  69.3 0.7 copy.82
  69.9 2.1 %fusion.3 = f32[8,5,1,64]{3,2,1,0:T(1,128)} fusion(bf16[8,128,5,64]{1,3,0,2:T(8,128)(2,1)} %get-tuple-element.38, bf16[8,5,128,1]{2,0,1,3:T(8,128)(2,1)S(1)} %get-tuple-element.32), kind=kOutput, calls=%fused_computation.20 | convolution fusion | flops 655360 | bytes 675840 | tf_op jit(solution)/shard_map/rsj,rjsd->rsd/dot_general | solution.py:299
  72.1 9.6 %all-to-all-done.1 = bf16[64,8,384]{2,1,0:T(8,128)(2,1)S(1)} async-done(((bf16[64,8,384]{2,1,0:T(8,128)(2,1)}), bf16[64,8,384]{2,1,0:T(8,128)(2,1)S(1)}, u32[]{:S(2)}, u32[]{:S(2)}) %all-to-all-start.1) | async-done | bytes 393248 | tf_op jit(solution)/shard_map/all_to_all | solution.py:271
  82.3 0.8 fusion.17
  83.2 1.1 fusion
  84.3 1.4 %reduce_sum.109 = f32[8,5,64]{2,1,0:T(8,128)} reshape(f32[8,320]{1,0:T(8,128)} %fusion) | data formatting | bytes 20480 | tf_op jit(solution)/shard_map/reduce_sum | solution.py:280
  85.6 1.3 %multiply_add_fusion.1 = (f32[8,5]{1,0:T(8,128)}, f32[8,5]{1,0:T(8,128)}, f32[8,5]{1,0:T(8,128)}) fusion(f32[8,5]{1,0:T(8,128)} %copy.86, f32[8,5]{1,0:T(8,128)} %get-tuple-element.17, f32[8,5]{1,0:T(8,128)} %copy-done.7, f32[8,5]{1,0:T(8,128)S(1)} %copy.77, f32[8,5]{1,0:T(8,128)} %copy-done.8), kind=kLoop, calls=%fused_computation.85 | loop fusion | flops 360 | bytes 1280 | tf_op jit(solution)/shard_map/add | solution.py:308
  86.9 0.8 copy.87
  87.7 1.3 %copy.81 = f32[8,5]{0,1:T(8,128)} copy(f32[8,5]{1,0:T(8,128)} %get-tuple-element.16) | data formatting | bytes 320 | tf_op jit(solution)/shard_map/exp | solution.py:307
  89.0 1.3 %copy.79 = f32[8,5]{0,1:T(8,128)} copy(f32[8,5]{1,0:T(8,128)} %get-tuple-element.15) | data formatting | bytes 320 | tf_op jit(solution)/shard_map/exp | solution.py:306
  90.4 0.9 fusion.29
  91.3 0.7 reshape.227
  91.9 1.3 %convolution_convert_fusion.1 = bf16[8,1152]{1,0:T(8,128)(2,1)S(1)} fusion(bf16[8,320]{1,0:T(8,128)(2,1)} %reshape.227, bf16[320,1152]{1,0:T(8,128)(2,1)} %param.28), kind=kOutput, calls=%fused_computation.7 | convolution fusion | flops 5907456 | bytes 760832 | tf_op jit(solution)/shard_map/dot_general | solution.py:311
  93.9 2.4 %collective-permute-start.1 = (bf16[8,1152]{1,0:T(8,128)(2,1)S(1)}, bf16[8,1152]{1,0:T(8,128)(2,1)S(1)}, u32[]{:S(2)}, u32[]{:S(2)}) collective-permute-start(bf16[8,1152]{1,0:T(8,128)(2,1)S(1)} %convolution_convert_fusion.1), channel_id=1, source_target_pairs={{0,2},{1,3},{2,0},{3,1},{4,6},{5,7},{6,4},{7,5},{8,10},{9,11},{10,... | collective-permute-start | bytes 55304 | tf_op jit(solution)/shard_map/ppermute | solution.py:199
  96.3 1.8 %collective-permute-start = (bf16[8,1152]{1,0:T(8,128)(2,1)S(1)}, bf16[8,1152]{1,0:T(8,128)(2,1)S(1)}, u32[]{:S(2)}, u32[]{:S(2)}) collective-permute-start(bf16[8,1152]{1,0:T(8,128)(2,1)S(1)} %convolution_convert_fusion.1), channel_id=1, source_target_pairs={{0,1},{1,2},{2,3},{3,0},{4,5},{5,6},{6,7},{7,4},{8,9},{9,10},{10,1... | collective-permute-start | bytes 55304 | tf_op jit(solution)/shard_map/ppermute | solution.py:199
  98.1 1.0 collective-permute-done.1
  99.1 0.9 collective-permute-done
  100.1 0.9 fusion.12
  100.9 0.6 copy-done.4
  101.5 1.7 %fusion.39 = f32[8,768]{1,0:T(8,128)} fusion(bf16[1152,768]{1,0:T(8,128)(2,1)S(1)} %copy-done.1, bf16[8,1152]{1,0:T(8,128)(2,1)S(1)} %get-tuple-element.11, f32[1152]{0:T(1024)} %param.36, f32[8]{0:T(128)S(1)} %add_rsqrt_fusion), kind=kOutput, calls=%fused_computation.103 | convolution fusion | flops 14192640 | bytes 1817120 | tf_op jit(solution)/shard_map/dot_general | solution.py:317
  103.2 2.2 %convolution_convert_fusion = bf16[8,1152]{1,0:T(8,128)(2,1)S(1)} fusion(bf16[768,1152]{1,0:T(8,128)(2,1)S(1)} %copy-done, bf16[1152,768]{1,0:T(8,128)(2,1)} %param.38, f32[8,768]{1,0:T(8,128)} %fusion.39, bf16[8,1152]{1,0:T(8,128)(2,1)} %copy-done.4, f32[1152]{0:T(1024)S(1)} %copy-done.9, f32[8]{0:T(128)S(1)} %add_rsqrt_fusion), kind=kOutput, calls=%fused_computation.6 | convolution fusion | flops 28394496 | bytes 3605024 | tf_op jit(solution)/shard_map/dot_general | solution.py:320
  105.5 2.4 %collective-permute-start.5 = (bf16[8,1152]{1,0:T(8,128)(2,1)S(1)}, bf16[8,1152]{1,0:T(8,128)(2,1)S(1)}, u32[]{:S(2)}, u32[]{:S(2)}) collective-permute-start(bf16[8,1152]{1,0:T(8,128)(2,1)S(1)} %convolution_convert_fusion), channel_id=1, source_target_pairs={{0,3},{1,0},{2,1},{3,2},{4,7},{5,4},{6,5},{7,6},{8,11},{9,8},{10,9... | collective-permute-start | bytes 55304 | tf_op jit(solution)/shard_map/ppermute | solution.py:199
  107.8 0.9 collective-permute-start.4
  108.7 0.9 collective-permute-start.3
  109.6 3.5 %collective-permute-done.4 = bf16[8,1152]{1,0:T(8,128)(2,1)S(1)} collective-permute-done((bf16[8,1152]{1,0:T(8,128)(2,1)S(1)}, bf16[8,1152]{1,0:T(8,128)(2,1)S(1)}, u32[]{:S(2)}, u32[]{:S(2)}) %collective-permute-start.4) | collective-permute-done | bytes 18464 | tf_op jit(solution)/shard_map/ppermute | solution.py:199
  113.1 0.6 fusion.15
  (82 shorter events, 8.4 us)
Async XLA Ops:
  0.0 103.2 %copy-start = (bf16[768,1152]{1,0:T(8,128)(2,1)S(1)}, bf16[768,1152]{1,0:T(8,128)(2,1)}, u32[]{:S(2)}) copy-start(bf16[768,1152]{1,0:T(8,128)(2,1)} %param.39) | copy-start | bytes 5308420
  0.0 4.7 %copy-start.10 = (s32[512]{0:T(512)S(1)}, s32[512]{0:T(512)}, u32[]{:S(2)}) copy-start(s32[512]{0:T(512)} %param.33) | copy-start | bytes 6148
  0.0 4.8 %copy-start.12 = (s32[8]{0:T(128)S(1)}, s32[8]{0:T(128)}, u32[]{:S(2)}) copy-start(s32[8]{0:T(128)} %param.34) | copy-start | bytes 100
  0.6 28.0 %copy-start.11 = (pred[5]{0:T(512)(128)(4,1)}, pred[5]{0:T(512)(128)(4,1)S(1)}, u32[]{:S(2)}) copy-start(pred[5]{0:T(512)(128)(4,1)S(1)} %get-tuple-element.39) | copy-start | bytes 19
  7.6 29.7 %all-to-all-start = ((bf16[64,8,384]{2,1,0:T(8,128)(2,1)}), bf16[64,8,384]{2,1,0:T(8,128)(2,1)}, u32[]{:S(2)}, u32[]{:S(2)}) async-start(bf16[64,8,384]{2,1,0:T(8,128)(2,1)} %broadcast_in_dim.116), calls=%async_computation | async-start | bytes 786432 | tf_op jit(solution)/shard_map/all_to_all | solution.py:258
  58.9 8.3 %copy-start.2 = (bf16[1152,384]{1,0:T(8,128)(2,1)S(1)}, bf16[1152,384]{1,0:T(8,128)(2,1)}, u32[]{:S(2)}) copy-start(bf16[1152,384]{1,0:T(8,128)(2,1)} %param.27) | copy-start | bytes 2654212
  58.9 8.3 %copy-start.3 = (bf16[8,1152]{1,0:T(8,128)(2,1)S(1)}, bf16[8,1152]{1,0:T(8,128)(2,1)}, u32[]{:S(2)}) copy-start(bf16[8,1152]{1,0:T(8,128)(2,1)} %param.23) | copy-start | bytes 55300
  58.9 8.3 %copy-start.6 = (f32[1152]{0:T(1024)S(1)}, f32[1152]{0:T(1024)}, u32[]{:S(2)}) copy-start(f32[1152]{0:T(1024)} %param.24) | copy-start | bytes 13828
  61.3 20.4 %all-to-all-start.1 = ((bf16[64,8,384]{2,1,0:T(8,128)(2,1)}), bf16[64,8,384]{2,1,0:T(8,128)(2,1)S(1)}, u32[]{:S(2)}, u32[]{:S(2)}) async-start(bf16[64,8,384]{2,1,0:T(8,128)(2,1)} %fusion.1), calls=%async_computation.1 | async-start | bytes 786432 | tf_op jit(solution)/shard_map/all_to_all | solution.py:271
  67.2 0.6 copy-start.7
  82.3 0.8 copy-start.8
  83.2 18.4 %copy-start.1 = (bf16[1152,768]{1,0:T(8,128)(2,1)S(1)}, bf16[1152,768]{1,0:T(8,128)(2,1)}, u32[]{:S(2)}) copy-start(bf16[1152,768]{1,0:T(8,128)(2,1)} %param.37) | copy-start | bytes 5308420
  91.9 11.3 %copy-start.9 = (f32[1152]{0:T(1024)S(1)}, f32[1152]{0:T(1024)}, u32[]{:S(2)}) copy-start(f32[1152]{0:T(1024)} %param.36) | copy-start | bytes 13828
  93.3 4.8 %collective-permute-start.2 = (bf16[8,1152]{1,0:T(8,128)(2,1)S(1)}, bf16[8,1152]{1,0:T(8,128)(2,1)S(1)}, u32[]{:S(2)}, u32[]{:S(2)}) collective-permute-start(bf16[8,1152]{1,0:T(8,128)(2,1)S(1)} %convolution_convert_fusion.1), channel_id=1, source_target_pairs={{0,3},{1,0},{2,1},{3,2},{4,7},{5,4},{6,5},{7,6},{8,11},{9,8},{10,9... | collective-permute-start | bytes 55304 | tf_op jit(solution)/shard_map/ppermute | solution.py:199
  93.9 5.3 %collective-permute-start.1 = (bf16[8,1152]{1,0:T(8,128)(2,1)S(1)}, bf16[8,1152]{1,0:T(8,128)(2,1)S(1)}, u32[]{:S(2)}, u32[]{:S(2)}) collective-permute-start(bf16[8,1152]{1,0:T(8,128)(2,1)S(1)} %convolution_convert_fusion.1), channel_id=1, source_target_pairs={{0,2},{1,3},{2,0},{3,1},{4,6},{5,7},{6,4},{7,5},{8,10},{9,11},{10,... | collective-permute-start | bytes 55304 | tf_op jit(solution)/shard_map/ppermute | solution.py:199
  96.3 3.8 %collective-permute-start = (bf16[8,1152]{1,0:T(8,128)(2,1)S(1)}, bf16[8,1152]{1,0:T(8,128)(2,1)S(1)}, u32[]{:S(2)}, u32[]{:S(2)}) collective-permute-start(bf16[8,1152]{1,0:T(8,128)(2,1)S(1)} %convolution_convert_fusion.1), channel_id=1, source_target_pairs={{0,1},{1,2},{2,3},{3,0},{4,5},{5,6},{6,7},{7,4},{8,9},{9,10},{10,1... | collective-permute-start | bytes 55304 | tf_op jit(solution)/shard_map/ppermute | solution.py:199
  100.9 0.6 copy-start.4
  103.2 9.9 %copy-start.5 = (bf16[8,1152]{1,0:T(8,128)(2,1)S(1)}, bf16[8,1152]{1,0:T(8,128)(2,1)}, u32[]{:S(2)}) copy-start(bf16[8,1152]{1,0:T(8,128)(2,1)} %copy-done.4) | copy-start | bytes 55300
  105.5 4.2 %collective-permute-start.5 = (bf16[8,1152]{1,0:T(8,128)(2,1)S(1)}, bf16[8,1152]{1,0:T(8,128)(2,1)S(1)}, u32[]{:S(2)}, u32[]{:S(2)}) collective-permute-start(bf16[8,1152]{1,0:T(8,128)(2,1)S(1)} %convolution_convert_fusion), channel_id=1, source_target_pairs={{0,3},{1,0},{2,1},{3,2},{4,7},{5,4},{6,5},{7,6},{8,11},{9,8},{10,9... | collective-permute-start | bytes 55304 | tf_op jit(solution)/shard_map/ppermute | solution.py:199
  107.8 5.3 %collective-permute-start.4 = (bf16[8,1152]{1,0:T(8,128)(2,1)S(1)}, bf16[8,1152]{1,0:T(8,128)(2,1)S(1)}, u32[]{:S(2)}, u32[]{:S(2)}) collective-permute-start(bf16[8,1152]{1,0:T(8,128)(2,1)S(1)} %convolution_convert_fusion), channel_id=1, source_target_pairs={{0,2},{1,3},{2,0},{3,1},{4,6},{5,7},{6,4},{7,5},{8,10},{9,11},{10,... | collective-permute-start | bytes 55304 | tf_op jit(solution)/shard_map/ppermute | solution.py:199
  108.7 4.4 %collective-permute-start.3 = (bf16[8,1152]{1,0:T(8,128)(2,1)S(1)}, bf16[8,1152]{1,0:T(8,128)(2,1)S(1)}, u32[]{:S(2)}, u32[]{:S(2)}) collective-permute-start(bf16[8,1152]{1,0:T(8,128)(2,1)S(1)} %convolution_convert_fusion), channel_id=1, source_target_pairs={{0,1},{1,2},{2,3},{3,0},{4,5},{5,6},{6,7},{7,4},{8,9},{9,10},{10,1... | collective-permute-start | bytes 55304 | tf_op jit(solution)/shard_map/ppermute | solution.py:199

commit v8 on v7

--- a/solution.py
+++ b/solution.py
@@ -1,4 +1,7 @@
+import functools
+
 import jax
+import numpy as np
 import jax.numpy as jnp
 from jax import lax
 from jax.experimental import pallas as pl
@@ -24,7 +27,17 @@
     return parts
 
 
-def prefix_kernel(tile_of, group_at, valid, limit, kv, perm_ref, sg_ref, q_ref, k_ref, v_ref, o_ref):
+def pair_window(tp_count, slot_count, width):
+    spans = []
+    for device_tp in range(tp_count):
+        per_device = HEADS // tp_count
+        start_head = per_device * device_tp + min(device_tp, HEADS % tp_count)
+        heads = np.minimum(start_head + np.arange(slot_count), HEADS - 1) // (HEADS // KV_HEADS)
+        spans.append(heads.max() // 2 - heads.min() // 2 + 1)
+    return int(min(max(spans), width // 128))
+
+
+def prefix_kernel(tile_of, group_at, valid, limit, kv, perm_ref, sg_ref, q_ref, k_ref, v_ref, o_ref, *, window):
     step = pl.program_id(0)
     tile = tile_of[step]
     first = jnp.logical_or(step == 0, tile_of[jnp.maximum(step - 1, 0)] != tile)
@@ -50,7 +63,12 @@
         row_live = sg_ref[...] == group
         lane = lax.broadcasted_iota(jnp.int32, (rows, lanes), 1)
         upper = lane >= HD
-        tile_total = width // lanes
+        tile_total = window
+        base = kv[0] // 2
+        for slot in range(1, slot_count):
+            base = jnp.minimum(base, kv[slot] // 2)
+        base = jnp.minimum(base, width // lanes - window)
+        start = pl.multiple_of(base * lanes, lanes)
         padded = []
         for slot in range(slot_count):
             head = kv[slot]
@@ -61,12 +79,12 @@
             block = jnp.where(odd == half, block, pltpu.roll(block, HD, 1))
             padded.append(
                 jnp.concatenate(
-                    [jnp.where(head // 2 == j, block, 0.0) for j in range(tile_total)], axis=1
+                    [jnp.where(head // 2 - base == j, block, 0.0) for j in range(tile_total)], axis=1
                 ).astype(jnp.bfloat16)
             )
         padded = jnp.concatenate(padded, axis=0)
         scores = lax.dot_general(
-            padded, k_ref[0], (((1,), (1,)), ((), ())), preferred_element_type=jnp.float32
+            padded, k_ref[0, :, pl.ds(start, window * lanes)], (((1,), (1,)), ((), ())), preferred_element_type=jnp.float32
         ) * (HD ** (-0.5))
         all_live = jnp.concatenate([row_live] * slot_count, axis=0)
         spots = lax.broadcasted_iota(jnp.int32, scores.shape, 1)
@@ -74,7 +92,9 @@
         top = jnp.max(jnp.where(live, scores, NEG_FILL), axis=1, keepdims=True)
         weights = jnp.where(live, jnp.exp(scores - top), 0.0)
         total = jnp.sum(weights, axis=1, keepdims=True)
-        mixed = jnp.dot(weights.astype(jnp.bfloat16), v_ref[0], preferred_element_type=jnp.float32)
+        mixed = jnp.dot(
+            weights.astype(jnp.bfloat16), v_ref[0, :, pl.ds(start, window * lanes)], preferred_element_type=jnp.float32
+        )
         pieces = []
         for slot in range(slot_count):
             head = kv[slot]
@@ -83,7 +103,7 @@
             mine = mixed[slot * rows : (slot + 1) * rows]
             chosen = mine[:, 0:lanes]
             for j in range(1, tile_total):
-                chosen = jnp.where(head // 2 == j, mine[:, j * lanes : (j + 1) * lanes], chosen)
+                chosen = jnp.where(head // 2 - base == j, mine[:, j * lanes : (j + 1) * lanes], chosen)
             pieces.append(jnp.where(odd == half, chosen, pltpu.roll(chosen, HD, 1)))
         if slot_count % 2:
             pieces.append(jnp.zeros((rows, lanes), jnp.float32))
@@ -97,7 +117,7 @@
         o_ref[...] = jnp.where(row_live, jnp.concatenate(out, axis=1).astype(o_ref.dtype), o_ref[...])
 
 
-def prefix_partials(every_query, group_of, prefix_len, seq_index, prefix_keys, prefix_values, kv_ids):
+def prefix_partials(every_query, group_of, prefix_len, seq_index, prefix_keys, prefix_values, kv_ids, tp_count):
     request_count, width = every_query.shape
     group_count, prefix_span, _ = prefix_keys.shape
     tile_count = request_count // TILE
@@ -133,8 +153,9 @@
     )
     lanes = 128
     flops = visit_count * (2 * TILE * request_count * width + slot_count * 4 * TILE * width * prefix_span)
+    window = pair_window(tp_count, slot_count, width)
     out = pl.pallas_call(
-        prefix_kernel,
+        functools.partial(prefix_kernel, window=window),
         grid_spec=grid_spec,
         out_shape=jax.ShapeDtypeStruct((request_count, width), jnp.bfloat16),
         compiler_params=pltpu.CompilerParams(dimension_semantics=("arbitrary",)),
@@ -265,7 +286,7 @@
     every_query = every_query.reshape(-1, query_width)
     score_scale = HD ** (-0.5)
     payload = prefix_partials(
-        every_query, group_of, prefix_len, seq_index, prefix_keys, prefix_values, kv_ids
+        every_query, group_of, prefix_len, seq_index, prefix_keys, prefix_values, kv_ids, lax.axis_size("tp")
     )
     payload = payload.reshape(seq_count, row_count, query_width)
     gathered = lax.all_to_all(payload, "seq", 0, 0, tiled=True).astype(jnp.float32)

time: 114 us -> 113 us (level)
  Pallas kernels: 21.6 us -> 18.8 us
    pallas_call x1, Pallas kernels: 21.6 us -> 18.8 us  [prefix_partials(): pl.pallas_call(functools.partial(prefix_kernel, window=window), grid_spec...]
  transfers between devices with their start and end apart: 8 -> 8, of which waited for: 4 -> 4; matrix products, arithmetic and copies ran while one was open for 19% -> 20% of each run, Pallas kernels for 0% -> 0%
where the time goes in v8:
time: 113 us; the launch traced here: 112 us
  starting transfers between devices  28 us (25%)
  local copies, waits for them, and re-layouts  21.8 us (19%)
  Pallas kernels  18.8 us (17%)
  waiting for transfers between devices  15 us (13%)
  other arithmetic  14.8 us (13%)
  matrix products  13.1 us (12%)
    pallas_call x1, Pallas kernels, prefix_partials(): pl.pallas_call(functools.partial(prefix_kernel, window=window), grid_spec...  18.8 us
    all_to_all x1, starting transfers between devices, on_device(): lax.all_to_all(jnp.broadcast_to(own_query, (seq_count, row_count, query_w...  12.3 us
    all_to_all x1, waiting for transfers between devices, on_device(): lax.all_to_all(payload, 'seq', 0, 0, tiled=True).astype(jnp.float32)  9.58 us
    ppermute x6, starting transfers between devices, tp_sum(): lax.ppermute(sent, 'tp', [(j, (j + shift) % count) for j in range(count)])  9 us
    all_to_all x1, starting transfers between devices, on_device(): lax.all_to_all(payload, 'seq', 0, 0, tiled=True).astype(jnp.float32)  6.71 us
    ppermute x6, waiting for transfers between devices, tp_sum(): lax.ppermute(sent, 'tp', [(j, (j + shift) % count) for j in range(count)])  5.4 us
    unnamed x28, local copies, waits for them, and re-layouts  4.68 us
    dot_general x1, matrix products, prefix_partials(): jnp.dot(unsort, out, preferred_element_type=jnp.float32)  2.32 us
  transfers between devices with their start and end apart: 8, of which 4 were waited for; matrix products, arithmetic and copies ran while one was open for 20% of the time, Pallas kernels for 0%

profile of v8, /device:TPU:2, one launch (start us, length us, event | category | flops | bytes accessed | tf_op | source)
XLA Modules:
  0.0 111.8 jit_solution(2169220819532939647)
XLA Ops:
  0.6 0.8 fusion.8
  1.5 1.4 %fusion.45 = f32[8,384]{1,0:T(8,128)S(1)} fusion(bf16[1152,384]{1,0:T(8,128)(2,1)} %param.26, bf16[8,1152]{1,0:T(8,128)(2,1)} %param.23, f32[1152]{0:T(1024)} %param.24, f32[8]{0:T(128)S(1)} %add_rsqrt_fusion.1), kind=kOutput, calls=%fused_computation.117 | convolution fusion | flops 7114752 | bytes 920096 | tf_op jit(solution)/shard_map/dot_general | solution.py:255
  3.1 1.4 %fusion.47 = f32[8,320]{1,0:T(8,128)S(1)} fusion(bf16[1152,320]{0,1:T(8,128)(2,1)} %param.25, bf16[8,1152]{1,0:T(8,128)(2,1)} %param.23, f32[1152]{0:T(1024)} %param.24, f32[8]{0:T(128)S(1)} %add_rsqrt_fusion.1), kind=kOutput, calls=%fused_computation.118 | convolution fusion | flops 5935104 | bytes 770592 | tf_op jit(solution)/shard_map/dot_general | solution.py:252
  5.0 0.8 add_convert_fusion.1
  6.8 0.8 broadcast_in_dim.116
  7.6 12.3 %all-to-all-start = ((bf16[64,8,384]{2,1,0:T(8,128)(2,1)}), bf16[64,8,384]{2,1,0:T(8,128)(2,1)}, u32[]{:S(2)}, u32[]{:S(2)}) async-start(bf16[64,8,384]{2,1,0:T(8,128)(2,1)} %broadcast_in_dim.116), calls=%async_computation | async-start | bytes 786432 | tf_op jit(solution)/shard_map/all_to_all | solution.py:279
  20.8 0.6 slice.49
  22.2 1.5 %copy.74 = bf16[8,128,384]{1,2,0:T(8,128)(2,1)S(1)} copy(bf16[8,128,384]{2,1,0:T(8,128)(2,1)} %param.31) | data formatting | bytes 1572864 | tf_op args[8]
  23.7 0.7 gather_fusion.2
  24.4 2.3 %copy.85 = bf16[8,128,384]{1,2,0:T(8,128)(2,1)} copy(bf16[8,128,384]{2,1,0:T(8,128)(2,1)} %param.32) | data formatting | bytes 1572864 | tf_op args[9]
  26.7 1.8 %gather_fusion.5 = bf16[5,8,128,64]{2,3,1,0:T(8,128)(2,1)S(1)} fusion(bf16[8,128,6,64]{1,3,2,0:T(8,128)(2,1)} %bitcast.61, s32[1024]{0:T(1024)S(1)} %pad_clamp_fusion), kind=kCustom, calls=%fused_computation.4.clone | custom fusion | bytes 1310740 | tf_op jit(solution)/shard_map/jit(_take)/gather | solution.py:303
  28.7 1.0 select_bitcast_fusion.1
  30.2 0.7 gather_fusion
  30.9 0.7 gather_fusion.1
  31.6 0.9 copy.71.perm_ref
  32.4 0.9 copy.72.sg_ref
  33.8 1.2 %compare_convert_fusion.1.valid = s32[15]{0:T(128)} fusion(s32[]{:T(128)} %bitcast.2), kind=kLoop, calls=%fused_computation.101 | loop fusion | flops 30 | bytes 64 | tf_op jit(solution)/shard_map/convert_element_type | solution.py:138
  35.5 1.8 %compare_select_fusion.2 = (s32[15]{0:T(128)}, s32[15]{0:T(128)}) fusion(s32[15]{0:T(128)S(1)} %gather_fusion.1, s32[15]{0:T(128)S(1)} %gather_fusion, s32[]{:T(128)} %bitcast.3, s32[]{:T(128)} %bitcast.2, s32[15]{0:T(128)S(1)} %convert_reduce_fusion.1), kind=kLoop, calls=%fused_computation.100 | loop fusion | flops 225 | bytes 308 | tf_op jit(solution)/shard_map/jit(_where)/select_n | solution.py:139
  37.4 18.8 %shard_map.163 = bf16[512,384]{1,0:T(8,128)(2,1)} custom-call(s32[15]{0:T(128)} %get-tuple-element.36.tile_of, s32[15]{0:T(128)} %get-tuple-element.35.group_at, s32[15]{0:T(128)} %compare_convert_fusion.1.valid, s32[8]{0:T(128)} %subtract_clamp_fusion.limit, s32[5]{0:T(128)} %and_select_fusion.kv, s32[512,1]{1,0:T(8,128)} %copy.71.perm_ref, ...), custom_call_target="tpu_custom_call" | custom-call | flops 4152360960 | bytes 12976128 | tf_op jit(solution)/shard_map/pallas_call | solution.py:157
  56.2 2.3 %fusion.1 = bf16[64,8,384]{2,1,0:T(8,128)(2,1)} fusion(bf16[512,384]{1,0:T(8,128)(2,1)} %shard_map.163, s32[512]{0:T(512)S(1)} %convert_reduce_fusion), kind=kOutput, calls=%fused_computation.11 | convolution fusion | flops 201785344 | bytes 788480 | tf_op jit(solution)/shard_map/dot_general | solution.py:180
  58.5 6.7 %all-to-all-start.1 = ((bf16[64,8,384]{2,1,0:T(8,128)(2,1)}), bf16[64,8,384]{2,1,0:T(8,128)(2,1)S(1)}, u32[]{:S(2)}, u32[]{:S(2)}) async-start(bf16[64,8,384]{2,1,0:T(8,128)(2,1)} %fusion.1), calls=%async_computation.1 | async-start | bytes 786432 | tf_op jit(solution)/shard_map/all_to_all | solution.py:292
  66.7 0.7 copy.86
  67.4 0.7 copy.82
  68.0 2.1 %fusion.3 = f32[8,5,1,64]{3,2,1,0:T(1,128)} fusion(bf16[8,128,5,64]{1,3,0,2:T(8,128)(2,1)} %get-tuple-element.38, bf16[8,5,128,1]{2,0,1,3:T(8,128)(2,1)S(1)} %get-tuple-element.32), kind=kOutput, calls=%fused_computation.20 | convolution fusion | flops 655360 | bytes 675840 | tf_op jit(solution)/shard_map/rsj,rjsd->rsd/dot_general | solution.py:320
  70.2 9.6 %all-to-all-done.1 = bf16[64,8,384]{2,1,0:T(8,128)(2,1)S(1)} async-done(((bf16[64,8,384]{2,1,0:T(8,128)(2,1)}), bf16[64,8,384]{2,1,0:T(8,128)(2,1)S(1)}, u32[]{:S(2)}, u32[]{:S(2)}) %all-to-all-start.1) | async-done | bytes 393248 | tf_op jit(solution)/shard_map/all_to_all | solution.py:292
  80.4 0.8 fusion.17
  81.3 1.1 fusion
  82.4 1.4 %reduce_sum.109 = f32[8,5,64]{2,1,0:T(8,128)} reshape(f32[8,320]{1,0:T(8,128)} %fusion) | data formatting | bytes 20480 | tf_op jit(solution)/shard_map/reduce_sum | solution.py:301
  83.7 1.3 %multiply_add_fusion.1 = (f32[8,5]{1,0:T(8,128)}, f32[8,5]{1,0:T(8,128)}, f32[8,5]{1,0:T(8,128)}) fusion(f32[8,5]{1,0:T(8,128)} %copy.86, f32[8,5]{1,0:T(8,128)} %get-tuple-element.17, f32[8,5]{1,0:T(8,128)} %copy-done.7, f32[8,5]{1,0:T(8,128)S(1)} %copy.77, f32[8,5]{1,0:T(8,128)} %copy-done.8), kind=kLoop, calls=%fused_computation.85 | loop fusion | flops 360 | bytes 1280 | tf_op jit(solution)/shard_map/add | solution.py:329
  85.0 0.8 copy.87
  85.8 1.3 %copy.81 = f32[8,5]{0,1:T(8,128)} copy(f32[8,5]{1,0:T(8,128)} %get-tuple-element.16) | data formatting | bytes 320 | tf_op jit(solution)/shard_map/exp | solution.py:328
  87.1 1.3 %copy.79 = f32[8,5]{0,1:T(8,128)} copy(f32[8,5]{1,0:T(8,128)} %get-tuple-element.15) | data formatting | bytes 320 | tf_op jit(solution)/shard_map/exp | solution.py:327
  88.5 0.9 fusion.29
  89.4 0.7 reshape.227
  90.0 1.3 %convolution_convert_fusion.1 = bf16[8,1152]{1,0:T(8,128)(2,1)S(1)} fusion(bf16[8,320]{1,0:T(8,128)(2,1)} %reshape.227, bf16[320,1152]{1,0:T(8,128)(2,1)} %param.28), kind=kOutput, calls=%fused_computation.7 | convolution fusion | flops 5907456 | bytes 760832 | tf_op jit(solution)/shard_map/dot_general | solution.py:332
  91.4 0.6 collective-permute-start.2
  92.0 2.4 %collective-permute-start.1 = (bf16[8,1152]{1,0:T(8,128)(2,1)S(1)}, bf16[8,1152]{1,0:T(8,128)(2,1)S(1)}, u32[]{:S(2)}, u32[]{:S(2)}) collective-permute-start(bf16[8,1152]{1,0:T(8,128)(2,1)S(1)} %convolution_convert_fusion.1), channel_id=1, source_target_pairs={{0,2},{1,3},{2,0},{3,1},{4,6},{5,7},{6,4},{7,5},{8,10},{9,11},{10,... | collective-permute-start | bytes 55304 | tf_op jit(solution)/shard_map/ppermute | solution.py:220
  94.4 1.8 %collective-permute-start = (bf16[8,1152]{1,0:T(8,128)(2,1)S(1)}, bf16[8,1152]{1,0:T(8,128)(2,1)S(1)}, u32[]{:S(2)}, u32[]{:S(2)}) collective-permute-start(bf16[8,1152]{1,0:T(8,128)(2,1)S(1)} %convolution_convert_fusion.1), channel_id=1, source_target_pairs={{0,1},{1,2},{2,3},{3,0},{4,5},{5,6},{6,7},{7,4},{8,9},{9,10},{10,1... | collective-permute-start | bytes 55304 | tf_op jit(solution)/shard_map/ppermute | solution.py:220
  96.2 1.0 collective-permute-done.1
  97.3 0.9 collective-permute-done
  98.2 0.9 fusion.12
  99.7 1.7 %fusion.39 = f32[8,768]{1,0:T(8,128)} fusion(bf16[1152,768]{1,0:T(8,128)(2,1)S(1)} %copy-done.1, bf16[8,1152]{1,0:T(8,128)(2,1)S(1)} %get-tuple-element.11, f32[1152]{0:T(1024)} %param.36, f32[8]{0:T(128)S(1)} %add_rsqrt_fusion), kind=kOutput, calls=%fused_computation.103 | convolution fusion | flops 14192640 | bytes 1817120 | tf_op jit(solution)/shard_map/dot_general | solution.py:338
  101.3 2.2 %convolution_convert_fusion = bf16[8,1152]{1,0:T(8,128)(2,1)S(1)} fusion(bf16[768,1152]{1,0:T(8,128)(2,1)S(1)} %copy-done, bf16[1152,768]{1,0:T(8,128)(2,1)} %param.38, f32[8,768]{1,0:T(8,128)} %fusion.39, bf16[8,1152]{1,0:T(8,128)(2,1)} %copy-done.4, f32[1152]{0:T(1024)S(1)} %copy-done.9, f32[8]{0:T(128)S(1)} %add_rsqrt_fusion), kind=kOutput, calls=%fused_computation.6 | convolution fusion | flops 28394496 | bytes 3605024 | tf_op jit(solution)/shard_map/dot_general | solution.py:341
  103.6 2.3 %collective-permute-start.5 = (bf16[8,1152]{1,0:T(8,128)(2,1)S(1)}, bf16[8,1152]{1,0:T(8,128)(2,1)S(1)}, u32[]{:S(2)}, u32[]{:S(2)}) collective-permute-start(bf16[8,1152]{1,0:T(8,128)(2,1)S(1)} %convolution_convert_fusion), channel_id=1, source_target_pairs={{0,3},{1,0},{2,1},{3,2},{4,7},{5,4},{6,5},{7,6},{8,11},{9,8},{10,9... | collective-permute-start | bytes 55304 | tf_op jit(solution)/shard_map/ppermute | solution.py:220
  105.9 0.9 collective-permute-start.4
  106.9 0.9 collective-permute-start.3
  107.7 3.5 %collective-permute-done.4 = bf16[8,1152]{1,0:T(8,128)(2,1)S(1)} collective-permute-done((bf16[8,1152]{1,0:T(8,128)(2,1)S(1)}, bf16[8,1152]{1,0:T(8,128)(2,1)S(1)}, u32[]{:S(2)}, u32[]{:S(2)}) %collective-permute-start.4) | collective-permute-done | bytes 18464 | tf_op jit(solution)/shard_map/ppermute | solution.py:220
  111.2 0.6 fusion.15
  (82 shorter events, 8.4 us)
Async XLA Ops:
  0.0 101.3 %copy-start = (bf16[768,1152]{1,0:T(8,128)(2,1)S(1)}, bf16[768,1152]{1,0:T(8,128)(2,1)}, u32[]{:S(2)}) copy-start(bf16[768,1152]{1,0:T(8,128)(2,1)} %param.39) | copy-start | bytes 5308420
  0.0 4.7 %copy-start.10 = (s32[512]{0:T(512)S(1)}, s32[512]{0:T(512)}, u32[]{:S(2)}) copy-start(s32[512]{0:T(512)} %param.33) | copy-start | bytes 6148
  0.0 4.8 %copy-start.12 = (s32[8]{0:T(128)S(1)}, s32[8]{0:T(128)}, u32[]{:S(2)}) copy-start(s32[8]{0:T(128)} %param.34) | copy-start | bytes 100
  0.6 28.0 %copy-start.11 = (pred[5]{0:T(512)(128)(4,1)}, pred[5]{0:T(512)(128)(4,1)S(1)}, u32[]{:S(2)}) copy-start(pred[5]{0:T(512)(128)(4,1)S(1)} %get-tuple-element.39) | copy-start | bytes 19
  7.6 29.7 %all-to-all-start = ((bf16[64,8,384]{2,1,0:T(8,128)(2,1)}), bf16[64,8,384]{2,1,0:T(8,128)(2,1)}, u32[]{:S(2)}, u32[]{:S(2)}) async-start(bf16[64,8,384]{2,1,0:T(8,128)(2,1)} %broadcast_in_dim.116), calls=%async_computation | async-start | bytes 786432 | tf_op jit(solution)/shard_map/all_to_all | solution.py:279
  56.2 9.2 %copy-start.2 = (bf16[1152,384]{1,0:T(8,128)(2,1)S(1)}, bf16[1152,384]{1,0:T(8,128)(2,1)}, u32[]{:S(2)}) copy-start(bf16[1152,384]{1,0:T(8,128)(2,1)} %param.27) | copy-start | bytes 2654212
  56.2 9.2 %copy-start.3 = (bf16[8,1152]{1,0:T(8,128)(2,1)S(1)}, bf16[8,1152]{1,0:T(8,128)(2,1)}, u32[]{:S(2)}) copy-start(bf16[8,1152]{1,0:T(8,128)(2,1)} %param.23) | copy-start | bytes 55300
  56.2 9.2 %copy-start.6 = (f32[1152]{0:T(1024)S(1)}, f32[1152]{0:T(1024)}, u32[]{:S(2)}) copy-start(f32[1152]{0:T(1024)} %param.24) | copy-start | bytes 13828
  58.5 21.2 %all-to-all-start.1 = ((bf16[64,8,384]{2,1,0:T(8,128)(2,1)}), bf16[64,8,384]{2,1,0:T(8,128)(2,1)S(1)}, u32[]{:S(2)}, u32[]{:S(2)}) async-start(bf16[64,8,384]{2,1,0:T(8,128)(2,1)} %fusion.1), calls=%async_computation.1 | async-start | bytes 786432 | tf_op jit(solution)/shard_map/all_to_all | solution.py:292
  65.3 0.6 copy-start.7
  80.4 0.8 copy-start.8
  81.3 18.4 %copy-start.1 = (bf16[1152,768]{1,0:T(8,128)(2,1)S(1)}, bf16[1152,768]{1,0:T(8,128)(2,1)}, u32[]{:S(2)}) copy-start(bf16[1152,768]{1,0:T(8,128)(2,1)} %param.37) | copy-start | bytes 5308420
  90.0 11.3 %copy-start.9 = (f32[1152]{0:T(1024)S(1)}, f32[1152]{0:T(1024)}, u32[]{:S(2)}) copy-start(f32[1152]{0:T(1024)} %param.36) | copy-start | bytes 13828
  91.4 4.8 %collective-permute-start.2 = (bf16[8,1152]{1,0:T(8,128)(2,1)S(1)}, bf16[8,1152]{1,0:T(8,128)(2,1)S(1)}, u32[]{:S(2)}, u32[]{:S(2)}) collective-permute-start(bf16[8,1152]{1,0:T(8,128)(2,1)S(1)} %convolution_convert_fusion.1), channel_id=1, source_target_pairs={{0,3},{1,0},{2,1},{3,2},{4,7},{5,4},{6,5},{7,6},{8,11},{9,8},{10,9... | collective-permute-start | bytes 55304 | tf_op jit(solution)/shard_map/ppermute | solution.py:220
  92.0 5.3 %collective-permute-start.1 = (bf16[8,1152]{1,0:T(8,128)(2,1)S(1)}, bf16[8,1152]{1,0:T(8,128)(2,1)S(1)}, u32[]{:S(2)}, u32[]{:S(2)}) collective-permute-start(bf16[8,1152]{1,0:T(8,128)(2,1)S(1)} %convolution_convert_fusion.1), channel_id=1, source_target_pairs={{0,2},{1,3},{2,0},{3,1},{4,6},{5,7},{6,4},{7,5},{8,10},{9,11},{10,... | collective-permute-start | bytes 55304 | tf_op jit(solution)/shard_map/ppermute | solution.py:220
  94.4 3.8 %collective-permute-start = (bf16[8,1152]{1,0:T(8,128)(2,1)S(1)}, bf16[8,1152]{1,0:T(8,128)(2,1)S(1)}, u32[]{:S(2)}, u32[]{:S(2)}) collective-permute-start(bf16[8,1152]{1,0:T(8,128)(2,1)S(1)} %convolution_convert_fusion.1), channel_id=1, source_target_pairs={{0,1},{1,2},{2,3},{3,0},{4,5},{5,6},{6,7},{7,4},{8,9},{9,10},{10,1... | collective-permute-start | bytes 55304 | tf_op jit(solution)/shard_map/ppermute | solution.py:220
  99.0 0.6 copy-start.4
  101.3 9.9 %copy-start.5 = (bf16[8,1152]{1,0:T(8,128)(2,1)S(1)}, bf16[8,1152]{1,0:T(8,128)(2,1)}, u32[]{:S(2)}) copy-start(bf16[8,1152]{1,0:T(8,128)(2,1)} %copy-done.4) | copy-start | bytes 55300
  103.6 4.2 %collective-permute-start.5 = (bf16[8,1152]{1,0:T(8,128)(2,1)S(1)}, bf16[8,1152]{1,0:T(8,128)(2,1)S(1)}, u32[]{:S(2)}, u32[]{:S(2)}) collective-permute-start(bf16[8,1152]{1,0:T(8,128)(2,1)S(1)} %convolution_convert_fusion), channel_id=1, source_target_pairs={{0,3},{1,0},{2,1},{3,2},{4,7},{5,4},{6,5},{7,6},{8,11},{9,8},{10,9... | collective-permute-start | bytes 55304 | tf_op jit(solution)/shard_map/ppermute | solution.py:220
  105.9 5.3 %collective-permute-start.4 = (bf16[8,1152]{1,0:T(8,128)(2,1)S(1)}, bf16[8,1152]{1,0:T(8,128)(2,1)S(1)}, u32[]{:S(2)}, u32[]{:S(2)}) collective-permute-start(bf16[8,1152]{1,0:T(8,128)(2,1)S(1)} %convolution_convert_fusion), channel_id=1, source_target_pairs={{0,2},{1,3},{2,0},{3,1},{4,6},{5,7},{6,4},{7,5},{8,10},{9,11},{10,... | collective-permute-start | bytes 55304 | tf_op jit(solution)/shard_map/ppermute | solution.py:220
  106.9 4.3 %collective-permute-start.3 = (bf16[8,1152]{1,0:T(8,128)(2,1)S(1)}, bf16[8,1152]{1,0:T(8,128)(2,1)S(1)}, u32[]{:S(2)}, u32[]{:S(2)}) collective-permute-start(bf16[8,1152]{1,0:T(8,128)(2,1)S(1)} %convolution_convert_fusion), channel_id=1, source_target_pairs={{0,1},{1,2},{2,3},{3,0},{4,5},{5,6},{6,7},{7,4},{8,9},{9,10},{10,1... | collective-permute-start | bytes 55304 | tf_op jit(solution)/shard_map/ppermute | solution.py:220
